TPU v7x, 256 devices: a whole 4x4x8 slice. The times are simulated.
256 devices in a mesh: ctx: 16 (over z_lo, x), ch: 16 (over y, z_hi, core).
Axes of the slice: x: 4, y: 4, z: 8 (z_hi: 2, z_lo: 4; z = z_hi * 4 + z_lo), core: 2. Of those that a mesh axis runs over, the one named last changes fastest.
Arguments:
- tokens: bfloat16 [4096, 8192], P('ctx', 'ch'), may hold values from -6 to 6
- in_weight: bfloat16 [8192, 3, 8192], P('ctx', None, 'ch'), may hold values from -0.0625 to 0.0625
- short_filter: bfloat16 [3, 3, 8192], P(None, None, 'ch'), may hold values from -3 to 3
- decay_rate: float32 [8192, 16], P('ch'), may hold values from 1.2207031e-05 to 0.0333333333
- residue: float32 [8192, 16], P('ch'), may hold values from -0.12 to 0.12
- skip_gain: float32 [8192], P('ch'), may hold values from -4 to 4
Outputs:
- filtered: bfloat16 [4096, 8192], P('ctx', 'ch')
All inputs are finite; a program needn't handle non-finite values.
Results may differ from a plain program's by a relative error of at most 0.007.
Values may be sent and summed in bfloat16 or wider, within the bound.
No kernel may reach another device: no remote copies, remote signals or barrier semaphores. Data moves between devices by JAX's collectives and lax.ppermute only.
A program may use at most 128 MiB of HBM per device.

v0:
```python
import jax
import jax.numpy as jnp
from jax import lax
from jax.sharding import PartitionSpec as P

exact_mode = lax.Precision.HIGHEST


def from_behind(block, axis, distance):
    devices = range(lax.axis_size(axis))
    route = [(i - distance, i) for i in devices if i - distance in devices]
    return lax.ppermute(block, axis, route)


def copy_for_each(value, axis):
    size = lax.axis_size(axis)
    return lax.all_to_all(
        jnp.broadcast_to(value[None], (size, *value.shape)), axis, 0, 0, tiled=True
    )


def all_in_one(value, axis):
    leaves = jax.tree.leaves(value)
    sequence = sorted(range(len(leaves)), key=lambda k: -leaves[k].size)
    width = (1, *leaves[sequence[0]].shape)[-1]
    lines = [
        jnp.pad(leaves[k].reshape(-1), (0, -leaves[k].size % width)).reshape(-1, width)
        for k in sequence
    ]
    both, at, found = (copy_for_each(jnp.concatenate(lines), axis), 0, {})
    for k, line in zip(sequence, lines):
        section = both[:, at : at + len(line)].reshape(len(both), -1)
        found[k] = section[:, : leaves[k].size].reshape(-1, *leaves[k].shape)
        at += len(line)
    numbers = iter(range(len(leaves)))
    return jax.tree.map(lambda _: found[next(numbers)], value)


def folded_in_pairs(pieces, combine):
    while len(jax.tree.leaves(pieces)[0]) > 1:
        pieces = jax.vmap(combine)(
            *(jax.tree.map(lambda part: part[side::2], pieces) for side in (0, 1))
        )
    return jax.tree.map(lambda part: part[0], pieces)


def entering_2(value, axis, combine, identity):
    size, position = (lax.axis_size(axis), lax.axis_index(axis))
    passed = jnp.arange(size) < position

    def kept(part, zero, own):
        part = jnp.where(
            passed.reshape(-1, *(1 for _ in own.shape)), part, jnp.asarray(zero, own.dtype)
        )
        return part

    pieces = all_in_one(value, axis)
    return folded_in_pairs(jax.tree.map(kept, pieces, identity, value), combine)


def local(tokens, in_weight, short_filter, decay_rate, residue, skip_gain):
    tok_rows = tokens.shape[0]
    width_local = in_weight.shape[2]
    mode_count = decay_rate.shape[1]
    gathered = lax.all_gather(tokens, "ch", axis=1, tiled=True)
    portion = lax.all_gather(in_weight, "ctx", axis=0, tiled=True)
    flat_part = portion.reshape(portion.shape[0], 3 * width_local)
    projected = jnp.dot(gathered, flat_part, preferred_element_type=jnp.float32)
    streams = projected.astype(jnp.bfloat16).reshape(tok_rows, 3, width_local)
    tap_count = short_filter.shape[0]
    last_rows = streams[tok_rows - (tap_count - 1) :]
    before = from_behind(last_rows, "ctx", 1)
    padded = jnp.concatenate([before, streams], axis=0).astype(jnp.float32)
    filter_taps = short_filter.astype(jnp.float32)
    featured = jnp.zeros((tok_rows, 3, width_local), jnp.float32)
    for shift_back in range(tap_count):
        begin = tap_count - 1 - shift_back
        featured = featured + filter_taps[shift_back][None] * padded[begin : begin + tok_rows]
    query_gate = featured[:, 0]
    gated_rows = (featured[:, 1] * featured[:, 2]).astype(jnp.bfloat16)
    gated_wide = gated_rows.astype(jnp.float32)
    position = jnp.arange(tok_rows, dtype=jnp.float32)
    powers = jnp.exp(-decay_rate[None, :, :] * (tok_rows - 1.0 - position)[:, None, None])
    zero_state = jnp.zeros(decay_rate.shape, jnp.float32)
    local_state = jnp.einsum("jc,jcr->cr", gated_wide, powers, precision=exact_mode)
    block_decay = jnp.exp(-decay_rate * float(tok_rows))

    def compose(earlier, later):
        return (earlier[0] * later[0], earlier[1] * later[0] + later[1])

    unused, incoming = entering_2(
        (block_decay, local_state), "ctx", compose, (jnp.ones_like(block_decay), zero_state)
    )
    growth = jnp.exp(decay_rate[None, :, :] * position[:, None, None])
    scaled = (gated_wide[:, :, None] * growth).reshape(tok_rows, width_local * mode_count)
    lower_mask = (jnp.arange(tok_rows)[:, None] >= jnp.arange(tok_rows)[None, :]).astype(
        jnp.float32
    )
    running_sum = jnp.dot(lower_mask, scaled, precision=exact_mode).reshape(
        tok_rows, width_local, mode_count
    )
    shrink = jnp.exp(-decay_rate[None, :, :] * position[:, None, None])
    entering = (incoming * jnp.exp(-decay_rate))[None]
    convolved = jnp.sum(residue[None] * shrink * (running_sum + entering), axis=2)
    long_mix = convolved + skip_gain[None, :] * gated_wide
    return (query_gate * long_mix).astype(jnp.bfloat16)


def solution(mesh):
    in_specs = (
        P("ctx", "ch"),
        P("ctx", None, "ch"),
        P(None, None, "ch"),
        P("ch", None),
        P("ch", None),
        P("ch"),
    )
    out_specs = P("ctx", "ch")
    return jax.shard_map(local, mesh=mesh, in_specs=in_specs, out_specs=out_specs, check_vma=False)
```

profile of v0, /device:TPU:32, one launch (start us, length us, event | category | flops | bytes accessed | tf_op | source)
XLA Modules:
  0.0 433.5 jit_solution(10381329436334477997)
XLA Ops:
  6.5 0.7 all-gather.3.cloned.1.call-update
  7.3 2.6 copy.15
  9.9 0.7 convert_element_type.30
  10.7 0.8 multiply_exponential_fusion
  11.4 77.8 %all-gather.3.cloned.1.call-done = bf16[256,8192]{1,0:T(8,128)(2,1)} async-done(((bf16[256,512]{1,0:T(8,128)(2,1)}), bf16[256,8192]{1,0:T(8,128)(2,1)}) %all-gather.3.cloned.1.call-update) | async-done | bytes 4194320 | tf_op jit(solution)/shard_map/all_gather | solution.py:65
  89.3 267.0 %all-gather.5.cloned.1.call-done = bf16[8192,3,512]{0,2,1:T(8,128)(2,1)} async-done(((bf16[512,3,512]{0,2,1:T(8,128)(2,1)}), bf16[8192,3,512]{0,2,1:T(8,128)(2,1)}) %all-gather.5.cloned.1.call-update) | async-done | bytes 25165840 | tf_op jit(solution)/shard_map/all_gather | solution.py:66
  356.3 12.8 %convolution_convert_fusion = bf16[256,1536]{1,0:T(8,128)(2,1)S(1)} fusion(bf16[256,8192]{1,0:T(8,128)(2,1)} %all-gather.3.cloned.1.call-done, bf16[8192,1536]{0,1:T(8,128)(2,1)} %bitcast.41), kind=kOutput, calls=%fused_computation.5 | convolution fusion | flops 6442844160 | bytes 30146560 | tf_op jit(solution)/shard_map/dot_general | solution.py:68
  369.2 2.2 collective-permute-start
  371.4 0.3 copy.17
  371.7 0.3 copy.18
  371.9 4.8 %collective-permute-done = bf16[2,3,512]{2,0,1:T(2,128)(2,1)S(1)} collective-permute-done((bf16[2,3,512]{2,0,1:T(2,128)(2,1)S(1)}, bf16[2,3,512]{2,0,1:T(2,128)(2,1)S(1)}, u32[]{:S(2)}, u32[]{:S(2)}) %collective-permute-start) | collective-permute-done | bytes 6176 | tf_op jit(solution)/shard_map/ppermute | solution.py:12
  376.8 0.2 maximum_convert_fusion
  377.0 0.5 fusion.4
  377.7 1.5 multiply_reduce_fusion
  379.2 1.2 broadcast_in_dim.21
  380.4 5.4 %all-to-all-start = ((f32[16,1024,16]{1,2,0:T(8,128)}), f32[16,1024,16]{1,2,0:T(8,128)S(1)}, u32[]{:S(2)}, u32[]{:S(2)}) async-start(f32[16,1024,16]{1,2,0:T(8,128)} %broadcast_in_dim.21), calls=%async_computation | async-start | bytes 2097152 | tf_op jit(solution)/shard_map/all_to_all | solution.py:17
  385.8 0.8 copy.20
  386.6 1.1 mul.158
  387.7 1.0 copy.19
  388.7 4.8 %bitcast_multiply_fusion = f32[256,8192]{0,1:T(8,128)} fusion(f32[8192]{0:T(1024)S(1)} %mul.158, f32[256,512]{0,1:T(8,128)} %copy.19), kind=kLoop, calls=%fused_computation | loop fusion | flops 4194304 | bytes 8945664 | tf_op jit(solution)/shard_map/mul | solution.py:95
  393.5 16.7 %all-to-all-done = f32[16,1024,16]{1,2,0:T(8,128)S(1)} async-done(((f32[16,1024,16]{1,2,0:T(8,128)}), f32[16,1024,16]{1,2,0:T(8,128)S(1)}, u32[]{:S(2)}, u32[]{:S(2)}) %all-to-all-start) | async-done | bytes 1048608 | tf_op jit(solution)/shard_map/all_to_all | solution.py:17
  410.2 0.1 slice_select_fusion
  410.6 15.2 %multiply_reduce_fusion.1 = f32[256,512]{1,0:T(8,128)S(1)} fusion(f32[512,16]{0,1:T(8,128)S(1)} %fusion.12, f32[512,16]{0,1:T(8,128)S(1)} %get-tuple-element.17, f32[512,16]{0,1:T(8,128)S(1)} %copy-done.2, f32[512,16,256]{2,1,0:T(8,128)} %bitcast.38), kind=kOutput, calls=%fused_computation.4 | convolution fusion | flops 6452871168 | bytes 9011200 | tf_op jit(solution)/shard_map/dot_general | solution.py:99
  425.8 0.8 fusion.8
  (20 shorter events, 0.4 us)
Async XLA Ops:
  6.5 82.7 %all-gather.3.cloned.1.call-start = ((), (), s32[]{:S(2)}) async-start(), calls=%async_computation.1 | async-start | bytes 4456448 | tf_op jit(solution)/shard_map/all_gather | solution.py:65
  7.3 349.1 %all-gather.5.cloned.1.call-start = ((), (), s32[]{:S(2)}) async-start(), calls=%async_computation.2 | async-start | bytes 26738688 | tf_op jit(solution)/shard_map/all_gather | solution.py:66
  369.2 7.6 %collective-permute-start = (bf16[2,3,512]{2,0,1:T(2,128)(2,1)S(1)}, bf16[2,3,512]{2,0,1:T(2,128)(2,1)S(1)}, u32[]{:S(2)}, u32[]{:S(2)}) collective-permute-start(bf16[2,3,512]{2,0,1:T(2,128)(2,1)S(1)} %bitcast.40), channel_id=1, source_target_pairs={{0,16},{16,32},{32,48},{48,64},{64,80},{80,96},{96,112},{112,128},... | collective-permute-start | bytes 18440 | tf_op jit(solution)/shard_map/ppermute | solution.py:12
  377.0 8.8 %copy-start = (f32[512,16]{0,1:T(8,128)S(1)}, f32[512,16]{0,1:T(8,128)}, u32[]{:S(2)}) copy-start(f32[512,16]{0,1:T(8,128)} %param.9) | copy-start | bytes 98308
  380.4 30.2 %copy-start.2 = (f32[512,16]{0,1:T(8,128)S(1)}, f32[512,16]{0,1:T(8,128)}, u32[]{:S(2)}) copy-start(f32[512,16]{0,1:T(8,128)} %param.10) | copy-start | bytes 98308
  380.4 29.9 %all-to-all-start = ((f32[16,1024,16]{1,2,0:T(8,128)}), f32[16,1024,16]{1,2,0:T(8,128)S(1)}, u32[]{:S(2)}, u32[]{:S(2)}) async-start(f32[16,1024,16]{1,2,0:T(8,128)} %broadcast_in_dim.21), calls=%async_computation | async-start | bytes 2097152 | tf_op jit(solution)/shard_map/all_to_all | solution.py:17
  410.5 15.3 %copy-start.1 = (f32[512]{0:T(512)S(1)}, f32[512]{0:T(512)}, u32[]{:S(2)}) copy-start(f32[512]{0:T(512)} %param.11) | copy-start | bytes 6148
Sparse Core Ops, SparseCore 0:
  9.9 79.3 all-gather.2
  91.1 265.1 all-gather.4
where the time goes:
time: 434 us; the launch traced here: 433 us
  waiting for transfers between devices  367 us (85%)
  matrix products  28 us (6%)
  between operations  13.6 us (3%)
  other arithmetic  9.77 us (2%)
  starting transfers between devices  7.67 us (2%)
  local copies, waits for them, and re-layouts  7.3 us (2%)
    all_gather x1, waiting for transfers between devices, local(): portion = lax.all_gather(in_weight, 'ctx', axis=0, tiled=True)  267 us
    all_gather x1, waiting for transfers between devices, local(): gathered = lax.all_gather(tokens, 'ch', axis=1, tiled=True)  77.8 us
    all_to_all x1, waiting for transfers between devices, copy_for_each(): lax.all_to_all(jnp.broadcast_to(value[None], (size, *value.shape)), axis,...  16.7 us
    dot_general x1, matrix products, local(): jnp.dot(lower_mask, scaled, precision=exact_mode)  15.2 us
    dot_general x1, matrix products, local(): projected = jnp.dot(gathered, flat_part, preferred_element_type=jnp.float32)  12.8 us
  transfers between devices with their start and end apart: 4, of which 4 were waited for; matrix products, arithmetic and copies ran while one was open for 3% of the time, Pallas kernels for 0%

commit v1 on v0

v1 whole, which is shorter than its diff:
```python
import jax
import jax.numpy as jnp
import numpy as np
from jax import lax
from jax.sharding import Mesh, PartitionSpec as P

exact_mode = lax.Precision.HIGHEST
SEQ = ("zl", "x")


def from_behind(block, axis, distance):
    devices = range(lax.axis_size(axis))
    route = [(i - distance, i) for i in devices if i - distance in devices]
    return lax.ppermute(block, axis, route)


def folded_in_pairs(pieces, combine):
    while len(jax.tree.leaves(pieces)[0]) > 1:
        pieces = jax.vmap(combine)(
            *(jax.tree.map(lambda part: part[side::2], pieces) for side in (0, 1))
        )
    return jax.tree.map(lambda part: part[0], pieces)


def entering_2(value, axis, combine, identity):
    size, position = (lax.axis_size(axis), lax.axis_index(axis))
    passed = jnp.arange(size) < position

    def kept(part, zero, own):
        return jnp.where(
            passed.reshape(-1, *(1 for _ in own.shape)), part, jnp.asarray(zero, own.dtype)
        )

    pieces = jax.tree.map(lambda v: lax.all_gather(v, axis, axis=0, tiled=False), value)
    return folded_in_pairs(jax.tree.map(kept, pieces, identity, value), combine)


def local(tokens, in_weight, short_filter, decay_rate, residue, skip_gain):
    tok_rows = tokens.shape[0]
    width_local = in_weight.shape[2]
    mode_count = decay_rate.shape[1]
    gathered = lax.all_gather(tokens, "ch", axis=1, tiled=True)
    column = lax.all_to_all(gathered, "zl", 1, 0, tiled=True)
    portion = lax.all_gather(in_weight, "x", axis=0, tiled=True)
    flat_part = portion.reshape(portion.shape[0], 3 * width_local)
    partial = jnp.dot(column, flat_part, preferred_element_type=jnp.float32)
    projected = lax.psum_scatter(partial, "zl", scatter_dimension=0, tiled=True)
    streams = projected.astype(jnp.bfloat16).reshape(tok_rows, 3, width_local)
    tap_count = short_filter.shape[0]
    last_rows = streams[tok_rows - (tap_count - 1) :]
    before = from_behind(last_rows, SEQ, 1)
    padded = jnp.concatenate([before, streams], axis=0).astype(jnp.float32)
    filter_taps = short_filter.astype(jnp.float32)
    featured = jnp.zeros((tok_rows, 3, width_local), jnp.float32)
    for shift_back in range(tap_count):
        begin = tap_count - 1 - shift_back
        featured = featured + filter_taps[shift_back][None] * padded[begin : begin + tok_rows]
    query_gate = featured[:, 0]
    gated_rows = (featured[:, 1] * featured[:, 2]).astype(jnp.bfloat16)
    gated_wide = gated_rows.astype(jnp.float32)
    position = jnp.arange(tok_rows, dtype=jnp.float32)
    powers = jnp.exp(-decay_rate[None, :, :] * (tok_rows - 1.0 - position)[:, None, None])
    zero_state = jnp.zeros(decay_rate.shape, jnp.float32)
    local_state = jnp.einsum("jc,jcr->cr", gated_wide, powers, precision=exact_mode)
    block_decay = jnp.exp(-decay_rate * float(tok_rows))

    def compose(earlier, later):
        return (earlier[0] * later[0], earlier[1] * later[0] + later[1])

    unused, incoming = entering_2(
        (block_decay, local_state), SEQ, compose, (jnp.ones_like(block_decay), zero_state)
    )
    growth = jnp.exp(decay_rate[None, :, :] * position[:, None, None])
    scaled = (gated_wide[:, :, None] * growth).reshape(tok_rows, width_local * mode_count)
    lower_mask = (jnp.arange(tok_rows)[:, None] >= jnp.arange(tok_rows)[None, :]).astype(
        jnp.float32
    )
    running_sum = jnp.dot(lower_mask, scaled, precision=exact_mode).reshape(
        tok_rows, width_local, mode_count
    )
    shrink = jnp.exp(-decay_rate[None, :, :] * position[:, None, None])
    entering = (incoming * jnp.exp(-decay_rate))[None]
    convolved = jnp.sum(residue[None] * shrink * (running_sum + entering), axis=2)
    long_mix = convolved + skip_gain[None, :] * gated_wide
    return (query_gate * long_mix).astype(jnp.bfloat16)


def split_mesh(mesh):
    ctx, ch = mesh.shape["ctx"], mesh.shape["ch"]
    inner = 4 if ctx % 4 == 0 else 1
    devices = np.asarray(mesh.devices).reshape(ctx // inner, inner, ch)
    return Mesh(devices, ("zl", "x", "ch"))


def solution(mesh):
    fine = split_mesh(mesh)
    in_specs = (
        P(SEQ, "ch"),
        P(SEQ, None, "ch"),
        P(None, None, "ch"),
        P("ch", None),
        P("ch", None),
        P("ch"),
    )
    out_specs = P(SEQ, "ch")
    return jax.shard_map(local, mesh=fine, in_specs=in_specs, out_specs=out_specs, check_vma=False)
```

time: 434 us -> 411 us (0.947); the launches traced: 433 us -> 403 us
  waiting for transfers between devices: 367 us -> 155 us
  blocking collectives: 0 us -> 179 us
  local copies, waits for them, and re-layouts: 7.3 us -> 22.7 us
  matrix products: 28 us -> 22 us
  starting transfers between devices: 7.67 us -> 2.01 us
    all_gather x1, waiting for transfers between devices: 267 us -> 0.01 us  [local(): portion = lax.all_gather(in_weight, 'x', axis=0, tiled=True)]
    all_to_all x0 -> x1, blocking collectives: none -> 99 us  [local(): column = lax.all_to_all(gathered, 'zl', 1, 0, tiled=True)]
    all_gather x0 -> x2, blocking collectives: none -> 79.7 us  [entering_2(): lax.all_gather(v, axis, axis=0, tiled=False)]
    reduce_scatter x0 -> x1, waiting for transfers between devices: none -> 73 us  [local(): projected = lax.psum_scatter(partial, 'zl', scatter_dimension=0, tiled=True)]
    all_to_all x1 -> x0, waiting for transfers between devices: 16.7 us -> none  [copy_for_each(): lax.all_to_all(jnp.broadcast_to(value[None], (size, *value.shape)), axis,...]
    slice x0 -> x12, local copies, waits for them, and re-layouts: none -> 9.72 us  [folded_in_pairs(): part[side::2]]
    all_to_all x0 -> x1, local copies, waits for them, and re-layouts: none -> 6.27 us  [local(): column = lax.all_to_all(gathered, 'zl', 1, 0, tiled=True)]
    all_to_all x1 -> x0, starting transfers between devices: 5.42 us -> none  [copy_for_each(): lax.all_to_all(jnp.broadcast_to(value[None], (size, *value.shape)), axis,...]
  transfers between devices with their start and end apart: 4 -> 4, of which waited for: 4 -> 3; matrix products, arithmetic and copies ran while one was open for 3% -> 2% of each run, Pallas kernels for 0% -> 0%
where the time goes in v1:
time: 411 us; the launch traced here: 403 us
  blocking collectives  179 us (44%)
  waiting for transfers between devices  155 us (38%)
  local copies, waits for them, and re-layouts  22.7 us (6%)
  matrix products  22 us (5%)
  between operations  13.4 us (3%)
  other arithmetic  8.33 us (2%)
    all_to_all x1, blocking collectives, local(): column = lax.all_to_all(gathered, 'zl', 1, 0, tiled=True)  99 us
    all_gather x2, blocking collectives, entering_2(): lax.all_gather(v, axis, axis=0, tiled=False)  79.7 us
    all_gather x1, waiting for transfers between devices, local(): gathered = lax.all_gather(tokens, 'ch', axis=1, tiled=True)  77.8 us
    reduce_scatter x1, waiting for transfers between devices, local(): projected = lax.psum_scatter(partial, 'zl', scatter_dimension=0, tiled=True)  73 us
    dot_general x1, matrix products, local(): partial = jnp.dot(column, flat_part, preferred_element_type=jnp.float32)  11.9 us
    dot_general x1, matrix products, local(): jnp.dot(lower_mask, scaled, precision=exact_mode)  10.1 us
    slice x12, local copies, waits for them, and re-layouts, folded_in_pairs(): part[side::2]  9.72 us
  transfers between devices with their start and end apart: 4, of which 3 were waited for; matrix products, arithmetic and copies ran while one was open for 2% of the time, Pallas kernels for 0%

profile of v1, /device:TPU:32, one launch (start us, length us, event | category | flops | bytes accessed | tf_op | source)
XLA Modules:
  0.0 402.5 jit_solution(10510586935251717624)
XLA Ops:
  6.5 1.8 copy.23
  8.4 2.6 copy.25
  11.1 77.8 %all-gather.5.cloned.1.call-done = bf16[256,8192]{0,1:T(8,128)(2,1)} async-done(((bf16[256,512]{0,1:T(8,128)(2,1)}), bf16[256,8192]{0,1:T(8,128)(2,1)}) %all-gather.5.cloned.1.call-update) | async-done | bytes 4194320 | tf_op jit(solution)/shard_map/all_gather | solution.py:42
  88.8 99.0 %all_to_all.19 = bf16[256,4,2048]{0,2,1:T(8,128)(2,1)} all-to-all(bf16[256,4,2048]{0,2,1:T(8,128)(2,1)} %bitcast.61), channel_id=1, replica_groups=mesh['zl'=4,'x'=4,'ch'=16] {'zl'}, dimensions={1} | all-to-all | bytes 8388608 | tf_op jit(solution)/shard_map/all_to_all | solution.py:43
  187.8 6.3 %copy.24 = bf16[4,256,2048]{2,1,0:T(8,128)(2,1)} copy(bf16[4,256,2048]{1,2,0:T(8,128)(2,1)} %bitcast.59) | data formatting | bytes 8388608 | tf_op jit(solution)/shard_map/all_to_all | solution.py:43
  194.1 11.9 %fusion.15 = f32[1024,1536]{1,0:T(8,128)} fusion(bf16[1024,2048]{1,0:T(8,128)(2,1)} %bitcast.62, bf16[2048,1536]{0,1:T(8,128)(2,1)} %bitcast.79), kind=kOutput, calls=%fused_computation.37 | convolution fusion | flops 6442450944 | bytes 16777216 | tf_op jit(solution)/shard_map/dot_general | solution.py:46
  206.1 0.7 copy-done.1
  206.8 43.5 %all-gather.1 = f32[8192,16]{0,1:T(8,128)S(1)} all-gather(f32[512,16]{0,1:T(8,128)S(1)} %get-tuple-element.11), channel_id=3, replica_groups=mesh['zl'=4,'x'=4,'ch'=16] {'zl','x'}, dimensions={0}, use_global_device_ids=true | all-gather | bytes 557056 | tf_op jit(solution)/shard_map/all_gather | solution.py:34
  250.3 73.0 %reduce-scatter.2.cloned.1.call-done = f32[256,1536]{1,0:T(8,128)} async-done(((f32[1024,1536]{1,0:T(8,128)}), f32[256,1536]{1,0:T(8,128)}) %reduce-scatter.2.cloned.1.call-update) | async-done | bytes 1572880 | tf_op jit(solution)/shard_map/reduce_scatter | solution.py:47
  323.4 1.5 convert_element_type.31
  324.9 1.9 collective-permute-start
  328.0 4.6 %collective-permute-done = bf16[2,3,512]{2,0,1:T(2,128)(2,1)S(1)} collective-permute-done((bf16[2,3,512]{2,0,1:T(2,128)(2,1)S(1)}, bf16[2,3,512]{2,0,1:T(2,128)(2,1)S(1)}, u32[]{:S(2)}, u32[]{:S(2)}) %collective-permute-start) | collective-permute-done | bytes 6176 | tf_op jit(solution)/shard_map/ppermute | solution.py:14
  332.7 0.5 fusion.4
  333.4 1.5 multiply_reduce_fusion
  334.9 36.2 %all-gather = f32[8192,16]{0,1:T(8,128)S(1)} all-gather(f32[512,16]{0,1:T(8,128)S(1)} %multiply_reduce_fusion), channel_id=2, replica_groups=mesh['zl'=4,'x'=4,'ch'=16] {'zl','x'}, dimensions={0}, use_global_device_ids=true | all-gather | bytes 557056 | tf_op jit(solution)/shard_map/all_gather | solution.py:34
  371.4 1.0 bitcast_select_fusion
  372.4 1.9 slice.92
  374.3 2.5 slice.94
  376.8 1.4 slice.93
  378.2 1.4 slice.96
  379.5 1.2 fusion.13
  383.8 1.3 bitcast_multiply_fusion
  385.1 10.1 %multiply_reduce_fusion.1 = f32[256,512]{1,0:T(8,128)S(1)} fusion(f32[512,16]{0,1:T(8,128)S(1)} %bitcast_multiply_fusion.1, f32[512,16]{0,1:T(8,128)S(1)} %get-tuple-element.12, f32[512,16]{0,1:T(8,128)S(1)} %copy-done.3, f32[512,16,256]{2,1,0:T(8,128)S(1)} %bitcast.60), kind=kOutput, calls=%fused_computation.4 | convolution fusion | flops 6452871168 | bytes 9011200 | tf_op jit(solution)/shard_map/dot_general | solution.py:78
  395.1 0.8 fusion.8
  (42 shorter events, 5.0 us)
Async XLA Ops:
  6.5 82.3 %all-gather.5.cloned.1.call-start = ((), (), s32[]{:S(2)}) async-start(), calls=%async_computation.2 | async-start | bytes 4456448 | tf_op jit(solution)/shard_map/all_gather | solution.py:42
  8.4 185.8 %all-gather.7.cloned.1.call-start = ((), (), s32[]{:S(2)}) async-start(), calls=%async_computation.3 | async-start | bytes 7864320 | tf_op jit(solution)/shard_map/all_gather | solution.py:44
  11.0 312.3 %reduce-scatter.2.cloned.1.call-start = ((), (), s32[]{:S(2)}) async-start(), calls=%async_computation.4 | async-start | bytes 7864320 | tf_op jit(solution)/shard_map/reduce_scatter | solution.py:47
  206.0 0.7 copy-start.1
  206.0 0.8 copy-start
  324.9 7.6 %collective-permute-start = (bf16[2,3,512]{2,0,1:T(2,128)(2,1)S(1)}, bf16[2,3,512]{2,0,1:T(2,128)(2,1)S(1)}, u32[]{:S(2)}, u32[]{:S(2)}) collective-permute-start(bf16[2,3,512]{2,0,1:T(2,128)(2,1)S(1)} %bitcast.78), channel_id=1, source_target_pairs={{0,16},{16,32},{32,48},{48,64},{64,80},{80,96},{96,112},{112,128},... | collective-permute-start | bytes 18440 | tf_op jit(solution)/shard_map/ppermute | solution.py:14
  381.0 4.0 copy-start.3
  385.1 10.1 %copy-start.2 = (f32[512]{0:T(512)S(1)}, f32[512]{0:T(512)}, u32[]{:S(2)}) copy-start(f32[512]{0:T(512)} %param.11) | copy-start | bytes 6148
Sparse Core Ops, SparseCore 0:
  10.0 78.7 all-gather.4
  90.6 64.7 all-gather.6
  206.2 117.1 reduce-scatter.1

commit v2 on v1

--- a/solution.py
+++ b/solution.py
@@ -14,37 +14,43 @@
     return lax.ppermute(block, axis, route)
 
 
-def folded_in_pairs(pieces, combine):
-    while len(jax.tree.leaves(pieces)[0]) > 1:
-        pieces = jax.vmap(combine)(
-            *(jax.tree.map(lambda part: part[side::2], pieces) for side in (0, 1))
-        )
-    return jax.tree.map(lambda part: part[0], pieces)
-
-
-def entering_2(value, axis, combine, identity):
-    size, position = (lax.axis_size(axis), lax.axis_index(axis))
-    passed = jnp.arange(size) < position
-
-    def kept(part, zero, own):
-        return jnp.where(
-            passed.reshape(-1, *(1 for _ in own.shape)), part, jnp.asarray(zero, own.dtype)
-        )
-
-    pieces = jax.tree.map(lambda v: lax.all_gather(v, axis, axis=0, tiled=False), value)
-    return folded_in_pairs(jax.tree.map(kept, pieces, identity, value), combine)
+def ring_sends(pieces, axis, size):
+    position = lax.axis_index(axis)
+    received = []
+    for k in range(1, size):
+        route = [(i, (i + k) % size) for i in range(size)]
+        received.append(lax.ppermute(pieces(k, position), axis, route))
+    return received
 
 
 def local(tokens, in_weight, short_filter, decay_rate, residue, skip_gain):
     tok_rows = tokens.shape[0]
     width_local = in_weight.shape[2]
     mode_count = decay_rate.shape[1]
+    feat_block = in_weight.shape[0]
+    across, down = lax.axis_size("x"), lax.axis_size("zl")
+    me_x, me_z = lax.axis_index("x"), lax.axis_index("zl")
+    flat_own = in_weight.reshape(feat_block, 3 * width_local)
+    weights = [flat_own] + ring_sends(lambda k, p: flat_own, "x", across)
     gathered = lax.all_gather(tokens, "ch", axis=1, tiled=True)
-    column = lax.all_to_all(gathered, "zl", 1, 0, tiled=True)
-    portion = lax.all_gather(in_weight, "x", axis=0, tiled=True)
-    flat_part = portion.reshape(portion.shape[0], 3 * width_local)
-    partial = jnp.dot(column, flat_part, preferred_element_type=jnp.float32)
-    projected = lax.psum_scatter(partial, "zl", scatter_dimension=0, tiled=True)
+    chunk = gathered.shape[1] // down
+
+    def chunk_for(k, p):
+        return lax.dynamic_slice_in_dim(gathered, ((p + k) % down) * chunk, chunk, axis=1)
+
+    rows = [chunk_for(0, me_z)] + ring_sends(chunk_for, "zl", down)
+    column = jnp.concatenate(rows, axis=0)
+    partial = jnp.zeros((column.shape[0], 3 * width_local), jnp.float32)
+    for k in range(across):
+        source = (me_x - k) % across
+        taken = lax.dynamic_slice_in_dim(column, source * feat_block, feat_block, axis=1)
+        partial = partial + jnp.dot(taken, weights[k], preferred_element_type=jnp.float32)
+    pieces = partial.reshape(down, tok_rows, 3 * width_local)
+    projected = pieces[0]
+    for k in range(1, down):
+        route = [(i, (i - k) % down) for i in range(down)]
+        back = lax.ppermute(pieces[k].astype(jnp.bfloat16), "zl", route)
+        projected = projected + back.astype(jnp.float32)
     streams = projected.astype(jnp.bfloat16).reshape(tok_rows, 3, width_local)
     tap_count = short_filter.shape[0]
     last_rows = streams[tok_rows - (tap_count - 1) :]
@@ -60,16 +66,18 @@
     gated_wide = gated_rows.astype(jnp.float32)
     position = jnp.arange(tok_rows, dtype=jnp.float32)
     powers = jnp.exp(-decay_rate[None, :, :] * (tok_rows - 1.0 - position)[:, None, None])
-    zero_state = jnp.zeros(decay_rate.shape, jnp.float32)
     local_state = jnp.einsum("jc,jcr->cr", gated_wide, powers, precision=exact_mode)
-    block_decay = jnp.exp(-decay_rate * float(tok_rows))
-
-    def compose(earlier, later):
-        return (earlier[0] * later[0], earlier[1] * later[0] + later[1])
-
-    unused, incoming = entering_2(
-        (block_decay, local_state), SEQ, compose, (jnp.ones_like(block_decay), zero_state)
-    )
+    along = [local_state] + ring_sends(lambda k, p: local_state, "x", across)
+    row = jnp.stack(along)
+    states = jnp.stack([row] + ring_sends(lambda k, p: row, "zl", down))
+    step_z = jnp.arange(down)[:, None]
+    step_x = jnp.arange(across)[None, :]
+    source = ((me_z - step_z) % down) * across + (me_x - step_x) % across
+    lag = (me_z * across + me_x - 1 - source).astype(jnp.float32)
+    decay_b = decay_rate[None, None]
+    weight = jnp.exp(-decay_b * (float(tok_rows) * jnp.maximum(lag, 0.0))[:, :, None, None])
+    weight = jnp.where((lag >= 0)[:, :, None, None], weight, 0.0)
+    incoming = jnp.sum(weight * states, axis=(0, 1))
     growth = jnp.exp(decay_rate[None, :, :] * position[:, None, None])
     scaled = (gated_wide[:, :, None] * growth).reshape(tok_rows, width_local * mode_count)
     lower_mask = (jnp.arange(tok_rows)[:, None] >= jnp.arange(tok_rows)[None, :]).astype(

time: 411 us -> 327 us (0.80); the launches traced: 403 us -> 327 us
  blocking collectives: 179 us -> 0 us
  waiting for transfers between devices: 155 us -> 244 us
  starting transfers between devices: 2.01 us -> 24.3 us
  local copies, waits for them, and re-layouts: 22.7 us -> 7.05 us
  matrix products: 22 us -> 29.6 us
    ppermute x0 -> x15, waiting for transfers between devices: none -> 156 us  [the longest x12 91.4 us: ring_sends(): received.append(lax.ppermute(pieces(k, position), axis, route))]
    all_to_all x1 -> x0, blocking collectives: 99 us -> none  [local(): column = lax.all_to_all(gathered, 'zl', 1, 0, tiled=True)]
    all_gather x2 -> x0, blocking collectives: 79.7 us -> none  [entering_2(): lax.all_gather(v, axis, axis=0, tiled=False)]
    reduce_scatter x1 -> x0, waiting for transfers between devices: 73 us -> none  [local(): projected = lax.psum_scatter(partial, 'zl', scatter_dimension=0, tiled=True)]
    ppermute x0 -> x15, starting transfers between devices: none -> 20.9 us  [the longest x12 17.7 us: ring_sends(): received.append(lax.ppermute(pieces(k, position), axis, route))]
    slice x12 -> x1, local copies, waits for them, and re-layouts: 9.72 us -> 0.15 us  [local(): back = lax.ppermute(pieces[k].astype(jnp.bfloat16), 'zl', route)]
    dot_general x1 -> x4, matrix products: 11.9 us -> 19.5 us  [local(): jnp.dot(taken, weights[k], preferred_element_type=jnp.float32)]
    all_to_all x1 -> x0, local copies, waits for them, and re-layouts: 6.27 us -> none  [local(): column = lax.all_to_all(gathered, 'zl', 1, 0, tiled=True)]
  transfers between devices with their start and end apart: 4 -> 17, of which waited for: 3 -> 13; matrix products, arithmetic and copies ran while one was open for 2% -> 6% of each run, Pallas kernels for 0% -> 0%
where the time goes in v2:
time: 327 us
  waiting for transfers between devices  244 us (75%)
  matrix products  29.6 us (9%)
  starting transfers between devices  24.3 us (7%)
  between operations  13.7 us (4%)
  other arithmetic  8.26 us (3%)
  local copies, waits for them, and re-layouts  7.05 us (2%)
    ppermute x12, waiting for transfers between devices, ring_sends(): received.append(lax.ppermute(pieces(k, position), axis, route))  91.4 us
    all_gather x1, waiting for transfers between devices, local(): gathered = lax.all_gather(tokens, 'ch', axis=1, tiled=True)  82 us
    ppermute x3, waiting for transfers between devices, local(): back = lax.ppermute(pieces[k].astype(jnp.bfloat16), 'zl', route)  64.9 us
    dot_general x4, matrix products, local(): jnp.dot(taken, weights[k], preferred_element_type=jnp.float32)  19.5 us
    ppermute x12, starting transfers between devices, ring_sends(): received.append(lax.ppermute(pieces(k, position), axis, route))  17.7 us
    dot_general x1, matrix products, local(): jnp.dot(lower_mask, scaled, precision=exact_mode)  10.1 us
  transfers between devices with their start and end apart: 17, of which 13 were waited for; matrix products, arithmetic and copies ran while one was open for 6% of the time, Pallas kernels for 0%

profile of v2, /device:TPU:32, one launch (start us, length us, event | category | flops | bytes accessed | tf_op | source)
XLA Modules:
  0.0 327.1 jit_solution(8033702825253924592)
XLA Ops:
  7.3 82.0 %all-gather.2.cloned.1.call-done = bf16[256,8192]{1,0:T(8,128)(2,1)} async-done(((bf16[256,512]{1,0:T(8,128)(2,1)}), bf16[256,8192]{1,0:T(8,128)(2,1)}) %all-gather.2.cloned.1.call-update) | async-done | bytes 4194320 | tf_op jit(solution)/shard_map/all_gather | solution.py:35
  89.3 4.1 %constant_dynamic-slice_fusion.3 = (bf16[256,2048]{1,0:T(8,128)(2,1)S(1)}, bf16[256,2048]{1,0:T(8,128)(2,1)}, bf16[256,2048]{1,0:T(8,128)(2,1)}, bf16[256,2048]{1,0:T(8,128)(2,1)}) fusion(bf16[256,8192]{1,0:T(8,128)(2,1)} %all-gather.2.cloned.1.call-done, s32[]{:T(128)S(6)} %select_n.86, s32[]{:T(128)S(6)} %select_n.92, s32[]{:T(128)S(6)} %select_n.90, ...), kind=kLoop, calls=%fused_computation.55 | loop fusion | bytes 8388624 | tf_op jit(solution)/shard_map/dynamic_slice | solution.py:39
  93.7 2.9 collective-permute-start.1
  96.9 1.6 copy.17
  99.9 2.7 collective-permute-start.4
  102.6 17.1 %collective-permute-done = bf16[256,2048]{1,0:T(8,128)(2,1)} collective-permute-done((bf16[256,2048]{1,0:T(8,128)(2,1)}, bf16[256,2048]{1,0:T(8,128)(2,1)}, u32[]{:S(2)}, u32[]{:S(2)}) %collective-permute-start) | collective-permute-done | bytes 1048608 | tf_op jit(solution)/shard_map/ppermute | solution.py:22
  119.7 2.7 collective-permute-start.5
  122.4 61.9 %collective-permute-done.1 = bf16[256,2048]{1,0:T(8,128)(2,1)} collective-permute-done((bf16[256,2048]{1,0:T(8,128)(2,1)}, bf16[256,2048]{1,0:T(8,128)(2,1)}, u32[]{:S(2)}, u32[]{:S(2)}) %collective-permute-start.1) | collective-permute-done | bytes 1048608 | tf_op jit(solution)/shard_map/ppermute | solution.py:22
  184.2 3.4 %collective-permute-done.2 = bf16[256,2048]{1,0:T(8,128)(2,1)} collective-permute-done((bf16[256,2048]{1,0:T(8,128)(2,1)}, bf16[256,2048]{1,0:T(8,128)(2,1)}, u32[]{:S(2)}, u32[]{:S(2)}) %collective-permute-start.2) | collective-permute-done | bytes 1048608 | tf_op jit(solution)/shard_map/ppermute | solution.py:22
  187.6 2.1 pad_maximum_fusion
  190.0 1.8 fusion.17
  191.8 5.9 %fusion.15 = f32[1024,1536]{1,0:T(8,128)} fusion(bf16[512,1536]{0,1:T(8,128)(2,1)} %collective-permute-done.3, bf16[1024,2048]{1,0:T(8,128)(2,1)S(1)} %pad_maximum_fusion, s32[]{:T(128)S(6)} %select_n.96), kind=kOutput, calls=%fused_computation.20 | convolution fusion | flops 1610612736 | bytes 8912900 | tf_op jit(solution)/shard_map/dot_general | solution.py:47
  197.7 4.4 %fusion.13 = f32[1024,1536]{1,0:T(8,128)} fusion(bf16[512,1536]{0,1:T(8,128)(2,1)S(1)} %collective-permute-done.4, bf16[1024,2048]{1,0:T(8,128)(2,1)S(1)} %pad_maximum_fusion, s32[]{:T(128)S(6)} %select_n.98), kind=kOutput, calls=%fused_computation.18 | convolution fusion | flops 1610612736 | bytes 8912900 | tf_op jit(solution)/shard_map/dot_general | solution.py:47
  202.1 7.4 %fusion.35 = (bf16[1024,1536]{1,0:T(8,128)(2,1)S(1)}, f32[1024,1536]{1,0:T(8,128)S(1)}) fusion(bf16[512,1536]{0,1:T(8,128)(2,1)} %collective-permute-done.5, bf16[1024,2048]{1,0:T(8,128)(2,1)S(1)} %pad_maximum_fusion, s32[]{:T(128)S(6)} %select_n.100, f32[1024,1536]{1,0:T(8,128)} %fusion.13, f32[1024,1536]{1,0:T(8,128)S(1)} %fusion.17, f32[1024,1536]{1,0:T(8,128)} %fusion.15), kind=kOutput, calls=%fused_computation.64 | convolution fusion | flops 1616904192 | bytes 30932996 | tf_op jit(solution)/shard_map/dot_general | solution.py:47
  211.0 1.9 collective-permute-start.8
  212.9 51.2 %collective-permute-done.6 = bf16[256,1536]{1,0:T(8,128)(2,1)S(1)} collective-permute-done((bf16[256,1536]{1,0:T(8,128)(2,1)S(1)}, bf16[256,1536]{1,0:T(8,128)(2,1)S(1)}, u32[]{:S(2)}, u32[]{:S(2)}) %collective-permute-start.6) | collective-permute-done | bytes 786464 | tf_op jit(solution)/shard_map/ppermute | solution.py:52
  264.1 13.7 %collective-permute-done.8 = bf16[256,1536]{1,0:T(8,128)(2,1)S(1)} collective-permute-done((bf16[256,1536]{1,0:T(8,128)(2,1)S(1)}, bf16[256,1536]{1,0:T(8,128)(2,1)S(1)}, u32[]{:S(2)}, u32[]{:S(2)}) %collective-permute-start.8) | collective-permute-done | bytes 786464 | tf_op jit(solution)/shard_map/ppermute | solution.py:52
  278.2 3.4 %collective-permute-start.9 = (bf16[2,3,512]{2,0,1:T(2,128)(2,1)S(1)}, bf16[2,3,512]{2,0,1:T(2,128)(2,1)S(1)}, u32[]{:S(2)}, u32[]{:S(2)}) collective-permute-start(bf16[2,3,512]{2,0,1:T(2,128)(2,1)S(1)} %bitcast.57), channel_id=1, source_target_pairs={{0,16},{16,32},{32,48},{48,64},{64,80},{80,96},{96,112},{112,128},... | collective-permute-start | bytes 18440 | tf_op jit(solution)/shard_map/ppermute | solution.py:14
  282.2 5.2 %collective-permute-done.9 = bf16[2,3,512]{2,0,1:T(2,128)(2,1)S(1)} collective-permute-done((bf16[2,3,512]{2,0,1:T(2,128)(2,1)S(1)}, bf16[2,3,512]{2,0,1:T(2,128)(2,1)S(1)}, u32[]{:S(2)}, u32[]{:S(2)}) %collective-permute-start.9) | collective-permute-done | bytes 6176 | tf_op jit(solution)/shard_map/ppermute | solution.py:14
  290.5 2.5 collective-permute-start.12
  297.2 3.0 collective-permute-start.14
  301.8 2.8 collective-permute-done.13
  306.1 2.1 collective-permute-done.15
  309.3 10.1 %multiply_reduce_fusion.1 = f32[256,512]{1,0:T(8,128)S(1)} fusion(f32[512,16]{0,1:T(8,128)S(1)} %exponential_multiply_fusion, f32[512,16]{0,1:T(8,128)S(1)} %neg.8, f32[512,16]{0,1:T(8,128)S(1)} %copy-done.5, f32[512,16,256]{2,1,0:T(8,128)S(1)} %bitcast.45), kind=kOutput, calls=%fused_computation.4 | convolution fusion | flops 6452871168 | bytes 9011200 | tf_op jit(solution)/shard_map/dot_general | solution.py:86
  (56 shorter events, 17.5 us)
Async XLA Ops:
  6.5 82.7 %all-gather.2.cloned.1.call-start = ((), (), s32[]{:S(2)}) async-start(), calls=%async_computation | async-start | bytes 4456448 | tf_op jit(solution)/shard_map/all_gather | solution.py:35
  7.3 89.5 %copy-start = (bf16[512,3,512]{2,0,1:T(8,128)(2,1)S(1)}, bf16[512,3,512]{2,0,1:T(8,128)(2,1)}, u32[]{:S(2)}) copy-start(bf16[512,3,512]{2,0,1:T(8,128)(2,1)} %param.7) | copy-start | bytes 4718596
  93.3 26.3 %collective-permute-start = (bf16[256,2048]{1,0:T(8,128)(2,1)}, bf16[256,2048]{1,0:T(8,128)(2,1)}, u32[]{:S(2)}, u32[]{:S(2)}) collective-permute-start(bf16[256,2048]{1,0:T(8,128)(2,1)} %get-tuple-element.10), channel_id=1, source_target_pairs={{0,64},{64,128},{128,192},{192,0},{1,65},{65,129},{129,193},{193,1... | collective-permute-start | bytes 3145736 | tf_op jit(solution)/shard_map/ppermute | solution.py:22
  93.7 90.6 %collective-permute-start.1 = (bf16[256,2048]{1,0:T(8,128)(2,1)}, bf16[256,2048]{1,0:T(8,128)(2,1)}, u32[]{:S(2)}, u32[]{:S(2)}) collective-permute-start(bf16[256,2048]{1,0:T(8,128)(2,1)} %get-tuple-element.9), channel_id=1, source_target_pairs={{0,128},{64,192},{128,0},{192,64},{1,129},{65,193},{129,1},{193,65... | collective-permute-start | bytes 3145736 | tf_op jit(solution)/shard_map/ppermute | solution.py:22
  96.6 91.0 %collective-permute-start.2 = (bf16[256,2048]{1,0:T(8,128)(2,1)}, bf16[256,2048]{1,0:T(8,128)(2,1)}, u32[]{:S(2)}, u32[]{:S(2)}) collective-permute-start(bf16[256,2048]{1,0:T(8,128)(2,1)} %get-tuple-element.8), channel_id=1, source_target_pairs={{0,192},{64,0},{128,64},{192,128},{1,193},{65,1},{129,65},{193,129... | collective-permute-start | bytes 3145736 | tf_op jit(solution)/shard_map/ppermute | solution.py:22
  98.4 93.3 %collective-permute-start.3 = (bf16[512,1536]{0,1:T(8,128)(2,1)}, bf16[512,1536]{0,1:T(8,128)(2,1)}, u32[]{:S(2)}, u32[]{:S(2)}) collective-permute-start(bf16[512,1536]{0,1:T(8,128)(2,1)} %bitcast.47), channel_id=1, source_target_pairs={{0,16},{16,32},{32,48},{48,0},{1,17},{17,33},{33,49},{49,1},{2,18}... | collective-permute-start | bytes 4718600 | tf_op jit(solution)/shard_map/ppermute | solution.py:22
  99.9 97.8 %collective-permute-start.4 = (bf16[512,1536]{0,1:T(8,128)(2,1)}, bf16[512,1536]{0,1:T(8,128)(2,1)S(1)}, u32[]{:S(2)}, u32[]{:S(2)}) collective-permute-start(bf16[512,1536]{0,1:T(8,128)(2,1)} %bitcast.48), channel_id=1, source_target_pairs={{0,32},{16,48},{32,0},{48,16},{1,33},{17,49},{33,1},{49,17},{2,34}... | collective-permute-start | bytes 4718600 | tf_op jit(solution)/shard_map/ppermute | solution.py:22
  119.7 82.5 %collective-permute-start.5 = (bf16[512,1536]{0,1:T(8,128)(2,1)}, bf16[512,1536]{0,1:T(8,128)(2,1)}, u32[]{:S(2)}, u32[]{:S(2)}) collective-permute-start(bf16[512,1536]{0,1:T(8,128)(2,1)} %bitcast.49), channel_id=1, source_target_pairs={{0,48},{16,0},{32,16},{48,32},{1,49},{17,1},{33,17},{49,33},{2,50}... | collective-permute-start | bytes 4718600 | tf_op jit(solution)/shard_map/ppermute | solution.py:22
  187.6 2.4 copy-start.1
  209.5 3.4 %copy-start.3 = (bf16[3,3,512]{2,1,0:T(4,128)(2,1)S(1)}, bf16[3,3,512]{2,1,0:T(4,128)(2,1)}, u32[]{:S(2)}) copy-start(bf16[3,3,512]{2,1,0:T(4,128)(2,1)} %param.8) | copy-start | bytes 27652
  209.5 72.1 %copy-start.2 = (f32[512,16]{0,1:T(8,128)S(1)}, f32[512,16]{0,1:T(8,128)}, u32[]{:S(2)}) copy-start(f32[512,16]{0,1:T(8,128)} %param.9) | copy-start | bytes 98308
  209.7 54.4 %collective-permute-start.6 = (bf16[256,1536]{1,0:T(8,128)(2,1)S(1)}, bf16[256,1536]{1,0:T(8,128)(2,1)S(1)}, u32[]{:S(2)}, u32[]{:S(2)}) collective-permute-start(bf16[256,1536]{1,0:T(8,128)(2,1)S(1)} %get-tuple-element.11), channel_id=1, source_target_pairs={{0,192},{64,0},{128,64},{192,128},{1,193},{65,1},{129,65},{193,129... | collective-permute-start | bytes 2359304 | tf_op jit(solution)/shard_map/ppermute | solution.py:52
  210.0 54.1 %collective-permute-start.7 = (bf16[256,1536]{1,0:T(8,128)(2,1)S(1)}, bf16[256,1536]{1,0:T(8,128)(2,1)S(1)}, u32[]{:S(2)}, u32[]{:S(2)}) collective-permute-start(bf16[256,1536]{1,0:T(8,128)(2,1)S(1)} %get-tuple-element.13), channel_id=1, source_target_pairs={{0,128},{64,192},{128,0},{192,64},{1,129},{65,193},{129,1},{193,65... | collective-permute-start | bytes 2359304 | tf_op jit(solution)/shard_map/ppermute | solution.py:52
  211.0 66.9 %collective-permute-start.8 = (bf16[256,1536]{1,0:T(8,128)(2,1)S(1)}, bf16[256,1536]{1,0:T(8,128)(2,1)S(1)}, u32[]{:S(2)}, u32[]{:S(2)}) collective-permute-start(bf16[256,1536]{1,0:T(8,128)(2,1)S(1)} %get-tuple-element.12), channel_id=1, source_target_pairs={{0,64},{64,128},{128,192},{192,0},{1,65},{65,129},{129,193},{193,1... | collective-permute-start | bytes 2359304 | tf_op jit(solution)/shard_map/ppermute | solution.py:52
  278.2 9.2 %collective-permute-start.9 = (bf16[2,3,512]{2,0,1:T(2,128)(2,1)S(1)}, bf16[2,3,512]{2,0,1:T(2,128)(2,1)S(1)}, u32[]{:S(2)}, u32[]{:S(2)}) collective-permute-start(bf16[2,3,512]{2,0,1:T(2,128)(2,1)S(1)} %bitcast.57), channel_id=1, source_target_pairs={{0,16},{16,32},{32,48},{48,64},{64,80},{80,96},{96,112},{112,128},... | collective-permute-start | bytes 18440 | tf_op jit(solution)/shard_map/ppermute | solution.py:14
  289.8 5.2 %collective-permute-start.10 = (f32[512,16]{0,1:T(8,128)S(1)}, f32[512,16]{0,1:T(8,128)S(1)}, u32[]{:S(2)}, u32[]{:S(2)}) collective-permute-start(f32[512,16]{0,1:T(8,128)S(1)} %multiply_reduce_fusion), channel_id=1, source_target_pairs={{0,16},{16,32},{32,48},{48,0},{1,17},{17,33},{33,49},{49,1},{2,18}... | collective-permute-start | bytes 98312 | tf_op jit(solution)/shard_map/ppermute | solution.py:22
  289.9 5.5 %collective-permute-start.11 = (f32[512,16]{0,1:T(8,128)S(1)}, f32[512,16]{0,1:T(8,128)S(1)}, u32[]{:S(2)}, u32[]{:S(2)}) collective-permute-start(f32[512,16]{0,1:T(8,128)S(1)} %multiply_reduce_fusion), channel_id=1, source_target_pairs={{0,32},{16,48},{32,0},{48,16},{1,33},{17,49},{33,1},{49,17},{2,34}... | collective-permute-start | bytes 98312 | tf_op jit(solution)/shard_map/ppermute | solution.py:22
  290.5 5.6 %collective-permute-start.12 = (f32[512,16]{0,1:T(8,128)S(1)}, f32[512,16]{0,1:T(8,128)S(1)}, u32[]{:S(2)}, u32[]{:S(2)}) collective-permute-start(f32[512,16]{0,1:T(8,128)S(1)} %multiply_reduce_fusion), channel_id=1, source_target_pairs={{0,48},{16,0},{32,16},{48,32},{1,49},{17,1},{33,17},{49,33},{2,50}... | collective-permute-start | bytes 98312 | tf_op jit(solution)/shard_map/ppermute | solution.py:22
  296.2 8.4 %collective-permute-start.13 = (f32[4,512,16]{1,2,0:T(8,128)S(1)}, f32[4,512,16]{1,2,0:T(8,128)S(1)}, u32[]{:S(2)}, u32[]{:S(2)}) collective-permute-start(f32[4,512,16]{1,2,0:T(8,128)S(1)} %get-tuple-element.15), channel_id=1, source_target_pairs={{0,64},{64,128},{128,192},{192,0},{1,65},{65,129},{129,193},{193,1... | collective-permute-start | bytes 393224 | tf_op jit(solution)/shard_map/ppermute | solution.py:22
  297.2 8.8 %collective-permute-start.14 = (f32[4,512,16]{1,2,0:T(8,128)S(1)}, f32[4,512,16]{1,2,0:T(8,128)S(1)}, u32[]{:S(2)}, u32[]{:S(2)}) collective-permute-start(f32[4,512,16]{1,2,0:T(8,128)S(1)} %get-tuple-element.15), channel_id=1, source_target_pairs={{0,128},{64,192},{128,0},{192,64},{1,129},{65,193},{129,1},{193,65... | collective-permute-start | bytes 393224 | tf_op jit(solution)/shard_map/ppermute | solution.py:22
  300.3 7.9 %collective-permute-start.15 = (f32[4,512,16]{1,2,0:T(8,128)S(1)}, f32[4,512,16]{1,2,0:T(8,128)}, u32[]{:S(2)}, u32[]{:S(2)}) collective-permute-start(f32[4,512,16]{1,2,0:T(8,128)S(1)} %get-tuple-element.15), channel_id=1, source_target_pairs={{0,192},{64,0},{128,64},{192,128},{1,193},{65,1},{129,65},{193,129... | collective-permute-start | bytes 393224 | tf_op jit(solution)/shard_map/ppermute | solution.py:22
  300.5 8.7 %copy-start.5 = (f32[512,16]{0,1:T(8,128)S(1)}, f32[512,16]{0,1:T(8,128)}, u32[]{:S(2)}) copy-start(f32[512,16]{0,1:T(8,128)} %param.10) | copy-start | bytes 98308
  309.3 10.1 %copy-start.4 = (f32[512]{0:T(512)S(1)}, f32[512]{0:T(512)}, u32[]{:S(2)}) copy-start(f32[512]{0:T(512)} %param.11) | copy-start | bytes 6148
Sparse Core Ops, SparseCore 0:
  9.9 79.3 all-gather.1

commit v3 on v2

--- a/solution.py
+++ b/solution.py
@@ -23,7 +23,7 @@
     return received
 
 
-def local(tokens, in_weight, short_filter, decay_rate, residue, skip_gain):
+def block(tokens, in_weight, short_filter, decay_rate, residue, skip_gain):
     tok_rows = tokens.shape[0]
     width_local = in_weight.shape[2]
     mode_count = decay_rate.shape[1]
@@ -31,26 +31,26 @@
     across, down = lax.axis_size("x"), lax.axis_size("zl")
     me_x, me_z = lax.axis_index("x"), lax.axis_index("zl")
     flat_own = in_weight.reshape(feat_block, 3 * width_local)
-    weights = [flat_own] + ring_sends(lambda k, p: flat_own, "x", across)
+    weights = [flat_own] + ring_sends(lambda k, p: flat_own, "zl", down)
     gathered = lax.all_gather(tokens, "ch", axis=1, tiled=True)
-    chunk = gathered.shape[1] // down
+    blocks = gathered.reshape(tok_rows, -1, across, feat_block)
 
     def chunk_for(k, p):
-        return lax.dynamic_slice_in_dim(gathered, ((p + k) % down) * chunk, chunk, axis=1)
+        part = lax.dynamic_index_in_dim(blocks, (p + k) % across, axis=2, keepdims=False)
+        return part.reshape(tok_rows, -1)
 
-    rows = [chunk_for(0, me_z)] + ring_sends(chunk_for, "zl", down)
+    rows = [chunk_for(0, me_x)] + ring_sends(chunk_for, "x", across)
     column = jnp.concatenate(rows, axis=0)
     partial = jnp.zeros((column.shape[0], 3 * width_local), jnp.float32)
-    for k in range(across):
-        source = (me_x - k) % across
+    for k in range(down):
+        source = (me_z - k) % down
         taken = lax.dynamic_slice_in_dim(column, source * feat_block, feat_block, axis=1)
         partial = partial + jnp.dot(taken, weights[k], preferred_element_type=jnp.float32)
-    pieces = partial.reshape(down, tok_rows, 3 * width_local)
+    pieces = partial.reshape(across, tok_rows, 3 * width_local)
     projected = pieces[0]
-    for k in range(1, down):
-        route = [(i, (i - k) % down) for i in range(down)]
-        back = lax.ppermute(pieces[k].astype(jnp.bfloat16), "zl", route)
-        projected = projected + back.astype(jnp.float32)
+    for k in range(1, across):
+        route = [(i, (i - k) % across) for i in range(across)]
+        projected = projected + lax.ppermute(pieces[k], "x", route)
     streams = projected.astype(jnp.bfloat16).reshape(tok_rows, 3, width_local)
     tap_count = short_filter.shape[0]
     last_rows = streams[tok_rows - (tap_count - 1) :]
@@ -111,4 +111,4 @@
         P("ch"),
     )
     out_specs = P(SEQ, "ch")
-    return jax.shard_map(local, mesh=fine, in_specs=in_specs, out_specs=out_specs, check_vma=False)
+    return jax.shard_map(block, mesh=fine, in_specs=in_specs, out_specs=out_specs, check_vma=False)

time: 327 us -> 367 us (1.12)
  waiting for transfers between devices: 244 us -> 283 us
    ppermute x12, waiting for transfers between devices: 91.4 us -> 133 us  [ring_sends(): received.append(lax.ppermute(pieces(k, position), axis, route))]
  transfers between devices with their start and end apart: 17 -> 17, of which waited for: 13 -> 13; matrix products, arithmetic and copies ran while one was open for 6% -> 5% of each run, Pallas kernels for 0% -> 0%
where the time goes in v3:
time: 367 us; the launch traced here: 365 us
  waiting for transfers between devices  283 us (77%)
  matrix products  26.7 us (7%)
  starting transfers between devices  24 us (7%)
  between operations  13.7 us (4%)
  local copies, waits for them, and re-layouts  8.91 us (2%)
  other arithmetic  8.66 us (2%)
    ppermute x12, waiting for transfers between devices, ring_sends(): received.append(lax.ppermute(pieces(k, position), axis, route))  133 us
    all_gather x1, waiting for transfers between devices, block(): gathered = lax.all_gather(tokens, 'ch', axis=1, tiled=True)  80.4 us
    ppermute x3, waiting for transfers between devices, block(): projected = projected + lax.ppermute(pieces[k], 'x', route)  66.2 us
    dot_general x4, matrix products, block(): jnp.dot(taken, weights[k], preferred_element_type=jnp.float32)  16.7 us
    ppermute x12, starting transfers between devices, ring_sends(): received.append(lax.ppermute(pieces(k, position), axis, route))  15.5 us
    dot_general x1, matrix products, block(): jnp.dot(lower_mask, scaled, precision=exact_mode)  10.1 us
  transfers between devices with their start and end apart: 17, of which 13 were waited for; matrix products, arithmetic and copies ran while one was open for 5% of the time, Pallas kernels for 0%

profile of v3, /device:TPU:32, one launch (start us, length us, event | category | flops | bytes accessed | tf_op | source)
XLA Modules:
  0.0 365.4 jit_solution(17015356941709404954)
XLA Ops:
  6.5 1.8 copy.25
  8.4 80.4 %all-gather.2.cloned.1.call-done = bf16[256,8192]{0,1:T(8,128)(2,1)} async-done(((bf16[256,512]{0,1:T(8,128)(2,1)}), bf16[256,8192]{0,1:T(8,128)(2,1)}) %all-gather.2.cloned.1.call-update) | async-done | bytes 4194320 | tf_op jit(solution)/shard_map/all_gather | solution.py:35
  88.8 4.1 %constant_dynamic-slice_fusion.3 = (bf16[256,4,1,512]{0,3,2,1:T(8,128)(2,1)S(1)}, bf16[256,4,1,512]{0,3,2,1:T(8,128)(2,1)}, bf16[256,4,1,512]{0,3,2,1:T(8,128)(2,1)}, bf16[256,4,1,512]{0,3,2,1:T(8,128)(2,1)}) fusion(bf16[256,4,4,512]{0,3,2,1:T(8,128)(2,1)} %bitcast.51, s32[]{:T(128)S(6)} %select_n.87, s32[]{:T(128)S(6)} %select_n.93, s32[]{:T(128)S(6)} %select_n.91, ...), kind=kLoop, calls=%fused_computation.55 | loop fusion | bytes 8388624 | tf_op jit(solution)/shard_map/jit(dynamic_index_in_dim)/dynamic_slice | solution.py:39
  92.9 2.7 collective-permute-start.2
  99.5 2.2 collective-permute-start.3
  101.7 39.5 %collective-permute-done.2 = bf16[256,2048]{0,1:T(8,128)(2,1)} collective-permute-done((bf16[256,2048]{0,1:T(8,128)(2,1)}, bf16[256,2048]{0,1:T(8,128)(2,1)}, u32[]{:S(2)}, u32[]{:S(2)}) %collective-permute-start.2) | collective-permute-done | bytes 1048608 | tf_op jit(solution)/shard_map/ppermute | solution.py:22
  142.6 2.3 collective-permute-done
  144.9 2.2 pad_maximum_fusion
  147.3 1.9 fusion.17
  149.1 19.8 %collective-permute-done.4 = bf16[512,1536]{0,1:T(8,128)(2,1)} collective-permute-done((bf16[512,1536]{0,1:T(8,128)(2,1)}, bf16[512,1536]{0,1:T(8,128)(2,1)}, u32[]{:S(2)}, u32[]{:S(2)}) %collective-permute-start.4) | collective-permute-done | bytes 1572896 | tf_op jit(solution)/shard_map/ppermute | solution.py:22
  168.9 3.3 fusion.13
  172.2 62.1 %collective-permute-done.3 = bf16[512,1536]{0,1:T(8,128)(2,1)} collective-permute-done((bf16[512,1536]{0,1:T(8,128)(2,1)}, bf16[512,1536]{0,1:T(8,128)(2,1)}, u32[]{:S(2)}, u32[]{:S(2)}) %collective-permute-start.3) | collective-permute-done | bytes 1572896 | tf_op jit(solution)/shard_map/ppermute | solution.py:22
  234.2 5.9 %fusion.15 = f32[1024,1536]{1,0:T(8,128)} fusion(bf16[512,1536]{0,1:T(8,128)(2,1)} %collective-permute-done.3, bf16[1024,2048]{0,1:T(8,128)(2,1)S(1)} %pad_maximum_fusion, s32[]{:T(128)S(6)} %select_n.97), kind=kOutput, calls=%fused_computation.20 | convolution fusion | flops 1610612736 | bytes 8912900 | tf_op jit(solution)/shard_map/dot_general | solution.py:48
  240.1 5.6 %add_add_fusion = f32[1024,1536]{1,0:T(8,128)S(1)} fusion(f32[1024,1536]{1,0:T(8,128)S(1)} %fusion.13, f32[1024,1536]{1,0:T(8,128)S(1)} %fusion.17, f32[1024,1536]{1,0:T(8,128)} %fusion.15, bf16[512,1536]{0,1:T(8,128)(2,1)} %collective-permute-done.5, bf16[1024,2048]{0,1:T(8,128)(2,1)S(1)} %pad_maximum_fusion, s32[]{:T(128)S(6)} %select_n.101), kind=kOutput, calls=%fused_computation.5 | convolution fusion | flops 1615331328 | bytes 27787268 | tf_op jit(solution)/shard_map/dot_general | solution.py:48
  246.1 1.9 collective-permute-start.8
  248.0 2.1 collective-permute-start.7
  251.0 33.1 %collective-permute-done.8 = f32[256,1536]{1,0:T(8,128)S(1)} collective-permute-done((f32[256,1536]{1,0:T(8,128)S(1)}, f32[256,1536]{1,0:T(8,128)S(1)}, u32[]{:S(2)}, u32[]{:S(2)}) %collective-permute-start.8) | collective-permute-done | bytes 1572896 | tf_op jit(solution)/shard_map/ppermute | solution.py:53
  284.1 33.1 %collective-permute-done.7 = f32[256,1536]{1,0:T(8,128)S(1)} collective-permute-done((f32[256,1536]{1,0:T(8,128)S(1)}, f32[256,1536]{1,0:T(8,128)S(1)}, u32[]{:S(2)}, u32[]{:S(2)}) %collective-permute-start.7) | collective-permute-done | bytes 1572896 | tf_op jit(solution)/shard_map/ppermute | solution.py:53
  317.9 3.7 %collective-permute-start.9 = (bf16[2,3,512]{2,0,1:T(2,128)(2,1)S(1)}, bf16[2,3,512]{2,0,1:T(2,128)(2,1)S(1)}, u32[]{:S(2)}, u32[]{:S(2)}) collective-permute-start(bf16[2,3,512]{2,0,1:T(2,128)(2,1)S(1)} %bitcast.64), channel_id=1, source_target_pairs={{0,16},{16,32},{32,48},{48,64},{64,80},{80,96},{96,112},{112,128},... | collective-permute-start | bytes 18440 | tf_op jit(solution)/shard_map/ppermute | solution.py:14
  322.2 3.3 collective-permute-done.9
  331.9 2.3 collective-permute-done.11
  334.7 3.9 %collective-permute-start.14 = (f32[4,512,16]{1,2,0:T(8,128)S(1)}, f32[4,512,16]{1,2,0:T(8,128)S(1)}, u32[]{:S(2)}, u32[]{:S(2)}) collective-permute-start(f32[4,512,16]{1,2,0:T(8,128)S(1)} %get-tuple-element.15), channel_id=1, source_target_pairs={{0,128},{64,192},{128,0},{192,64},{1,129},{65,193},{129,1},{193,65... | collective-permute-start | bytes 393224 | tf_op jit(solution)/shard_map/ppermute | solution.py:22
  341.0 4.9 %collective-permute-done.15 = f32[4,512,16]{1,2,0:T(8,128)S(1)} collective-permute-done((f32[4,512,16]{1,2,0:T(8,128)S(1)}, f32[4,512,16]{1,2,0:T(8,128)S(1)}, u32[]{:S(2)}, u32[]{:S(2)}) %collective-permute-start.15) | collective-permute-done | bytes 131104 | tf_op jit(solution)/shard_map/ppermute | solution.py:22
  347.7 10.1 %multiply_reduce_fusion.1 = f32[256,512]{1,0:T(8,128)S(1)} fusion(f32[512,16]{0,1:T(8,128)S(1)} %exponential_multiply_fusion, f32[512,16]{0,1:T(8,128)S(1)} %neg.8, f32[512,16]{0,1:T(8,128)S(1)} %copy-done.5, f32[512,16,256]{2,1,0:T(8,128)S(1)} %bitcast.50), kind=kOutput, calls=%fused_computation.4 | convolution fusion | flops 6452871168 | bytes 9011200 | tf_op jit(solution)/shard_map/dot_general | solution.py:86
  (57 shorter events, 19.7 us)
Async XLA Ops:
  6.5 82.3 %all-gather.2.cloned.1.call-start = ((), (), s32[]{:S(2)}) async-start(), calls=%async_computation | async-start | bytes 4456448 | tf_op jit(solution)/shard_map/all_gather | solution.py:35
  88.8 8.5 %copy-start = (bf16[512,3,512]{2,0,1:T(8,128)(2,1)S(1)}, bf16[512,3,512]{2,0,1:T(8,128)(2,1)}, u32[]{:S(2)}) copy-start(bf16[512,3,512]{2,0,1:T(8,128)(2,1)} %param.7) | copy-start | bytes 4718596
  92.9 48.3 %collective-permute-start.2 = (bf16[256,2048]{0,1:T(8,128)(2,1)}, bf16[256,2048]{0,1:T(8,128)(2,1)}, u32[]{:S(2)}, u32[]{:S(2)}) collective-permute-start(bf16[256,2048]{0,1:T(8,128)(2,1)} %bitcast.7), channel_id=1, source_target_pairs={{0,48},{16,0},{32,16},{48,32},{1,49},{17,1},{33,17},{49,33},{2,50}... | collective-permute-start | bytes 3145736 | tf_op jit(solution)/shard_map/ppermute | solution.py:22
  95.6 47.0 %collective-permute-start.1 = (bf16[256,2048]{0,1:T(8,128)(2,1)}, bf16[256,2048]{0,1:T(8,128)(2,1)}, u32[]{:S(2)}, u32[]{:S(2)}) collective-permute-start(bf16[256,2048]{0,1:T(8,128)(2,1)} %bitcast.6), channel_id=1, source_target_pairs={{0,32},{16,48},{32,0},{48,16},{1,33},{17,49},{33,1},{49,17},{2,34}... | collective-permute-start | bytes 3145736 | tf_op jit(solution)/shard_map/ppermute | solution.py:22
  96.4 48.5 %collective-permute-start = (bf16[256,2048]{0,1:T(8,128)(2,1)}, bf16[256,2048]{0,1:T(8,128)(2,1)}, u32[]{:S(2)}, u32[]{:S(2)}) collective-permute-start(bf16[256,2048]{0,1:T(8,128)(2,1)} %bitcast.5), channel_id=1, source_target_pairs={{0,16},{16,32},{32,48},{48,0},{1,17},{17,33},{33,49},{49,1},{2,18}... | collective-permute-start | bytes 3145736 | tf_op jit(solution)/shard_map/ppermute | solution.py:22
  98.9 70.0 %collective-permute-start.4 = (bf16[512,1536]{0,1:T(8,128)(2,1)}, bf16[512,1536]{0,1:T(8,128)(2,1)}, u32[]{:S(2)}, u32[]{:S(2)}) collective-permute-start(bf16[512,1536]{0,1:T(8,128)(2,1)} %bitcast.54), channel_id=1, source_target_pairs={{0,128},{64,192},{128,0},{192,64},{1,129},{65,193},{129,1},{193,65... | collective-permute-start | bytes 4718600 | tf_op jit(solution)/shard_map/ppermute | solution.py:22
  99.5 134.7 %collective-permute-start.3 = (bf16[512,1536]{0,1:T(8,128)(2,1)}, bf16[512,1536]{0,1:T(8,128)(2,1)}, u32[]{:S(2)}, u32[]{:S(2)}) collective-permute-start(bf16[512,1536]{0,1:T(8,128)(2,1)} %bitcast.55), channel_id=1, source_target_pairs={{0,64},{64,128},{128,192},{192,0},{1,65},{65,129},{129,193},{193,1... | collective-permute-start | bytes 4718600 | tf_op jit(solution)/shard_map/ppermute | solution.py:22
  141.2 98.9 %collective-permute-start.5 = (bf16[512,1536]{0,1:T(8,128)(2,1)}, bf16[512,1536]{0,1:T(8,128)(2,1)}, u32[]{:S(2)}, u32[]{:S(2)}) collective-permute-start(bf16[512,1536]{0,1:T(8,128)(2,1)} %bitcast.56), channel_id=1, source_target_pairs={{0,192},{64,0},{128,64},{192,128},{1,193},{65,1},{129,65},{193,129... | collective-permute-start | bytes 4718600 | tf_op jit(solution)/shard_map/ppermute | solution.py:22
  144.9 2.4 copy-start.1
  245.8 5.2 %copy-start.3 = (bf16[3,3,512]{2,1,0:T(4,128)(2,1)S(1)}, bf16[3,3,512]{2,1,0:T(4,128)(2,1)}, u32[]{:S(2)}) copy-start(bf16[3,3,512]{2,1,0:T(4,128)(2,1)} %param.8) | copy-start | bytes 27652
  246.1 75.5 %copy-start.2 = (f32[512,16]{0,1:T(8,128)S(1)}, f32[512,16]{0,1:T(8,128)}, u32[]{:S(2)}) copy-start(f32[512,16]{0,1:T(8,128)} %param.9) | copy-start | bytes 98308
  246.1 38.0 %collective-permute-start.8 = (f32[256,1536]{1,0:T(8,128)S(1)}, f32[256,1536]{1,0:T(8,128)S(1)}, u32[]{:S(2)}, u32[]{:S(2)}) collective-permute-start(f32[256,1536]{1,0:T(8,128)S(1)} %get-tuple-element.8), channel_id=1, source_target_pairs={{0,16},{16,32},{32,48},{48,0},{1,17},{17,33},{33,49},{49,1},{2,18}... | collective-permute-start | bytes 4718600 | tf_op jit(solution)/shard_map/ppermute | solution.py:53
  248.0 69.2 %collective-permute-start.7 = (f32[256,1536]{1,0:T(8,128)S(1)}, f32[256,1536]{1,0:T(8,128)S(1)}, u32[]{:S(2)}, u32[]{:S(2)}) collective-permute-start(f32[256,1536]{1,0:T(8,128)S(1)} %get-tuple-element.9), channel_id=1, source_target_pairs={{0,32},{16,48},{32,0},{48,16},{1,33},{17,49},{33,1},{49,17},{2,34}... | collective-permute-start | bytes 4718600 | tf_op jit(solution)/shard_map/ppermute | solution.py:53
  250.0 67.2 %collective-permute-start.6 = (f32[256,1536]{1,0:T(8,128)S(1)}, f32[256,1536]{1,0:T(8,128)S(1)}, u32[]{:S(2)}, u32[]{:S(2)}) collective-permute-start(f32[256,1536]{1,0:T(8,128)S(1)} %get-tuple-element.7), channel_id=1, source_target_pairs={{0,48},{16,0},{32,16},{48,32},{1,49},{17,1},{33,17},{49,33},{2,50}... | collective-permute-start | bytes 4718600 | tf_op jit(solution)/shard_map/ppermute | solution.py:53
  317.9 7.6 %collective-permute-start.9 = (bf16[2,3,512]{2,0,1:T(2,128)(2,1)S(1)}, bf16[2,3,512]{2,0,1:T(2,128)(2,1)S(1)}, u32[]{:S(2)}, u32[]{:S(2)}) collective-permute-start(bf16[2,3,512]{2,0,1:T(2,128)(2,1)S(1)} %bitcast.64), channel_id=1, source_target_pairs={{0,16},{16,32},{32,48},{48,64},{64,80},{80,96},{96,112},{112,128},... | collective-permute-start | bytes 18440 | tf_op jit(solution)/shard_map/ppermute | solution.py:14
  327.9 4.0 %collective-permute-start.12 = (f32[512,16]{0,1:T(8,128)S(1)}, f32[512,16]{0,1:T(8,128)S(1)}, u32[]{:S(2)}, u32[]{:S(2)}) collective-permute-start(f32[512,16]{0,1:T(8,128)S(1)} %multiply_reduce_fusion), channel_id=1, source_target_pairs={{0,48},{16,0},{32,16},{48,32},{1,49},{17,1},{33,17},{49,33},{2,50}... | collective-permute-start | bytes 98312 | tf_op jit(solution)/shard_map/ppermute | solution.py:22
  328.7 5.4 %collective-permute-start.11 = (f32[512,16]{0,1:T(8,128)S(1)}, f32[512,16]{0,1:T(8,128)S(1)}, u32[]{:S(2)}, u32[]{:S(2)}) collective-permute-start(f32[512,16]{0,1:T(8,128)S(1)} %multiply_reduce_fusion), channel_id=1, source_target_pairs={{0,32},{16,48},{32,0},{48,16},{1,33},{17,49},{33,1},{49,17},{2,34}... | collective-permute-start | bytes 98312 | tf_op jit(solution)/shard_map/ppermute | solution.py:22
  329.5 5.1 %collective-permute-start.10 = (f32[512,16]{0,1:T(8,128)S(1)}, f32[512,16]{0,1:T(8,128)S(1)}, u32[]{:S(2)}, u32[]{:S(2)}) collective-permute-start(f32[512,16]{0,1:T(8,128)S(1)} %multiply_reduce_fusion), channel_id=1, source_target_pairs={{0,16},{16,32},{32,48},{48,0},{1,17},{17,33},{33,49},{49,1},{2,18}... | collective-permute-start | bytes 98312 | tf_op jit(solution)/shard_map/ppermute | solution.py:22
  334.6 11.3 %collective-permute-start.15 = (f32[4,512,16]{1,2,0:T(8,128)S(1)}, f32[4,512,16]{1,2,0:T(8,128)S(1)}, u32[]{:S(2)}, u32[]{:S(2)}) collective-permute-start(f32[4,512,16]{1,2,0:T(8,128)S(1)} %get-tuple-element.15), channel_id=1, source_target_pairs={{0,192},{64,0},{128,64},{192,128},{1,193},{65,1},{129,65},{193,129... | collective-permute-start | bytes 393224 | tf_op jit(solution)/shard_map/ppermute | solution.py:22
  334.7 11.2 %collective-permute-start.14 = (f32[4,512,16]{1,2,0:T(8,128)S(1)}, f32[4,512,16]{1,2,0:T(8,128)S(1)}, u32[]{:S(2)}, u32[]{:S(2)}) collective-permute-start(f32[4,512,16]{1,2,0:T(8,128)S(1)} %get-tuple-element.15), channel_id=1, source_target_pairs={{0,128},{64,192},{128,0},{192,64},{1,129},{65,193},{129,1},{193,65... | collective-permute-start | bytes 393224 | tf_op jit(solution)/shard_map/ppermute | solution.py:22
  338.6 7.9 %collective-permute-start.13 = (f32[4,512,16]{1,2,0:T(8,128)S(1)}, f32[4,512,16]{1,2,0:T(8,128)}, u32[]{:S(2)}, u32[]{:S(2)}) collective-permute-start(f32[4,512,16]{1,2,0:T(8,128)S(1)} %get-tuple-element.15), channel_id=1, source_target_pairs={{0,64},{64,128},{128,192},{192,0},{1,65},{65,129},{129,193},{193,1... | collective-permute-start | bytes 393224 | tf_op jit(solution)/shard_map/ppermute | solution.py:22
  339.7 7.9 %copy-start.5 = (f32[512,16]{0,1:T(8,128)S(1)}, f32[512,16]{0,1:T(8,128)}, u32[]{:S(2)}) copy-start(f32[512,16]{0,1:T(8,128)} %param.10) | copy-start | bytes 98308
  347.7 10.1 %copy-start.4 = (f32[512]{0:T(512)S(1)}, f32[512]{0:T(512)}, u32[]{:S(2)}) copy-start(f32[512]{0:T(512)} %param.11) | copy-start | bytes 6148
Sparse Core Ops, SparseCore 0:
  10.0 78.7 all-gather.1

commit v4 on v3

--- a/solution.py
+++ b/solution.py
@@ -6,6 +6,8 @@
 
 exact_mode = lax.Precision.HIGHEST
 SEQ = ("zl", "x")
+SUB = ("zh", "c")
+CH = ("y", "zh", "c")
 
 
 def from_behind(block, axis, distance):
@@ -32,25 +34,22 @@
     me_x, me_z = lax.axis_index("x"), lax.axis_index("zl")
     flat_own = in_weight.reshape(feat_block, 3 * width_local)
     weights = [flat_own] + ring_sends(lambda k, p: flat_own, "zl", down)
-    gathered = lax.all_gather(tokens, "ch", axis=1, tiled=True)
+    swap = [(a * across + b, b * across + a) for a in range(across) for b in range(across)]
+    moved = lax.ppermute(tokens, ("x",) + SUB, swap)
+    gathered = lax.all_gather(moved, CH, axis=1, tiled=True)
     blocks = gathered.reshape(tok_rows, -1, across, feat_block)
-
-    def chunk_for(k, p):
-        part = lax.dynamic_index_in_dim(blocks, (p + k) % across, axis=2, keepdims=False)
-        return part.reshape(tok_rows, -1)
-
-    rows = [chunk_for(0, me_x)] + ring_sends(chunk_for, "x", across)
-    column = jnp.concatenate(rows, axis=0)
-    partial = jnp.zeros((column.shape[0], 3 * width_local), jnp.float32)
+    partial = jnp.zeros((across, tok_rows, 3 * width_local), jnp.float32)
     for k in range(down):
         source = (me_z - k) % down
-        taken = lax.dynamic_slice_in_dim(column, source * feat_block, feat_block, axis=1)
-        partial = partial + jnp.dot(taken, weights[k], preferred_element_type=jnp.float32)
-    pieces = partial.reshape(across, tok_rows, 3 * width_local)
-    projected = pieces[0]
+        taken = lax.dynamic_index_in_dim(blocks, source, axis=1, keepdims=False)
+        partial = partial + jnp.einsum(
+            "rtu,uc->trc", taken, weights[k], preferred_element_type=jnp.float32
+        )
+    projected = lax.dynamic_index_in_dim(partial, me_x, axis=0, keepdims=False)
     for k in range(1, across):
-        route = [(i, (i - k) % across) for i in range(across)]
-        projected = projected + lax.ppermute(pieces[k], "x", route)
+        route = [(i, (i + k) % across) for i in range(across)]
+        piece = lax.dynamic_index_in_dim(partial, (me_x + k) % across, axis=0, keepdims=False)
+        projected = projected + lax.ppermute(piece, "x", route)
     streams = projected.astype(jnp.bfloat16).reshape(tok_rows, 3, width_local)
     tap_count = short_filter.shape[0]
     last_rows = streams[tok_rows - (tap_count - 1) :]
@@ -95,20 +94,19 @@
 
 def split_mesh(mesh):
     ctx, ch = mesh.shape["ctx"], mesh.shape["ch"]
-    inner = 4 if ctx % 4 == 0 else 1
-    devices = np.asarray(mesh.devices).reshape(ctx // inner, inner, ch)
-    return Mesh(devices, ("zl", "x", "ch"))
+    devices = np.asarray(mesh.devices).reshape(ctx // 4, 4, ch // 4, 2, 2)
+    return Mesh(devices, SEQ + CH)
 
 
 def solution(mesh):
     fine = split_mesh(mesh)
     in_specs = (
-        P(SEQ, "ch"),
-        P(SEQ, None, "ch"),
-        P(None, None, "ch"),
-        P("ch", None),
-        P("ch", None),
-        P("ch"),
+        P(SEQ, CH),
+        P(SEQ, None, CH),
+        P(None, None, CH),
+        P(CH, None),
+        P(CH, None),
+        P(CH),
     )
-    out_specs = P(SEQ, "ch")
+    out_specs = P(SEQ, CH)
     return jax.shard_map(block, mesh=fine, in_specs=in_specs, out_specs=out_specs, check_vma=False)

time: 367 us -> 328 us (0.89)
  waiting for transfers between devices: 283 us -> 226 us
  starting transfers between devices: 24 us -> 37.4 us
  local copies, waits for them, and re-layouts: 8.91 us -> 20.3 us
  matrix products: 26.7 us -> 21.8 us
    ppermute x12 -> x9, waiting for transfers between devices: 133 us -> 31.8 us  [ring_sends(): received.append(lax.ppermute(pieces(k, position), axis, route))]
    all_gather x1, waiting for transfers between devices: 80.4 us -> 123 us  [block(): gathered = lax.all_gather(moved, CH, axis=1, tiled=True)]
    ppermute x3 -> x4, starting transfers between devices: 4.82 us -> 20.7 us  [the longest x3 19.1 us: block(): projected = projected + lax.ppermute(piece, 'x', route)]
    reshape x0 -> x2, local copies, waits for them, and re-layouts: none -> 8.57 us  [the longest x1 7.86 us: block(): blocks = gathered.reshape(tok_rows, -1, across, feat_block)]
    dot_general x4, matrix products: 16.7 us -> 11.7 us  [block(): jnp.einsum('rtu,uc->trc', taken, weights[k], preferred_element_type=jnp.f...]
    ppermute x12 -> x9, starting transfers between devices: 15.5 us -> 14.3 us  [ring_sends(): received.append(lax.ppermute(pieces(k, position), axis, route))]
    ppermute x3 -> x4, waiting for transfers between devices: 66.2 us -> 66.3 us  [the longest x3 66.3 us: block(): projected = projected + lax.ppermute(piece, 'x', route)]
  transfers between devices with their start and end apart: 17 -> 15, of which waited for: 13 -> 11; matrix products, arithmetic and copies ran while one was open for 5% -> 8% of each run, Pallas kernels for 0% -> 0%
where the time goes in v4:
time: 328 us
  waiting for transfers between devices  226 us (69%)
  starting transfers between devices  37.4 us (11%)
  matrix products  21.8 us (7%)
  local copies, waits for them, and re-layouts  20.3 us (6%)
  between operations  13.7 us (4%)
  other arithmetic  8.65 us (3%)
    all_gather x1, waiting for transfers between devices, block(): gathered = lax.all_gather(moved, CH, axis=1, tiled=True)  123 us
    ppermute x3, waiting for transfers between devices, block(): projected = projected + lax.ppermute(piece, 'x', route)  66.3 us
    ppermute x9, waiting for transfers between devices, ring_sends(): received.append(lax.ppermute(pieces(k, position), axis, route))  31.8 us
    ppermute x3, starting transfers between devices, block(): projected = projected + lax.ppermute(piece, 'x', route)  19.1 us
    ppermute x9, starting transfers between devices, ring_sends(): received.append(lax.ppermute(pieces(k, position), axis, route))  14.3 us
    dot_general x4, matrix products, block(): jnp.einsum('rtu,uc->trc', taken, weights[k], preferred_element_type=jnp.f...  11.7 us
    dot_general x1, matrix products, block(): jnp.dot(lower_mask, scaled, precision=exact_mode)  10.1 us
    reshape x1, local copies, waits for them, and re-layouts, block(): blocks = gathered.reshape(tok_rows, -1, across, feat_block)  7.86 us
  transfers between devices with their start and end apart: 15, of which 11 were waited for; matrix products, arithmetic and copies ran while one was open for 8% of the time, Pallas kernels for 0%

profile of v4, /device:TPU:32, one launch (start us, length us, event | category | flops | bytes accessed | tf_op | source)
XLA Modules:
  0.0 327.7 jit_solution(11930890407086777361)
XLA Ops:
  11.3 2.0 collective-permute-start.1
  13.3 2.3 collective-permute-start.2
  16.7 123.2 %all-gather.2.cloned.1.call-done = bf16[256,8192]{1,0:T(8,128)(2,1)} async-done(((bf16[256,512]{1,0:T(8,128)(2,1)}), bf16[256,8192]{1,0:T(8,128)(2,1)}) %all-gather.2.cloned.1.call-update) | async-done | bytes 4194320 | tf_op jit(solution)/shard_map/all_gather | solution.py:39
  139.9 7.9 %reshape.153 = bf16[256,4,4,512]{3,2,1,0:T(4,128)(2,1)} reshape(bf16[256,8192]{1,0:T(8,128)(2,1)} %all-gather.2.cloned.1.call-done) | data formatting | bytes 8388608 | tf_op jit(solution)/shard_map/reshape | solution.py:40
  147.8 4.6 %constant_dynamic-slice_fusion = (bf16[256,1,4,512]{3,2,1,0:T(4,128)(2,1)}, bf16[256,1,4,512]{3,2,1,0:T(4,128)(2,1)S(1)}, bf16[256,1,4,512]{3,2,1,0:T(4,128)(2,1)S(1)}, bf16[256,1,4,512]{3,2,1,0:T(4,128)(2,1)S(1)}) fusion(bf16[256,4,4,512]{3,2,1,0:T(4,128)(2,1)} %reshape.153, s32[]{:T(128)S(6)} %select_n.90, s32[]{:T(128)S(6)} %select_n.88, ...), kind=kLoop, calls=%fused_computation.53 | loop fusion | bytes 8388624 | tf_op jit(solution)/shard_map/jit(dynamic_index_in_dim)/dynamic_slice | solution.py:44
  152.4 1.8 fusion.17
  154.3 3.2 fusion.15
  157.5 20.3 %collective-permute-done.2 = bf16[512,1536]{1,0:T(8,128)(2,1)} collective-permute-done((bf16[512,1536]{1,0:T(8,128)(2,1)S(1)}, bf16[512,1536]{1,0:T(8,128)(2,1)}, u32[]{:S(2)}, u32[]{:S(2)}) %collective-permute-start.2) | collective-permute-done | bytes 1572896 | tf_op jit(solution)/shard_map/ppermute | solution.py:24
  177.8 3.3 %fusion.13 = f32[256,4,1536]{2,0,1:T(8,128)S(1)} fusion(bf16[512,1536]{1,0:T(8,128)(2,1)} %collective-permute-done.2, bf16[256,1,4,512]{3,2,1,0:T(4,128)(2,1)S(1)} %get-tuple-element.11), kind=kOutput, calls=%fused_computation.17 | convolution fusion | flops 1610612736 | bytes 8912896 | tf_op jit(solution)/shard_map/rtu,uc->trc/dot_general | solution.py:45
  181.1 3.9 %collective-permute-done.3 = bf16[512,1536]{1,0:T(8,128)(2,1)} collective-permute-done((bf16[512,1536]{1,0:T(8,128)(2,1)S(1)}, bf16[512,1536]{1,0:T(8,128)(2,1)}, u32[]{:S(2)}, u32[]{:S(2)}) %collective-permute-start.3) | collective-permute-done | bytes 1572896 | tf_op jit(solution)/shard_map/ppermute | solution.py:24
  185.0 3.4 %add_add_fusion = f32[256,4,1536]{2,0,1:T(8,128)S(1)} fusion(f32[256,4,1536]{2,0,1:T(8,128)S(1)} %fusion.13, f32[256,4,1536]{2,0,1:T(8,128)S(1)} %fusion.17, f32[256,4,1536]{2,0,1:T(8,128)S(1)} %fusion.15, bf16[512,1536]{1,0:T(8,128)(2,1)} %collective-permute-done.3, bf16[256,1,4,512]{3,2,1,0:T(4,128)(2,1)S(1)} %copy-done.1), kind=kOutput, calls=%fused_computation.5 | convolution fusion | flops 1615331328 | bytes 27787264 | tf_op jit(solution)/shard_map/rtu,uc->trc/dot_general | solution.py:45
  188.5 2.3 dynamic-slice_bitcast_fusion.2
  193.6 16.8 %collective-permute-start.5 = (f32[256,1536]{1,0:T(8,128)}, f32[256,1536]{1,0:T(8,128)}, u32[]{:S(2)}, u32[]{:S(2)}) collective-permute-start(f32[256,1536]{1,0:T(8,128)} %get-tuple-element.9), channel_id=1, source_target_pairs={{0,32},{16,48},{32,0},{48,16},{1,33},{17,49},{33,1},{49,17},{2,34}... | collective-permute-start | bytes 4718600 | tf_op jit(solution)/shard_map/ppermute | solution.py:52
  211.1 32.3 %collective-permute-done.4 = f32[256,1536]{1,0:T(8,128)S(1)} collective-permute-done((f32[256,1536]{1,0:T(8,128)}, f32[256,1536]{1,0:T(8,128)S(1)}, u32[]{:S(2)}, u32[]{:S(2)}) %collective-permute-start.4) | collective-permute-done | bytes 1572896 | tf_op jit(solution)/shard_map/ppermute | solution.py:52
  243.4 34.0 %collective-permute-done.5 = f32[256,1536]{1,0:T(8,128)} collective-permute-done((f32[256,1536]{1,0:T(8,128)}, f32[256,1536]{1,0:T(8,128)}, u32[]{:S(2)}, u32[]{:S(2)}) %collective-permute-start.5) | collective-permute-done | bytes 1572896 | tf_op jit(solution)/shard_map/ppermute | solution.py:52
  277.4 2.9 fusion.8
  280.3 2.4 collective-permute-start.7
  283.3 4.6 %collective-permute-done.7 = bf16[2,3,512]{2,0,1:T(2,128)(2,1)S(1)} collective-permute-done((bf16[2,3,512]{2,0,1:T(2,128)(2,1)S(1)}, bf16[2,3,512]{2,0,1:T(2,128)(2,1)S(1)}, u32[]{:S(2)}, u32[]{:S(2)}) %collective-permute-start.7) | collective-permute-done | bytes 6176 | tf_op jit(solution)/shard_map/ppermute | solution.py:16
  291.8 1.8 collective-permute-start.10
  298.2 2.2 collective-permute-start.12
  300.4 1.9 collective-permute-start.13
  303.9 2.6 collective-permute-done.12
  306.5 2.1 collective-permute-done.13
  309.9 10.1 %multiply_reduce_fusion.1 = f32[256,512]{1,0:T(8,128)S(1)} fusion(f32[512,16]{0,1:T(8,128)S(1)} %exponential_multiply_fusion, f32[512,16]{0,1:T(8,128)S(1)} %neg.8, f32[512,16]{0,1:T(8,128)S(1)} %copy-done.6, f32[512,16,256]{2,1,0:T(8,128)S(1)} %bitcast.81), kind=kOutput, calls=%fused_computation.4 | convolution fusion | flops 6452871168 | bytes 9011200 | tf_op jit(solution)/shard_map/dot_general | solution.py:85
  (55 shorter events, 22.0 us)
Async XLA Ops:
  6.5 133.4 %all-gather.2.cloned.1.call-start = ((), (), s32[]{:S(2)}) async-start(), calls=%async_computation | async-start | bytes 4456448 | tf_op jit(solution)/shard_map/all_gather | solution.py:39
  6.5 1.6 collective-permute-start
  8.1 0.7 copy-start.3
  11.3 143.0 %collective-permute-start.1 = (bf16[512,1536]{1,0:T(8,128)(2,1)S(1)}, bf16[512,1536]{1,0:T(8,128)(2,1)}, u32[]{:S(2)}, u32[]{:S(2)}) collective-permute-start(bf16[512,1536]{1,0:T(8,128)(2,1)S(1)} %copy.60), channel_id=1, source_target_pairs={{0,64},{64,128},{128,192},{192,0},{1,65},{65,129},{129,193},{193,1... | collective-permute-start | bytes 4718600 | tf_op jit(solution)/shard_map/ppermute | solution.py:24
  13.3 164.5 %collective-permute-start.2 = (bf16[512,1536]{1,0:T(8,128)(2,1)S(1)}, bf16[512,1536]{1,0:T(8,128)(2,1)}, u32[]{:S(2)}, u32[]{:S(2)}) collective-permute-start(bf16[512,1536]{1,0:T(8,128)(2,1)S(1)} %copy.60), channel_id=1, source_target_pairs={{0,128},{64,192},{128,0},{192,64},{1,129},{65,193},{129,1},{193,65... | collective-permute-start | bytes 4718600 | tf_op jit(solution)/shard_map/ppermute | solution.py:24
  15.6 169.5 %collective-permute-start.3 = (bf16[512,1536]{1,0:T(8,128)(2,1)S(1)}, bf16[512,1536]{1,0:T(8,128)(2,1)}, u32[]{:S(2)}, u32[]{:S(2)}) collective-permute-start(bf16[512,1536]{1,0:T(8,128)(2,1)S(1)} %copy.60), channel_id=1, source_target_pairs={{0,192},{64,0},{128,64},{192,128},{1,193},{65,1},{129,65},{193,129... | collective-permute-start | bytes 4718600 | tf_op jit(solution)/shard_map/ppermute | solution.py:24
  177.8 7.2 %copy-start.1 = (bf16[256,1,4,512]{3,2,1,0:T(4,128)(2,1)S(1)}, bf16[256,1,4,512]{3,2,1,0:T(4,128)(2,1)}, u32[]{:S(2)}) copy-start(bf16[256,1,4,512]{3,2,1,0:T(4,128)(2,1)} %get-tuple-element.10) | copy-start | bytes 3145732
  188.4 3.6 %copy-start = (f32[256,4,1536]{2,0,1:T(8,128)}, f32[256,4,1536]{2,0,1:T(8,128)S(1)}, u32[]{:S(2)}) copy-start(f32[256,4,1536]{2,0,1:T(8,128)S(1)} %add_add_fusion) | copy-start | bytes 18874372
  188.4 22.7 %copy-start.4 = (bf16[3,3,512]{2,1,0:T(4,128)(2,1)S(1)}, bf16[3,3,512]{2,1,0:T(4,128)(2,1)}, u32[]{:S(2)}) copy-start(bf16[3,3,512]{2,1,0:T(4,128)(2,1)} %param.8) | copy-start | bytes 27652
  192.0 51.4 %collective-permute-start.4 = (f32[256,1536]{1,0:T(8,128)}, f32[256,1536]{1,0:T(8,128)S(1)}, u32[]{:S(2)}, u32[]{:S(2)}) collective-permute-start(f32[256,1536]{1,0:T(8,128)} %get-tuple-element.7), channel_id=1, source_target_pairs={{0,16},{16,32},{32,48},{48,0},{1,17},{17,33},{33,49},{49,1},{2,18}... | collective-permute-start | bytes 4718600 | tf_op jit(solution)/shard_map/ppermute | solution.py:52
  193.6 83.8 %collective-permute-start.5 = (f32[256,1536]{1,0:T(8,128)}, f32[256,1536]{1,0:T(8,128)}, u32[]{:S(2)}, u32[]{:S(2)}) collective-permute-start(f32[256,1536]{1,0:T(8,128)} %get-tuple-element.9), channel_id=1, source_target_pairs={{0,32},{16,48},{32,0},{48,16},{1,33},{17,49},{33,1},{49,17},{2,34}... | collective-permute-start | bytes 4718600 | tf_op jit(solution)/shard_map/ppermute | solution.py:52
  210.4 67.1 %collective-permute-start.6 = (f32[256,1536]{1,0:T(8,128)S(1)}, f32[256,1536]{1,0:T(8,128)}, u32[]{:S(2)}, u32[]{:S(2)}) collective-permute-start(f32[256,1536]{1,0:T(8,128)S(1)} %get-tuple-element.8), channel_id=1, source_target_pairs={{0,48},{16,0},{32,16},{48,32},{1,49},{17,1},{33,17},{49,33},{2,50}... | collective-permute-start | bytes 4718600 | tf_op jit(solution)/shard_map/ppermute | solution.py:52
  211.1 71.6 %copy-start.2 = (f32[512,16]{0,1:T(8,128)S(1)}, f32[512,16]{0,1:T(8,128)}, u32[]{:S(2)}) copy-start(f32[512,16]{0,1:T(8,128)} %param.9) | copy-start | bytes 98308
  280.3 7.6 %collective-permute-start.7 = (bf16[2,3,512]{2,0,1:T(2,128)(2,1)S(1)}, bf16[2,3,512]{2,0,1:T(2,128)(2,1)S(1)}, u32[]{:S(2)}, u32[]{:S(2)}) collective-permute-start(bf16[2,3,512]{2,0,1:T(2,128)(2,1)S(1)} %bitcast.90), channel_id=1, source_target_pairs={{0,16},{16,32},{32,48},{48,64},{64,80},{80,96},{96,112},{112,128},... | collective-permute-start | bytes 18440 | tf_op jit(solution)/shard_map/ppermute | solution.py:16
  290.3 5.2 %collective-permute-start.8 = (f32[512,16]{0,1:T(8,128)S(1)}, f32[512,16]{0,1:T(8,128)S(1)}, u32[]{:S(2)}, u32[]{:S(2)}) collective-permute-start(f32[512,16]{0,1:T(8,128)S(1)} %multiply_reduce_fusion), channel_id=1, source_target_pairs={{0,16},{16,32},{32,48},{48,0},{1,17},{17,33},{33,49},{49,1},{2,18}... | collective-permute-start | bytes 98312 | tf_op jit(solution)/shard_map/ppermute | solution.py:24
  290.4 5.5 %collective-permute-start.9 = (f32[512,16]{0,1:T(8,128)S(1)}, f32[512,16]{0,1:T(8,128)S(1)}, u32[]{:S(2)}, u32[]{:S(2)}) collective-permute-start(f32[512,16]{0,1:T(8,128)S(1)} %multiply_reduce_fusion), channel_id=1, source_target_pairs={{0,32},{16,48},{32,0},{48,16},{1,33},{17,49},{33,1},{49,17},{2,34}... | collective-permute-start | bytes 98312 | tf_op jit(solution)/shard_map/ppermute | solution.py:24
  291.8 4.9 %collective-permute-start.10 = (f32[512,16]{0,1:T(8,128)S(1)}, f32[512,16]{0,1:T(8,128)S(1)}, u32[]{:S(2)}, u32[]{:S(2)}) collective-permute-start(f32[512,16]{0,1:T(8,128)S(1)} %multiply_reduce_fusion), channel_id=1, source_target_pairs={{0,48},{16,0},{32,16},{48,32},{1,49},{17,1},{33,17},{49,33},{2,50}... | collective-permute-start | bytes 98312 | tf_op jit(solution)/shard_map/ppermute | solution.py:24
  296.7 7.2 %collective-permute-start.11 = (f32[4,512,16]{1,2,0:T(8,128)S(1)}, f32[4,512,16]{1,2,0:T(8,128)S(1)}, u32[]{:S(2)}, u32[]{:S(2)}) collective-permute-start(f32[4,512,16]{1,2,0:T(8,128)S(1)} %get-tuple-element.15), channel_id=1, source_target_pairs={{0,64},{64,128},{128,192},{192,0},{1,65},{65,129},{129,193},{193,1... | collective-permute-start | bytes 393224 | tf_op jit(solution)/shard_map/ppermute | solution.py:24
  298.2 8.4 %collective-permute-start.12 = (f32[4,512,16]{1,2,0:T(8,128)S(1)}, f32[4,512,16]{1,2,0:T(8,128)}, u32[]{:S(2)}, u32[]{:S(2)}) collective-permute-start(f32[4,512,16]{1,2,0:T(8,128)S(1)} %get-tuple-element.15), channel_id=1, source_target_pairs={{0,128},{64,192},{128,0},{192,64},{1,129},{65,193},{129,1},{193,65... | collective-permute-start | bytes 393224 | tf_op jit(solution)/shard_map/ppermute | solution.py:24
  300.4 8.3 %collective-permute-start.13 = (f32[4,512,16]{1,2,0:T(8,128)S(1)}, f32[4,512,16]{1,2,0:T(8,128)}, u32[]{:S(2)}, u32[]{:S(2)}) collective-permute-start(f32[4,512,16]{1,2,0:T(8,128)S(1)} %get-tuple-element.15), channel_id=1, source_target_pairs={{0,192},{64,0},{128,64},{192,128},{1,193},{65,1},{129,65},{193,129... | collective-permute-start | bytes 393224 | tf_op jit(solution)/shard_map/ppermute | solution.py:24
  302.6 7.3 %copy-start.6 = (f32[512,16]{0,1:T(8,128)S(1)}, f32[512,16]{0,1:T(8,128)}, u32[]{:S(2)}) copy-start(f32[512,16]{0,1:T(8,128)} %param.10) | copy-start | bytes 98308
  309.9 10.1 %copy-start.5 = (f32[512]{0:T(512)S(1)}, f32[512]{0:T(512)}, u32[]{:S(2)}) copy-start(f32[512]{0:T(512)} %param.11) | copy-start | bytes 6148
Sparse Core Ops, SparseCore 0:
  9.9 129.9 all-gather.1

commit v5 on v4

--- a/solution.py
+++ b/solution.py
@@ -34,17 +34,28 @@
     me_x, me_z = lax.axis_index("x"), lax.axis_index("zl")
     flat_own = in_weight.reshape(feat_block, 3 * width_local)
     weights = [flat_own] + ring_sends(lambda k, p: flat_own, "zl", down)
+    halves = lax.axis_size("zh")
+    pair = lax.axis_size("c")
+    me_h = lax.axis_index("zh")
     swap = [(a * across + b, b * across + a) for a in range(across) for b in range(across)]
-    moved = lax.ppermute(tokens, ("x",) + SUB, swap)
-    gathered = lax.all_gather(moved, CH, axis=1, tiled=True)
-    blocks = gathered.reshape(tok_rows, -1, across, feat_block)
-    partial = jnp.zeros((across, tok_rows, 3 * width_local), jnp.float32)
+    cross = [
+        (a * across + b, b * across + ((a // pair + 1) % halves) * pair + a % pair)
+        for a in range(across)
+        for b in range(across)
+    ]
+    near = lax.ppermute(tokens, ("x",) + SUB, swap)
+    far = lax.ppermute(tokens, ("x",) + SUB, cross)
+    both = jnp.stack([jnp.where(me_h == 0, near, far), jnp.where(me_h == 0, far, near)])
+    gathered = lax.all_gather(both, ("y", "c"), axis=0, tiled=False)
+    blocks = gathered.reshape(-1, pair, halves, tok_rows, feat_block)
+    partial = jnp.zeros((halves, pair, tok_rows, 3 * width_local), jnp.float32)
     for k in range(down):
         source = (me_z - k) % down
-        taken = lax.dynamic_index_in_dim(blocks, source, axis=1, keepdims=False)
+        taken = lax.dynamic_index_in_dim(blocks, source, axis=0, keepdims=False)
         partial = partial + jnp.einsum(
-            "rtu,uc->trc", taken, weights[k], preferred_element_type=jnp.float32
+            "chru,uk->hcrk", taken, weights[k], preferred_element_type=jnp.float32
         )
+    partial = partial.reshape(across, tok_rows, 3 * width_local)
     projected = lax.dynamic_index_in_dim(partial, me_x, axis=0, keepdims=False)
     for k in range(1, across):
         route = [(i, (i + k) % across) for i in range(across)]

time: 328 us -> 306 us (0.933)
  local copies, waits for them, and re-layouts: 20.3 us -> 7.38 us
  waiting for transfers between devices: 226 us -> 215 us
    all_gather x1, waiting for transfers between devices: 123 us -> 32.4 us  [block(): gathered = lax.all_gather(both, ('y', 'c'), axis=0, tiled=False)]
    ppermute x9, waiting for transfers between devices: 31.8 us -> 103 us  [ring_sends(): received.append(lax.ppermute(pieces(k, position), axis, route))]
    ppermute x1 -> x2, starting transfers between devices: 1.6 us -> 10.5 us  [the longest x1 8.78 us: block(): far = lax.ppermute(tokens, ('x',) + SUB, cross)]
    reshape x1 -> x0, local copies, waits for them, and re-layouts: 7.86 us -> none  [block(): blocks = gathered.reshape(tok_rows, -1, across, feat_block)]
    ppermute x3, starting transfers between devices: 19.1 us -> 11.3 us  [block(): projected = projected + lax.ppermute(piece, 'x', route)]
    ppermute x1 -> x2, waiting for transfers between devices: 0.01 us -> 7.34 us  [the longest x1 7.34 us: block(): far = lax.ppermute(tokens, ('x',) + SUB, cross)]
    dynamic_slice x1 -> x0, local copies, waits for them, and re-layouts: 4.65 us -> none  [block(): taken = lax.dynamic_index_in_dim(blocks, source, axis=1, keepdims=False)]
  transfers between devices with their start and end apart: 15 -> 16, of which waited for: 11 -> 12; matrix products, arithmetic and copies ran while one was open for 8% -> 4% of each run, Pallas kernels for 0% -> 0%
where the time goes in v5:
time: 306 us; the launch traced here: 303 us
  waiting for transfers between devices  215 us (70%)
  starting transfers between devices  36.1 us (12%)
  matrix products  21.8 us (7%)
  between operations  13.7 us (4%)
  other arithmetic  9.47 us (3%)
  local copies, waits for them, and re-layouts  7.38 us (2%)
    ppermute x9, waiting for transfers between devices, ring_sends(): received.append(lax.ppermute(pieces(k, position), axis, route))  103 us
    ppermute x3, waiting for transfers between devices, block(): projected = projected + lax.ppermute(piece, 'x', route)  67.9 us
    all_gather x1, waiting for transfers between devices, block(): gathered = lax.all_gather(both, ('y', 'c'), axis=0, tiled=False)  32.4 us
    ppermute x9, starting transfers between devices, ring_sends(): received.append(lax.ppermute(pieces(k, position), axis, route))  11.8 us
    dot_general x4, matrix products, block(): jnp.einsum('chru,uk->hcrk', taken, weights[k], preferred_element_type=jnp...  11.8 us
    ppermute x3, starting transfers between devices, block(): projected = projected + lax.ppermute(piece, 'x', route)  11.3 us
    dot_general x1, matrix products, block(): jnp.dot(lower_mask, scaled, precision=exact_mode)  10.1 us
    ppermute x1, starting transfers between devices, block(): far = lax.ppermute(tokens, ('x',) + SUB, cross)  8.78 us
  transfers between devices with their start and end apart: 16, of which 12 were waited for; matrix products, arithmetic and copies ran while one was open for 4% of the time, Pallas kernels for 0%

profile of v5, /device:TPU:32, one launch (start us, length us, event | category | flops | bytes accessed | tf_op | source)
XLA Modules:
  0.0 303.4 jit_solution(5082514362763699422)
XLA Ops:
  6.5 1.7 collective-permute-start
  8.3 8.8 %collective-permute-start.1 = (bf16[256,512]{1,0:T(8,128)(2,1)}, bf16[256,512]{1,0:T(8,128)(2,1)S(1)}, u32[]{:S(2)}, u32[]{:S(2)}) collective-permute-start(bf16[256,512]{1,0:T(8,128)(2,1)} %param.6), channel_id=1, source_target_pairs={{0,2},{1,18},{2,34},{3,50},{16,3},{17,19},{18,35},{19,51},{32,0},{... | collective-permute-start | bytes 786440 | tf_op jit(solution)/shard_map/ppermute | solution.py:47
  17.0 7.3 %collective-permute-done.1 = bf16[256,512]{1,0:T(8,128)(2,1)S(1)} collective-permute-done((bf16[256,512]{1,0:T(8,128)(2,1)}, bf16[256,512]{1,0:T(8,128)(2,1)S(1)}, u32[]{:S(2)}, u32[]{:S(2)}) %collective-permute-start.1) | collective-permute-done | bytes 262176 | tf_op jit(solution)/shard_map/ppermute | solution.py:47
  27.6 4.4 %collective-permute-start.3 = (bf16[512,1536]{1,0:T(8,128)(2,1)}, bf16[512,1536]{1,0:T(8,128)(2,1)}, u32[]{:S(2)}, u32[]{:S(2)}) collective-permute-start(bf16[512,1536]{1,0:T(8,128)(2,1)} %copy.45), channel_id=1, source_target_pairs={{0,128},{64,192},{128,0},{192,64},{1,129},{65,193},{129,1},{193,65... | collective-permute-start | bytes 4718600 | tf_op jit(solution)/shard_map/ppermute | solution.py:24
  32.0 1.7 collective-permute-start.2
  34.0 32.4 %all-gather.3.cloned.1.call-done = bf16[16,256,512]{2,1,0:T(8,128)(2,1)} async-done(((bf16[2,256,512]{2,1,0:T(8,128)(2,1)}), bf16[16,256,512]{2,1,0:T(8,128)(2,1)}) %all-gather.3.cloned.1.call-update) | async-done | bytes 4194320 | tf_op jit(solution)/shard_map/all_gather | solution.py:49
  66.4 3.2 %fusion.20 = f32[2,2,256,1536]{3,2,1,0:T(8,128)S(1)} fusion(bf16[512,1536,1,1]{0,1,3,2:T(8,128)(2,1)S(1)} %bitcast.99, bf16[4,2,2,256,512]{4,3,2,1,0:T(8,128)(2,1)} %bitcast.101, s32[]{:T(128)S(6)} %select_n.99), kind=kOutput, calls=%fused_computation.27 | convolution fusion | flops 1610612736 | bytes 8912900 | tf_op jit(solution)/shard_map/chru,uk->hcrk/dot_general | solution.py:55
  69.6 31.2 %collective-permute-done.3 = bf16[512,1536]{1,0:T(8,128)(2,1)} collective-permute-done((bf16[512,1536]{1,0:T(8,128)(2,1)}, bf16[512,1536]{1,0:T(8,128)(2,1)}, u32[]{:S(2)}, u32[]{:S(2)}) %collective-permute-start.3) | collective-permute-done | bytes 1572896 | tf_op jit(solution)/shard_map/ppermute | solution.py:24
  100.8 3.2 %fusion.10 = f32[2,2,256,1536]{3,2,1,0:T(8,128)S(1)} fusion(bf16[512,1536]{1,0:T(8,128)(2,1)} %collective-permute-done.3, bf16[4,2,2,256,512]{4,3,2,1,0:T(8,128)(2,1)S(1)} %bitcast.103, s32[]{:T(128)S(6)} %select_n.103), kind=kOutput, calls=%fused_computation.13 | convolution fusion | flops 1610612736 | bytes 8912900 | tf_op jit(solution)/shard_map/chru,uk->hcrk/dot_general | solution.py:55
  104.0 62.0 %collective-permute-done.2 = bf16[512,1536]{1,0:T(8,128)(2,1)S(1)} collective-permute-done((bf16[512,1536]{1,0:T(8,128)(2,1)}, bf16[512,1536]{1,0:T(8,128)(2,1)S(1)}, u32[]{:S(2)}, u32[]{:S(2)}) %collective-permute-start.2) | collective-permute-done | bytes 1572896 | tf_op jit(solution)/shard_map/ppermute | solution.py:24
  166.0 1.8 fusion.12
  167.8 3.6 %add_bitcast_fusion = f32[2,2,256,1536]{3,2,0,1:T(8,128)S(1)} fusion(f32[2,2,256,1536]{3,2,1,0:T(8,128)S(1)} %fusion.10, f32[2,2,256,1536]{3,2,1,0:T(8,128)S(1)} %fusion.20, f32[2,2,256,1536]{3,2,1,0:T(8,128)S(1)} %fusion.12, bf16[512,1536]{1,0:T(8,128)(2,1)} %collective-permute-done.4, bf16[4,2,2,256,512]{4,3,2,1,0:T(8,128)(2,1)} %bitcast.102, ...), kind=kOutput, calls=%fused_computation.5 | convolution fusion | flops 1615331328 | bytes 27787268 | tf_op jit(solution)/shard_map/chru,uk->hcrk/dot_general | solution.py:55
  171.9 2.3 dynamic-slice_bitcast_fusion.2
  175.4 8.0 %collective-permute-start.7 = (f32[256,1536]{1,0:T(8,128)}, f32[256,1536]{1,0:T(8,128)S(1)}, u32[]{:S(2)}, u32[]{:S(2)}) collective-permute-start(f32[256,1536]{1,0:T(8,128)} %get-tuple-element.8), channel_id=1, source_target_pairs={{0,48},{16,0},{32,16},{48,32},{1,49},{17,1},{33,17},{49,33},{2,50}... | collective-permute-start | bytes 4718600 | tf_op jit(solution)/shard_map/ppermute | solution.py:63
  183.5 1.8 collective-permute-start.6
  186.8 64.2 %collective-permute-done.7 = f32[256,1536]{1,0:T(8,128)S(1)} collective-permute-done((f32[256,1536]{1,0:T(8,128)}, f32[256,1536]{1,0:T(8,128)S(1)}, u32[]{:S(2)}, u32[]{:S(2)}) %collective-permute-start.7) | collective-permute-done | bytes 1572896 | tf_op jit(solution)/shard_map/ppermute | solution.py:63
  251.0 3.7 %collective-permute-done.5 = f32[256,1536]{1,0:T(8,128)} collective-permute-done((f32[256,1536]{1,0:T(8,128)S(1)}, f32[256,1536]{1,0:T(8,128)}, u32[]{:S(2)}, u32[]{:S(2)}) %collective-permute-start.5) | collective-permute-done | bytes 1572896 | tf_op jit(solution)/shard_map/ppermute | solution.py:63
  254.7 2.9 fusion.16
  257.6 2.5 collective-permute-start.8
  260.7 4.5 %collective-permute-done.8 = bf16[2,3,512]{2,0,1:T(2,128)(2,1)S(1)} collective-permute-done((bf16[2,3,512]{2,0,1:T(2,128)(2,1)S(1)}, bf16[2,3,512]{2,0,1:T(2,128)(2,1)S(1)}, u32[]{:S(2)}, u32[]{:S(2)}) %collective-permute-start.8) | collective-permute-done | bytes 6176 | tf_op jit(solution)/shard_map/ppermute | solution.py:16
  271.6 1.8 collective-permute-done.10
  274.4 3.2 %collective-permute-start.13 = (f32[4,512,16]{1,2,0:T(8,128)S(1)}, f32[4,512,16]{1,2,0:T(8,128)S(1)}, u32[]{:S(2)}, u32[]{:S(2)}) collective-permute-start(f32[4,512,16]{1,2,0:T(8,128)S(1)} %get-tuple-element.13), channel_id=1, source_target_pairs={{0,128},{64,192},{128,0},{192,64},{1,129},{65,193},{129,1},{193,65... | collective-permute-start | bytes 393224 | tf_op jit(solution)/shard_map/ppermute | solution.py:24
  279.2 5.1 %collective-permute-done.14 = f32[4,512,16]{1,2,0:T(8,128)S(1)} collective-permute-done((f32[4,512,16]{1,2,0:T(8,128)S(1)}, f32[4,512,16]{1,2,0:T(8,128)S(1)}, u32[]{:S(2)}, u32[]{:S(2)}) %collective-permute-start.14) | collective-permute-done | bytes 131104 | tf_op jit(solution)/shard_map/ppermute | solution.py:24
  285.6 10.1 %multiply_reduce_fusion.1 = f32[256,512]{1,0:T(8,128)S(1)} fusion(f32[512,16]{0,1:T(8,128)S(1)} %exponential_multiply_fusion, f32[512,16]{0,1:T(8,128)S(1)} %neg.8, f32[512,16]{0,1:T(8,128)S(1)} %copy-done.6, f32[512,16,256]{2,1,0:T(8,128)S(1)} %bitcast.97), kind=kOutput, calls=%fused_computation.4 | convolution fusion | flops 6452871168 | bytes 9011200 | tf_op jit(solution)/shard_map/dot_general | solution.py:96
  (58 shorter events, 18.3 us)
Async XLA Ops:
  6.5 18.8 %copy-start.1 = (bf16[512,3,512]{2,0,1:T(8,128)(2,1)S(1)}, bf16[512,3,512]{2,0,1:T(8,128)(2,1)}, u32[]{:S(2)}) copy-start(bf16[512,3,512]{2,0,1:T(8,128)(2,1)} %param.7) | copy-start | bytes 4718596
  6.5 59.9 %all-gather.3.cloned.1.call-start = ((), (), s32[]{:S(2)}) async-start(), calls=%async_computation | async-start | bytes 4718592 | tf_op jit(solution)/shard_map/all_gather | solution.py:49
  6.5 10.5 %collective-permute-start = (bf16[256,512]{1,0:T(8,128)(2,1)}, bf16[256,512]{1,0:T(8,128)(2,1)S(1)}, u32[]{:S(2)}, u32[]{:S(2)}) collective-permute-start(bf16[256,512]{1,0:T(8,128)(2,1)} %param.6), channel_id=1, source_target_pairs={{0,0},{1,16},{2,32},{3,48},{16,1},{17,17},{18,33},{19,49},{32,2},{... | collective-permute-start | bytes 786440 | tf_op jit(solution)/shard_map/ppermute | solution.py:46
  8.3 16.1 %collective-permute-start.1 = (bf16[256,512]{1,0:T(8,128)(2,1)}, bf16[256,512]{1,0:T(8,128)(2,1)S(1)}, u32[]{:S(2)}, u32[]{:S(2)}) collective-permute-start(bf16[256,512]{1,0:T(8,128)(2,1)} %param.6), channel_id=1, source_target_pairs={{0,2},{1,18},{2,34},{3,50},{16,3},{17,19},{18,35},{19,51},{32,0},{... | collective-permute-start | bytes 786440 | tf_op jit(solution)/shard_map/ppermute | solution.py:47
  27.6 73.1 %collective-permute-start.3 = (bf16[512,1536]{1,0:T(8,128)(2,1)}, bf16[512,1536]{1,0:T(8,128)(2,1)}, u32[]{:S(2)}, u32[]{:S(2)}) collective-permute-start(bf16[512,1536]{1,0:T(8,128)(2,1)} %copy.45), channel_id=1, source_target_pairs={{0,128},{64,192},{128,0},{192,64},{1,129},{65,193},{129,1},{193,65... | collective-permute-start | bytes 4718600 | tf_op jit(solution)/shard_map/ppermute | solution.py:24
  32.0 134.0 %collective-permute-start.2 = (bf16[512,1536]{1,0:T(8,128)(2,1)}, bf16[512,1536]{1,0:T(8,128)(2,1)S(1)}, u32[]{:S(2)}, u32[]{:S(2)}) collective-permute-start(bf16[512,1536]{1,0:T(8,128)(2,1)} %copy.45), channel_id=1, source_target_pairs={{0,64},{64,128},{128,192},{192,0},{1,65},{65,129},{129,193},{193,1... | collective-permute-start | bytes 4718600 | tf_op jit(solution)/shard_map/ppermute | solution.py:24
  33.7 134.1 %collective-permute-start.4 = (bf16[512,1536]{1,0:T(8,128)(2,1)}, bf16[512,1536]{1,0:T(8,128)(2,1)}, u32[]{:S(2)}, u32[]{:S(2)}) collective-permute-start(bf16[512,1536]{1,0:T(8,128)(2,1)} %copy.45), channel_id=1, source_target_pairs={{0,192},{64,0},{128,64},{192,128},{1,193},{65,1},{129,65},{193,129... | collective-permute-start | bytes 4718600 | tf_op jit(solution)/shard_map/ppermute | solution.py:24
  66.4 34.4 %copy-start.3 = (bf16[16,256,512]{2,1,0:T(8,128)(2,1)S(1)}, bf16[16,256,512]{2,1,0:T(8,128)(2,1)}, u32[]{:S(2)}) copy-start(bf16[16,256,512]{2,1,0:T(8,128)(2,1)} %all-gather.3.cloned.1.call-done) | copy-start | bytes 12582916
  171.9 3.6 %copy-start = (f32[2,2,256,1536]{3,2,1,0:T(8,128)}, f32[2,2,256,1536]{3,2,1,0:T(8,128)S(1)}, u32[]{:S(2)}) copy-start(f32[2,2,256,1536]{3,2,1,0:T(8,128)S(1)} %copy.48) | copy-start | bytes 18874372
  171.9 14.9 %copy-start.4 = (bf16[3,3,512]{2,1,0:T(4,128)(2,1)S(1)}, bf16[3,3,512]{2,1,0:T(4,128)(2,1)}, u32[]{:S(2)}) copy-start(bf16[3,3,512]{2,1,0:T(4,128)(2,1)} %param.8) | copy-start | bytes 27652
  175.4 75.5 %collective-permute-start.7 = (f32[256,1536]{1,0:T(8,128)}, f32[256,1536]{1,0:T(8,128)S(1)}, u32[]{:S(2)}, u32[]{:S(2)}) collective-permute-start(f32[256,1536]{1,0:T(8,128)} %get-tuple-element.8), channel_id=1, source_target_pairs={{0,48},{16,0},{32,16},{48,32},{1,49},{17,1},{33,17},{49,33},{2,50}... | collective-permute-start | bytes 4718600 | tf_op jit(solution)/shard_map/ppermute | solution.py:63
  183.5 67.5 %collective-permute-start.6 = (f32[256,1536]{1,0:T(8,128)}, f32[256,1536]{1,0:T(8,128)}, u32[]{:S(2)}, u32[]{:S(2)}) collective-permute-start(f32[256,1536]{1,0:T(8,128)} %get-tuple-element.9), channel_id=1, source_target_pairs={{0,32},{16,48},{32,0},{48,16},{1,33},{17,49},{33,1},{49,17},{2,34}... | collective-permute-start | bytes 4718600 | tf_op jit(solution)/shard_map/ppermute | solution.py:63
  185.3 69.4 %collective-permute-start.5 = (f32[256,1536]{1,0:T(8,128)S(1)}, f32[256,1536]{1,0:T(8,128)}, u32[]{:S(2)}, u32[]{:S(2)}) collective-permute-start(f32[256,1536]{1,0:T(8,128)S(1)} %get-tuple-element.7), channel_id=1, source_target_pairs={{0,16},{16,32},{32,48},{48,0},{1,17},{17,33},{33,49},{49,1},{2,18}... | collective-permute-start | bytes 4718600 | tf_op jit(solution)/shard_map/ppermute | solution.py:63
  186.7 73.3 %copy-start.2 = (f32[512,16]{0,1:T(8,128)S(1)}, f32[512,16]{0,1:T(8,128)}, u32[]{:S(2)}) copy-start(f32[512,16]{0,1:T(8,128)} %param.9) | copy-start | bytes 98308
  257.6 7.6 %collective-permute-start.8 = (bf16[2,3,512]{2,0,1:T(2,128)(2,1)S(1)}, bf16[2,3,512]{2,0,1:T(2,128)(2,1)S(1)}, u32[]{:S(2)}, u32[]{:S(2)}) collective-permute-start(bf16[2,3,512]{2,0,1:T(2,128)(2,1)S(1)} %bitcast.111), channel_id=1, source_target_pairs={{0,16},{16,32},{32,48},{48,64},{64,80},{80,96},{96,112},{112,128},... | collective-permute-start | bytes 18440 | tf_op jit(solution)/shard_map/ppermute | solution.py:16
  267.6 4.0 %collective-permute-start.11 = (f32[512,16]{0,1:T(8,128)S(1)}, f32[512,16]{0,1:T(8,128)S(1)}, u32[]{:S(2)}, u32[]{:S(2)}) collective-permute-start(f32[512,16]{0,1:T(8,128)S(1)} %multiply_reduce_fusion), channel_id=1, source_target_pairs={{0,48},{16,0},{32,16},{48,32},{1,49},{17,1},{33,17},{49,33},{2,50}... | collective-permute-start | bytes 98312 | tf_op jit(solution)/shard_map/ppermute | solution.py:24
  267.7 5.7 %collective-permute-start.10 = (f32[512,16]{0,1:T(8,128)S(1)}, f32[512,16]{0,1:T(8,128)S(1)}, u32[]{:S(2)}, u32[]{:S(2)}) collective-permute-start(f32[512,16]{0,1:T(8,128)S(1)} %multiply_reduce_fusion), channel_id=1, source_target_pairs={{0,32},{16,48},{32,0},{48,16},{1,33},{17,49},{33,1},{49,17},{2,34}... | collective-permute-start | bytes 98312 | tf_op jit(solution)/shard_map/ppermute | solution.py:24
  268.2 6.1 %collective-permute-start.9 = (f32[512,16]{0,1:T(8,128)S(1)}, f32[512,16]{0,1:T(8,128)S(1)}, u32[]{:S(2)}, u32[]{:S(2)}) collective-permute-start(f32[512,16]{0,1:T(8,128)S(1)} %multiply_reduce_fusion), channel_id=1, source_target_pairs={{0,16},{16,32},{32,48},{48,0},{1,17},{17,33},{33,49},{49,1},{2,18}... | collective-permute-start | bytes 98312 | tf_op jit(solution)/shard_map/ppermute | solution.py:24
  274.3 10.0 %collective-permute-start.14 = (f32[4,512,16]{1,2,0:T(8,128)S(1)}, f32[4,512,16]{1,2,0:T(8,128)S(1)}, u32[]{:S(2)}, u32[]{:S(2)}) collective-permute-start(f32[4,512,16]{1,2,0:T(8,128)S(1)} %get-tuple-element.13), channel_id=1, source_target_pairs={{0,192},{64,0},{128,64},{192,128},{1,193},{65,1},{129,65},{193,129... | collective-permute-start | bytes 393224 | tf_op jit(solution)/shard_map/ppermute | solution.py:24
  274.4 9.9 %collective-permute-start.13 = (f32[4,512,16]{1,2,0:T(8,128)S(1)}, f32[4,512,16]{1,2,0:T(8,128)S(1)}, u32[]{:S(2)}, u32[]{:S(2)}) collective-permute-start(f32[4,512,16]{1,2,0:T(8,128)S(1)} %get-tuple-element.13), channel_id=1, source_target_pairs={{0,128},{64,192},{128,0},{192,64},{1,129},{65,193},{129,1},{193,65... | collective-permute-start | bytes 393224 | tf_op jit(solution)/shard_map/ppermute | solution.py:24
  277.6 6.9 %collective-permute-start.12 = (f32[4,512,16]{1,2,0:T(8,128)S(1)}, f32[4,512,16]{1,2,0:T(8,128)}, u32[]{:S(2)}, u32[]{:S(2)}) collective-permute-start(f32[4,512,16]{1,2,0:T(8,128)S(1)} %get-tuple-element.13), channel_id=1, source_target_pairs={{0,64},{64,128},{128,192},{192,0},{1,65},{65,129},{129,193},{193,1... | collective-permute-start | bytes 393224 | tf_op jit(solution)/shard_map/ppermute | solution.py:24
  277.9 7.7 %copy-start.6 = (f32[512,16]{0,1:T(8,128)S(1)}, f32[512,16]{0,1:T(8,128)}, u32[]{:S(2)}) copy-start(f32[512,16]{0,1:T(8,128)} %param.10) | copy-start | bytes 98308
  285.6 10.1 %copy-start.5 = (f32[512]{0:T(512)S(1)}, f32[512]{0:T(512)}, u32[]{:S(2)}) copy-start(f32[512]{0:T(512)} %param.11) | copy-start | bytes 6148
Sparse Core Ops, SparseCore 0:
  25.4 40.9 all-gather.2

commit v6 on v5

--- a/solution.py
+++ b/solution.py
@@ -25,6 +25,20 @@
     return received
 
 
+def line_gather(piece, axis, size):
+    below, above = [], []
+    near_b = lax.ppermute(piece, axis, [(i, i + 1) for i in range(size - 1)])
+    near_a = lax.ppermute(piece, axis, [(i + 1, i) for i in range(size - 1)])
+    below.append(near_b)
+    above.append(near_a)
+    for d in range(2, size):
+        near_b = lax.ppermute(near_b, axis, [(i, i + 1) for i in range(d - 1, size - 1)])
+        near_a = lax.ppermute(near_a, axis, [(i + 1, i) for i in range(0, size - d)])
+        below.append(near_b)
+        above.append(near_a)
+    return below, above
+
+
 def block(tokens, in_weight, short_filter, decay_rate, residue, skip_gain):
     tok_rows = tokens.shape[0]
     width_local = in_weight.shape[2]
@@ -33,7 +47,7 @@
     across, down = lax.axis_size("x"), lax.axis_size("zl")
     me_x, me_z = lax.axis_index("x"), lax.axis_index("zl")
     flat_own = in_weight.reshape(feat_block, 3 * width_local)
-    weights = [flat_own] + ring_sends(lambda k, p: flat_own, "zl", down)
+    below, above = line_gather(flat_own, "zl", down)
     halves = lax.axis_size("zh")
     pair = lax.axis_size("c")
     me_h = lax.axis_index("zh")
@@ -48,13 +62,20 @@
     both = jnp.stack([jnp.where(me_h == 0, near, far), jnp.where(me_h == 0, far, near)])
     gathered = lax.all_gather(both, ("y", "c"), axis=0, tiled=False)
     blocks = gathered.reshape(-1, pair, halves, tok_rows, feat_block)
-    partial = jnp.zeros((halves, pair, tok_rows, 3 * width_local), jnp.float32)
-    for k in range(down):
-        source = (me_z - k) % down
+    def contribution(source, weight):
         taken = lax.dynamic_index_in_dim(blocks, source, axis=0, keepdims=False)
-        partial = partial + jnp.einsum(
-            "chru,uk->hcrk", taken, weights[k], preferred_element_type=jnp.float32
-        )
+        return jnp.einsum("chru,uk->hcrk", taken, weight, preferred_element_type=jnp.float32)
+
+    partial = contribution(me_z, flat_own)
+    for d in range(1, down):
+        low, high = jnp.maximum(me_z - d, 0), jnp.minimum(me_z + d, down - 1)
+        if 2 * d <= down - 1:
+            partial = partial + contribution(low, below[d - 1])
+            partial = partial + contribution(high, above[d - 1])
+        else:
+            use_low = me_z - d >= 0
+            weight = jnp.where(use_low, below[d - 1], above[d - 1])
+            partial = partial + contribution(jnp.where(use_low, low, high), weight)
     partial = partial.reshape(across, tok_rows, 3 * width_local)
     projected = lax.dynamic_index_in_dim(partial, me_x, axis=0, keepdims=False)
     for k in range(1, across):

time: 306 us -> 286 us (0.935)
  waiting for transfers between devices: 215 us -> 160 us
  matrix products: 21.8 us -> 41.3 us
  starting transfers between devices: 36.1 us -> 51.4 us
    ppermute x9 -> x6, waiting for transfers between devices: 103 us -> 8.29 us  [ring_sends(): received.append(lax.ppermute(pieces(k, position), axis, route))]
    ppermute x0 -> x6, waiting for transfers between devices: none -> 76.7 us  [the longest x1 31.7 us: line_gather(): near_b = lax.ppermute(piece, axis, [(i, i + 1) for i in range(size - 1)])]
    all_gather x1, waiting for transfers between devices: 32.4 us -> 0.01 us  [block(): gathered = lax.all_gather(both, ('y', 'c'), axis=0, tiled=False)]
    ppermute x0 -> x6, starting transfers between devices: none -> 20.7 us  [the longest x1 6.81 us: line_gather(): near_b = lax.ppermute(piece, axis, [(i, i + 1) for i in range(size - 1)])]
    dot_general x4 -> x5, matrix products: 11.8 us -> 31.2 us  [contribution(): jnp.einsum('chru,uk->hcrk', taken, weight, preferred_element_type=jnp.flo...]
    ppermute x9 -> x6, starting transfers between devices: 11.8 us -> 6.22 us  [ring_sends(): received.append(lax.ppermute(pieces(k, position), axis, route))]
    ppermute x3, waiting for transfers between devices: 67.9 us -> 64.7 us  [block(): projected = projected + lax.ppermute(piece, 'x', route)]
  transfers between devices with their start and end apart: 16 -> 19, of which waited for: 12 -> 14; matrix products, arithmetic and copies ran while one was open for 4% -> 9% of each run, Pallas kernels for 0% -> 0%
where the time goes in v6:
time: 286 us; the launch traced here: 283 us
  waiting for transfers between devices  160 us (56%)
  starting transfers between devices  51.4 us (18%)
  matrix products  41.3 us (14%)
  between operations  13.8 us (5%)
  other arithmetic  9.54 us (3%)
  local copies, waits for them, and re-layouts  6.56 us (2%)
    ppermute x3, waiting for transfers between devices, block(): projected = projected + lax.ppermute(piece, 'x', route)  64.7 us
    ppermute x1, waiting for transfers between devices, line_gather(): near_b = lax.ppermute(piece, axis, [(i, i + 1) for i in range(size - 1)])  31.7 us
    dot_general x5, matrix products, contribution(): jnp.einsum('chru,uk->hcrk', taken, weight, preferred_element_type=jnp.flo...  31.2 us
    ppermute x2, waiting for transfers between devices, line_gather(): lax.ppermute(near_b, axis, [(i, i + 1) for i in range(d - 1, size - 1)])  30.1 us
    ppermute x2, waiting for transfers between devices, line_gather(): lax.ppermute(near_a, axis, [(i + 1, i) for i in range(0, size - d)])  14.8 us
    ppermute x3, starting transfers between devices, block(): projected = projected + lax.ppermute(piece, 'x', route)  10.3 us
    dot_general x1, matrix products, block(): jnp.dot(lower_mask, scaled, precision=exact_mode)  10.1 us
    ppermute x1, starting transfers between devices, block(): far = lax.ppermute(tokens, ('x',) + SUB, cross)  8.78 us
  transfers between devices with their start and end apart: 19, of which 14 were waited for; matrix products, arithmetic and copies ran while one was open for 9% of the time, Pallas kernels for 0%

profile of v6, /device:TPU:32, one launch (start us, length us, event | category | flops | bytes accessed | tf_op | source)
XLA Modules:
  0.0 282.9 jit_solution(13951600284071007050)
XLA Ops:
  8.3 8.8 %collective-permute-start.1 = (bf16[256,512]{1,0:T(8,128)(2,1)}, bf16[256,512]{1,0:T(8,128)(2,1)S(1)}, u32[]{:S(2)}, u32[]{:S(2)}) collective-permute-start(bf16[256,512]{1,0:T(8,128)(2,1)} %param.6), channel_id=1, source_target_pairs={{0,2},{1,18},{2,34},{3,50},{16,3},{17,19},{18,35},{19,51},{32,0},{... | collective-permute-start | bytes 786440 | tf_op jit(solution)/shard_map/ppermute | solution.py:61
  17.0 7.3 %collective-permute-done.1 = bf16[256,512]{1,0:T(8,128)(2,1)S(1)} collective-permute-done((bf16[256,512]{1,0:T(8,128)(2,1)}, bf16[256,512]{1,0:T(8,128)(2,1)S(1)}, u32[]{:S(2)}, u32[]{:S(2)}) %collective-permute-start.1) | collective-permute-done | bytes 262176 | tf_op jit(solution)/shard_map/ppermute | solution.py:61
  26.8 6.8 %collective-permute-start.2 = (bf16[512,1536]{1,0:T(8,128)(2,1)S(1)}, bf16[512,1536]{1,0:T(8,128)(2,1)}, u32[]{:S(2)}, u32[]{:S(2)}) collective-permute-start(bf16[512,1536]{1,0:T(8,128)(2,1)S(1)} %copy.58), channel_id=1, source_target_pairs={{0,64},{64,128},{128,192},{1,65},{65,129},{129,193},{2,66},{66,130... | collective-permute-start | bytes 4718600 | tf_op jit(solution)/shard_map/ppermute | solution.py:30
  35.7 31.7 %collective-permute-done.2 = bf16[512,1536]{1,0:T(8,128)(2,1)} collective-permute-done((bf16[512,1536]{1,0:T(8,128)(2,1)S(1)}, bf16[512,1536]{1,0:T(8,128)(2,1)}, u32[]{:S(2)}, u32[]{:S(2)}) %collective-permute-start.2) | collective-permute-done | bytes 1572896 | tf_op jit(solution)/shard_map/ppermute | solution.py:30
  67.4 5.6 %collective-permute-start.4 = (bf16[512,1536]{1,0:T(8,128)(2,1)}, bf16[512,1536]{1,0:T(8,128)(2,1)}, u32[]{:S(2)}, u32[]{:S(2)}) collective-permute-start(bf16[512,1536]{1,0:T(8,128)(2,1)} %collective-permute-done.2), channel_id=1, source_target_pairs={{64,128},{128,192},{65,129},{129,193},{66,130},{130,194},{67,131},... | collective-permute-start | bytes 4718600 | tf_op jit(solution)/shard_map/ppermute | solution.py:35
  75.0 30.1 %collective-permute-done.4 = bf16[512,1536]{1,0:T(8,128)(2,1)} collective-permute-done((bf16[512,1536]{1,0:T(8,128)(2,1)}, bf16[512,1536]{1,0:T(8,128)(2,1)}, u32[]{:S(2)}, u32[]{:S(2)}) %collective-permute-start.4) | collective-permute-done | bytes 1572896 | tf_op jit(solution)/shard_map/ppermute | solution.py:35
  105.9 4.5 %collective-permute-done.5 = bf16[512,1536]{1,0:T(8,128)(2,1)} collective-permute-done((bf16[512,1536]{1,0:T(8,128)(2,1)}, bf16[512,1536]{1,0:T(8,128)(2,1)}, u32[]{:S(2)}, u32[]{:S(2)}) %collective-permute-start.5) | collective-permute-done | bytes 1572896 | tf_op jit(solution)/shard_map/ppermute | solution.py:36
  110.4 3.5 %collective-permute-start.7 = (bf16[512,1536]{1,0:T(8,128)(2,1)}, bf16[512,1536]{1,0:T(8,128)(2,1)}, u32[]{:S(2)}, u32[]{:S(2)}) collective-permute-start(bf16[512,1536]{1,0:T(8,128)(2,1)} %collective-permute-done.5), channel_id=1, source_target_pairs={{64,0},{65,1},{66,2},{67,3},{68,4},{69,5},{70,6},{71,7},{72,8},{73... | collective-permute-start | bytes 4718600 | tf_op jit(solution)/shard_map/ppermute | solution.py:36
  113.9 5.8 %fusion.24 = f32[2,2,256,1536]{3,2,1,0:T(8,128)} fusion(bf16[512,1536,1,1]{0,1,3,2:T(8,128)(2,1)S(1)} %bitcast.107, bf16[4,2,2,256,512]{4,3,2,1,0:T(8,128)(2,1)} %bitcast.109, s32[]{:T(128)S(6)} %select_n.103), kind=kOutput, calls=%fused_computation.34 | convolution fusion | flops 1610612736 | bytes 8912900 | tf_op jit(solution)/shard_map/chru,uk->hcrk/dot_general | solution.py:67
  119.7 5.9 %fusion.6 = f32[2,2,256,1536]{3,2,1,0:T(8,128)} fusion(bf16[512,1536]{1,0:T(8,128)(2,1)} %collective-permute-done.3, bf16[4,2,2,256,512]{4,3,2,1,0:T(8,128)(2,1)S(1)} %bitcast.111, s32[]{:T(128)S(6)} %select_n.104), kind=kOutput, calls=%fused_computation.12 | convolution fusion | flops 1610612736 | bytes 8912900 | tf_op jit(solution)/shard_map/chru,uk->hcrk/dot_general | solution.py:67
  125.5 5.8 %fusion.8 = f32[2,2,256,1536]{3,2,1,0:T(8,128)} fusion(bf16[512,1536]{1,0:T(8,128)(2,1)} %collective-permute-done.2, bf16[4,2,2,256,512]{4,3,2,1,0:T(8,128)(2,1)S(1)} %bitcast.112, s32[]{:T(128)S(6)} %max.16), kind=kOutput, calls=%fused_computation.14 | convolution fusion | flops 1610612736 | bytes 8912900 | tf_op jit(solution)/shard_map/chru,uk->hcrk/dot_general | solution.py:67
  131.3 3.3 %fusion.14 = f32[1536,2,2,256]{0,3,2,1:T(8,128)S(1)} fusion(bf16[512,1536]{1,0:T(8,128)(2,1)} %collective-permute-done.4, bf16[512,1536]{1,0:T(8,128)(2,1)} %collective-permute-done.5, pred[]{:T(512)S(6)} %ge.26, bf16[4,2,2,256,512]{4,3,2,1,0:T(8,128)(2,1)S(1)} %bitcast.113, s32[]{:T(128)S(6)} %select_n.108), kind=kOutput, calls=%fused_computation.21 | convolution fusion | flops 1611399168 | bytes 10485765 | tf_op jit(solution)/shard_map/chru,uk->hcrk/dot_general | solution.py:67
  134.7 10.3 %collective-permute-done.7 = bf16[512,1536]{1,0:T(8,128)(2,1)} collective-permute-done((bf16[512,1536]{1,0:T(8,128)(2,1)}, bf16[512,1536]{1,0:T(8,128)(2,1)}, u32[]{:S(2)}, u32[]{:S(2)}) %collective-permute-start.7) | collective-permute-done | bytes 1572896 | tf_op jit(solution)/shard_map/ppermute | solution.py:36
  145.0 10.4 %bitcast_add_fusion = f32[2,2,256,1536]{3,2,0,1:T(8,128)S(1)} fusion(f32[1536,2,2,256]{0,3,2,1:T(8,128)S(1)} %fusion.14, f32[2,2,256,1536]{3,2,1,0:T(8,128)} %fusion.6, f32[2,2,256,1536]{3,2,1,0:T(8,128)} %fusion.24, f32[2,2,256,1536]{3,2,1,0:T(8,128)} %fusion.8, bf16[512,1536]{1,0:T(8,128)(2,1)S(1)} %collective-permute-done.6, ...), kind=kOutput, calls=%fused_computation.5 | convolution fusion | flops 1617690624 | bytes 35651588 | tf_op jit(solution)/shard_map/chru,uk->hcrk/dot_general | solution.py:67
  156.0 2.3 dynamic-slice_bitcast_fusion.2
  159.6 6.6 %collective-permute-start.10 = (f32[256,1536]{1,0:T(8,128)}, f32[256,1536]{1,0:T(8,128)S(1)}, u32[]{:S(2)}, u32[]{:S(2)}) collective-permute-start(f32[256,1536]{1,0:T(8,128)} %get-tuple-element.8), channel_id=1, source_target_pairs={{0,48},{16,0},{32,16},{48,32},{1,49},{17,1},{33,17},{49,33},{2,50}... | collective-permute-start | bytes 4718600 | tf_op jit(solution)/shard_map/ppermute | solution.py:84
  166.1 2.4 collective-permute-start.9
  169.9 61.0 %collective-permute-done.10 = f32[256,1536]{1,0:T(8,128)S(1)} collective-permute-done((f32[256,1536]{1,0:T(8,128)}, f32[256,1536]{1,0:T(8,128)S(1)}, u32[]{:S(2)}, u32[]{:S(2)}) %collective-permute-start.10) | collective-permute-done | bytes 1572896 | tf_op jit(solution)/shard_map/ppermute | solution.py:84
  230.9 3.7 %collective-permute-done.8 = f32[256,1536]{1,0:T(8,128)} collective-permute-done((f32[256,1536]{1,0:T(8,128)S(1)}, f32[256,1536]{1,0:T(8,128)}, u32[]{:S(2)}, u32[]{:S(2)}) %collective-permute-start.8) | collective-permute-done | bytes 1572896 | tf_op jit(solution)/shard_map/ppermute | solution.py:84
  234.6 2.9 %fusion.12 = bf16[256,1536]{1,0:T(8,128)(2,1)S(1)} fusion(f32[256,1536]{1,0:T(8,128)S(1)} %collective-permute-done.10, f32[256,1536]{1,0:T(8,128)} %collective-permute-done.9, f32[256,1536]{1,0:T(8,128)} %collective-permute-done.8, f32[4,256,1536]{2,1,0:T(8,128)} %bitcast.104, s32[]{:T(128)S(6)} %select_n.113), kind=kLoop, calls=%fused_computation.19 | loop fusion | flops 1572864 | bytes 7077892 | tf_op jit(solution)/shard_map/convert_element_type | solution.py:85
  237.5 3.7 %collective-permute-start.11 = (bf16[2,3,512]{2,0,1:T(2,128)(2,1)S(1)}, bf16[2,3,512]{2,0,1:T(2,128)(2,1)S(1)}, u32[]{:S(2)}, u32[]{:S(2)}) collective-permute-start(bf16[2,3,512]{2,0,1:T(2,128)(2,1)S(1)} %bitcast.119), channel_id=1, source_target_pairs={{0,16},{16,32},{32,48},{48,64},{64,80},{80,96},{96,112},{112,128},... | collective-permute-start | bytes 18440 | tf_op jit(solution)/shard_map/ppermute | solution.py:16
  241.8 3.3 %collective-permute-done.11 = bf16[2,3,512]{2,0,1:T(2,128)(2,1)S(1)} collective-permute-done((bf16[2,3,512]{2,0,1:T(2,128)(2,1)S(1)}, bf16[2,3,512]{2,0,1:T(2,128)(2,1)S(1)}, u32[]{:S(2)}, u32[]{:S(2)}) %collective-permute-start.11) | collective-permute-done | bytes 6176 | tf_op jit(solution)/shard_map/ppermute | solution.py:16
  254.5 2.6 collective-permute-start.17
  265.1 10.1 %multiply_reduce_fusion.1 = f32[256,512]{1,0:T(8,128)S(1)} fusion(f32[512,16]{0,1:T(8,128)S(1)} %exponential_multiply_fusion, f32[512,16]{0,1:T(8,128)S(1)} %neg.8, f32[512,16]{0,1:T(8,128)S(1)} %copy-done.6, f32[512,16,256]{2,1,0:T(8,128)S(1)} %bitcast.105), kind=kOutput, calls=%fused_computation.4 | convolution fusion | flops 6452871168 | bytes 9011200 | tf_op jit(solution)/shard_map/dot_general | solution.py:117
  (65 shorter events, 30.9 us)
Async XLA Ops:
  6.5 18.8 %copy-start.1 = (bf16[512,3,512]{2,0,1:T(8,128)(2,1)S(1)}, bf16[512,3,512]{2,0,1:T(8,128)(2,1)}, u32[]{:S(2)}) copy-start(bf16[512,3,512]{2,0,1:T(8,128)(2,1)} %param.7) | copy-start | bytes 4718596
  6.5 107.3 %all-gather.3.cloned.1.call-start = ((), (), s32[]{:S(2)}) async-start(), calls=%async_computation | async-start | bytes 4718592 | tf_op jit(solution)/shard_map/all_gather | solution.py:63
  6.5 10.5 %collective-permute-start = (bf16[256,512]{1,0:T(8,128)(2,1)}, bf16[256,512]{1,0:T(8,128)(2,1)S(1)}, u32[]{:S(2)}, u32[]{:S(2)}) collective-permute-start(bf16[256,512]{1,0:T(8,128)(2,1)} %param.6), channel_id=1, source_target_pairs={{0,0},{1,16},{2,32},{3,48},{16,1},{17,17},{18,33},{19,49},{32,2},{... | collective-permute-start | bytes 786440 | tf_op jit(solution)/shard_map/ppermute | solution.py:60
  8.3 16.1 %collective-permute-start.1 = (bf16[256,512]{1,0:T(8,128)(2,1)}, bf16[256,512]{1,0:T(8,128)(2,1)S(1)}, u32[]{:S(2)}, u32[]{:S(2)}) collective-permute-start(bf16[256,512]{1,0:T(8,128)(2,1)} %param.6), channel_id=1, source_target_pairs={{0,2},{1,18},{2,34},{3,50},{16,3},{17,19},{18,35},{19,51},{32,0},{... | collective-permute-start | bytes 786440 | tf_op jit(solution)/shard_map/ppermute | solution.py:61
  26.8 40.6 %collective-permute-start.2 = (bf16[512,1536]{1,0:T(8,128)(2,1)S(1)}, bf16[512,1536]{1,0:T(8,128)(2,1)}, u32[]{:S(2)}, u32[]{:S(2)}) collective-permute-start(bf16[512,1536]{1,0:T(8,128)(2,1)S(1)} %copy.58), channel_id=1, source_target_pairs={{0,64},{64,128},{128,192},{1,65},{65,129},{129,193},{2,66},{66,130... | collective-permute-start | bytes 4718600 | tf_op jit(solution)/shard_map/ppermute | solution.py:30
  33.6 39.4 %collective-permute-start.3 = (bf16[512,1536]{1,0:T(8,128)(2,1)S(1)}, bf16[512,1536]{1,0:T(8,128)(2,1)}, u32[]{:S(2)}, u32[]{:S(2)}) collective-permute-start(bf16[512,1536]{1,0:T(8,128)(2,1)S(1)} %copy.58), channel_id=1, source_target_pairs={{64,0},{128,64},{192,128},{65,1},{129,65},{193,129},{66,2},{130,66... | collective-permute-start | bytes 4718600 | tf_op jit(solution)/shard_map/ppermute | solution.py:31
  67.4 37.8 %collective-permute-start.4 = (bf16[512,1536]{1,0:T(8,128)(2,1)}, bf16[512,1536]{1,0:T(8,128)(2,1)}, u32[]{:S(2)}, u32[]{:S(2)}) collective-permute-start(bf16[512,1536]{1,0:T(8,128)(2,1)} %collective-permute-done.2), channel_id=1, source_target_pairs={{64,128},{128,192},{65,129},{129,193},{66,130},{130,194},{67,131},... | collective-permute-start | bytes 4718600 | tf_op jit(solution)/shard_map/ppermute | solution.py:35
  73.0 37.4 %collective-permute-start.5 = (bf16[512,1536]{1,0:T(8,128)(2,1)}, bf16[512,1536]{1,0:T(8,128)(2,1)}, u32[]{:S(2)}, u32[]{:S(2)}) collective-permute-start(bf16[512,1536]{1,0:T(8,128)(2,1)} %collective-permute-done.3), channel_id=1, source_target_pairs={{64,0},{128,64},{65,1},{129,65},{66,2},{130,66},{67,3},{131,67},{6... | collective-permute-start | bytes 4718600 | tf_op jit(solution)/shard_map/ppermute | solution.py:36
  105.1 29.5 %collective-permute-start.6 = (bf16[512,1536]{1,0:T(8,128)(2,1)}, bf16[512,1536]{1,0:T(8,128)(2,1)S(1)}, u32[]{:S(2)}, u32[]{:S(2)}) collective-permute-start(bf16[512,1536]{1,0:T(8,128)(2,1)} %collective-permute-done.4), channel_id=1, source_target_pairs={{128,192},{129,193},{130,194},{131,195},{132,196},{133,197},{134,1... | collective-permute-start | bytes 4718600 | tf_op jit(solution)/shard_map/ppermute | solution.py:35
  110.4 34.6 %collective-permute-start.7 = (bf16[512,1536]{1,0:T(8,128)(2,1)}, bf16[512,1536]{1,0:T(8,128)(2,1)}, u32[]{:S(2)}, u32[]{:S(2)}) collective-permute-start(bf16[512,1536]{1,0:T(8,128)(2,1)} %collective-permute-done.5), channel_id=1, source_target_pairs={{64,0},{65,1},{66,2},{67,3},{68,4},{69,5},{70,6},{71,7},{72,8},{73... | collective-permute-start | bytes 4718600 | tf_op jit(solution)/shard_map/ppermute | solution.py:36
  156.0 13.9 %copy-start.4 = (bf16[3,3,512]{2,1,0:T(4,128)(2,1)S(1)}, bf16[3,3,512]{2,1,0:T(4,128)(2,1)}, u32[]{:S(2)}) copy-start(bf16[3,3,512]{2,1,0:T(4,128)(2,1)} %param.8) | copy-start | bytes 27652
  159.6 71.4 %collective-permute-start.10 = (f32[256,1536]{1,0:T(8,128)}, f32[256,1536]{1,0:T(8,128)S(1)}, u32[]{:S(2)}, u32[]{:S(2)}) collective-permute-start(f32[256,1536]{1,0:T(8,128)} %get-tuple-element.8), channel_id=1, source_target_pairs={{0,48},{16,0},{32,16},{48,32},{1,49},{17,1},{33,17},{49,33},{2,50}... | collective-permute-start | bytes 4718600 | tf_op jit(solution)/shard_map/ppermute | solution.py:84
  166.1 64.8 %collective-permute-start.9 = (f32[256,1536]{1,0:T(8,128)}, f32[256,1536]{1,0:T(8,128)}, u32[]{:S(2)}, u32[]{:S(2)}) collective-permute-start(f32[256,1536]{1,0:T(8,128)} %get-tuple-element.9), channel_id=1, source_target_pairs={{0,32},{16,48},{32,0},{48,16},{1,33},{17,49},{33,1},{49,17},{2,34}... | collective-permute-start | bytes 4718600 | tf_op jit(solution)/shard_map/ppermute | solution.py:84
  168.5 66.2 %collective-permute-start.8 = (f32[256,1536]{1,0:T(8,128)S(1)}, f32[256,1536]{1,0:T(8,128)}, u32[]{:S(2)}, u32[]{:S(2)}) collective-permute-start(f32[256,1536]{1,0:T(8,128)S(1)} %get-tuple-element.7), channel_id=1, source_target_pairs={{0,16},{16,32},{32,48},{48,0},{1,17},{17,33},{33,49},{49,1},{2,18}... | collective-permute-start | bytes 4718600 | tf_op jit(solution)/shard_map/ppermute | solution.py:84
  169.9 71.3 %copy-start.3 = (f32[512,16]{0,1:T(8,128)S(1)}, f32[512,16]{0,1:T(8,128)}, u32[]{:S(2)}) copy-start(f32[512,16]{0,1:T(8,128)} %param.9) | copy-start | bytes 98308
  237.5 7.6 %collective-permute-start.11 = (bf16[2,3,512]{2,0,1:T(2,128)(2,1)S(1)}, bf16[2,3,512]{2,0,1:T(2,128)(2,1)S(1)}, u32[]{:S(2)}, u32[]{:S(2)}) collective-permute-start(bf16[2,3,512]{2,0,1:T(2,128)(2,1)S(1)} %bitcast.119), channel_id=1, source_target_pairs={{0,16},{16,32},{32,48},{48,64},{64,80},{80,96},{96,112},{112,128},... | collective-permute-start | bytes 18440 | tf_op jit(solution)/shard_map/ppermute | solution.py:16
  247.5 4.0 %collective-permute-start.14 = (f32[512,16]{0,1:T(8,128)S(1)}, f32[512,16]{0,1:T(8,128)S(1)}, u32[]{:S(2)}, u32[]{:S(2)}) collective-permute-start(f32[512,16]{0,1:T(8,128)S(1)} %multiply_reduce_fusion), channel_id=1, source_target_pairs={{0,48},{16,0},{32,16},{48,32},{1,49},{17,1},{33,17},{49,33},{2,50}... | collective-permute-start | bytes 98312 | tf_op jit(solution)/shard_map/ppermute | solution.py:24
  247.6 5.7 %collective-permute-start.13 = (f32[512,16]{0,1:T(8,128)S(1)}, f32[512,16]{0,1:T(8,128)S(1)}, u32[]{:S(2)}, u32[]{:S(2)}) collective-permute-start(f32[512,16]{0,1:T(8,128)S(1)} %multiply_reduce_fusion), channel_id=1, source_target_pairs={{0,32},{16,48},{32,0},{48,16},{1,33},{17,49},{33,1},{49,17},{2,34}... | collective-permute-start | bytes 98312 | tf_op jit(solution)/shard_map/ppermute | solution.py:24
  249.3 5.1 %collective-permute-start.12 = (f32[512,16]{0,1:T(8,128)S(1)}, f32[512,16]{0,1:T(8,128)S(1)}, u32[]{:S(2)}, u32[]{:S(2)}) collective-permute-start(f32[512,16]{0,1:T(8,128)S(1)} %multiply_reduce_fusion), channel_id=1, source_target_pairs={{0,16},{16,32},{32,48},{48,0},{1,17},{17,33},{33,49},{49,1},{2,18}... | collective-permute-start | bytes 98312 | tf_op jit(solution)/shard_map/ppermute | solution.py:24
  254.5 6.9 %collective-permute-start.17 = (f32[4,512,16]{1,2,0:T(8,128)S(1)}, f32[4,512,16]{1,2,0:T(8,128)S(1)}, u32[]{:S(2)}, u32[]{:S(2)}) collective-permute-start(f32[4,512,16]{1,2,0:T(8,128)S(1)} %get-tuple-element.13), channel_id=1, source_target_pairs={{0,192},{64,0},{128,64},{192,128},{1,193},{65,1},{129,65},{193,129... | collective-permute-start | bytes 393224 | tf_op jit(solution)/shard_map/ppermute | solution.py:24
  257.0 6.1 %collective-permute-start.16 = (f32[4,512,16]{1,2,0:T(8,128)S(1)}, f32[4,512,16]{1,2,0:T(8,128)}, u32[]{:S(2)}, u32[]{:S(2)}) collective-permute-start(f32[4,512,16]{1,2,0:T(8,128)S(1)} %get-tuple-element.13), channel_id=1, source_target_pairs={{0,128},{64,192},{128,0},{192,64},{1,129},{65,193},{129,1},{193,65... | collective-permute-start | bytes 393224 | tf_op jit(solution)/shard_map/ppermute | solution.py:24
  257.0 6.9 %collective-permute-start.15 = (f32[4,512,16]{1,2,0:T(8,128)S(1)}, f32[4,512,16]{1,2,0:T(8,128)}, u32[]{:S(2)}, u32[]{:S(2)}) collective-permute-start(f32[4,512,16]{1,2,0:T(8,128)S(1)} %get-tuple-element.13), channel_id=1, source_target_pairs={{0,64},{64,128},{128,192},{192,0},{1,65},{65,129},{129,193},{193,1... | collective-permute-start | bytes 393224 | tf_op jit(solution)/shard_map/ppermute | solution.py:24
  258.9 6.3 %copy-start.6 = (f32[512,16]{0,1:T(8,128)S(1)}, f32[512,16]{0,1:T(8,128)}, u32[]{:S(2)}) copy-start(f32[512,16]{0,1:T(8,128)} %param.10) | copy-start | bytes 98308
  265.1 10.1 %copy-start.5 = (f32[512]{0:T(512)S(1)}, f32[512]{0:T(512)}, u32[]{:S(2)}) copy-start(f32[512]{0:T(512)} %param.11) | copy-start | bytes 6148
  (2 other events, 9.4 us)
Sparse Core Ops, SparseCore 0:
  25.4 40.9 all-gather.2

commit v7 on v6

--- a/solution.py
+++ b/solution.py
@@ -46,11 +46,14 @@
     feat_block = in_weight.shape[0]
     across, down = lax.axis_size("x"), lax.axis_size("zl")
     me_x, me_z = lax.axis_index("x"), lax.axis_index("zl")
-    flat_own = in_weight.reshape(feat_block, 3 * width_local)
-    below, above = line_gather(flat_own, "zl", down)
     halves = lax.axis_size("zh")
     pair = lax.axis_size("c")
     me_h = lax.axis_index("zh")
+    stream_count = in_weight.shape[1]
+    order = tuple(range(1, stream_count)) + (0,)
+    relays = {}
+    for s in order:
+        relays[s] = line_gather(in_weight[:, s, :], "zl", down)
     swap = [(a * across + b, b * across + a) for a in range(across) for b in range(across)]
     cross = [
         (a * across + b, b * across + ((a // pair + 1) % halves) * pair + a % pair)
@@ -62,27 +65,33 @@
     both = jnp.stack([jnp.where(me_h == 0, near, far), jnp.where(me_h == 0, far, near)])
     gathered = lax.all_gather(both, ("y", "c"), axis=0, tiled=False)
     blocks = gathered.reshape(-1, pair, halves, tok_rows, feat_block)
+
     def contribution(source, weight):
         taken = lax.dynamic_index_in_dim(blocks, source, axis=0, keepdims=False)
         return jnp.einsum("chru,uk->hcrk", taken, weight, preferred_element_type=jnp.float32)
 
-    partial = contribution(me_z, flat_own)
-    for d in range(1, down):
-        low, high = jnp.maximum(me_z - d, 0), jnp.minimum(me_z + d, down - 1)
-        if 2 * d <= down - 1:
-            partial = partial + contribution(low, below[d - 1])
-            partial = partial + contribution(high, above[d - 1])
-        else:
-            use_low = me_z - d >= 0
-            weight = jnp.where(use_low, below[d - 1], above[d - 1])
-            partial = partial + contribution(jnp.where(use_low, low, high), weight)
-    partial = partial.reshape(across, tok_rows, 3 * width_local)
-    projected = lax.dynamic_index_in_dim(partial, me_x, axis=0, keepdims=False)
-    for k in range(1, across):
-        route = [(i, (i + k) % across) for i in range(across)]
-        piece = lax.dynamic_index_in_dim(partial, (me_x + k) % across, axis=0, keepdims=False)
-        projected = projected + lax.ppermute(piece, "x", route)
-    streams = projected.astype(jnp.bfloat16).reshape(tok_rows, 3, width_local)
+    reduced = {}
+    for s in order:
+        below, above = relays[s]
+        partial = contribution(me_z, in_weight[:, s, :])
+        for d in range(1, down):
+            low, high = jnp.maximum(me_z - d, 0), jnp.minimum(me_z + d, down - 1)
+            if 2 * d <= down - 1:
+                partial = partial + contribution(low, below[d - 1])
+                partial = partial + contribution(high, above[d - 1])
+            else:
+                use_low = me_z - d >= 0
+                weight = jnp.where(use_low, below[d - 1], above[d - 1])
+                partial = partial + contribution(jnp.where(use_low, low, high), weight)
+        partial = partial.reshape(across, tok_rows, width_local)
+        total = lax.dynamic_index_in_dim(partial, me_x, axis=0, keepdims=False)
+        for k in range(1, across):
+            route = [(i, (i + k) % across) for i in range(across)]
+            piece = lax.dynamic_index_in_dim(partial, (me_x + k) % across, axis=0, keepdims=False)
+            total = total + lax.ppermute(piece, "x", route)
+        reduced[s] = total
+    projected = jnp.stack([reduced[s] for s in range(stream_count)], axis=1)
+    streams = projected.astype(jnp.bfloat16)
     tap_count = short_filter.shape[0]
     last_rows = streams[tok_rows - (tap_count - 1) :]
     before = from_behind(last_rows, SEQ, 1)

time: 286 us -> 253 us (0.88)
  waiting for transfers between devices: 160 us -> 121 us
  starting transfers between devices: 51.4 us -> 80.2 us
  matrix products: 41.3 us -> 25.9 us
  local copies, waits for them, and re-layouts: 6.56 us -> 2.63 us
    ppermute x1 -> x3, waiting for transfers between devices: 31.7 us -> 0.01 us  [line_gather(): near_b = lax.ppermute(piece, axis, [(i, i + 1) for i in range(size - 1)])]
    ppermute x2 -> x6, waiting for transfers between devices: 30.1 us -> 0.8 us  [line_gather(): lax.ppermute(near_b, axis, [(i, i + 1) for i in range(d - 1, size - 1)])]
    all_gather x1, waiting for transfers between devices: 0.01 us -> 21.2 us  [block(): gathered = lax.all_gather(both, ('y', 'c'), axis=0, tiled=False)]
    ppermute x3 -> x9, waiting for transfers between devices: 64.7 us -> 44.6 us  [block(): total = total + lax.ppermute(piece, 'x', route)]
    ppermute x2 -> x6, waiting for transfers between devices: 14.8 us -> 33.6 us  [line_gather(): lax.ppermute(near_a, axis, [(i + 1, i) for i in range(0, size - d)])]
    dot_general x5 -> x15, matrix products: 31.2 us -> 15.8 us  [contribution(): jnp.einsum('chru,uk->hcrk', taken, weight, preferred_element_type=jnp.flo...]
    ppermute x1 -> x3, starting transfers between devices: 6.81 us -> 14.6 us  [line_gather(): near_b = lax.ppermute(piece, axis, [(i, i + 1) for i in range(size - 1)])]
    ppermute x2 -> x6, starting transfers between devices: 5.37 us -> 12.9 us  [line_gather(): lax.ppermute(near_a, axis, [(i + 1, i) for i in range(0, size - d)])]
  transfers between devices with their start and end apart: 19 -> 37, of which waited for: 14 -> 21; matrix products, arithmetic and copies ran while one was open for 9% -> 8% of each run, Pallas kernels for 0% -> 0%
where the time goes in v7:
time: 253 us; the launch traced here: 252 us
  waiting for transfers between devices  121 us (48%)
  starting transfers between devices  80.2 us (32%)
  matrix products  25.9 us (10%)
  between operations  14.1 us (6%)
  other arithmetic  7.38 us (3%)
  local copies, waits for them, and re-layouts  2.63 us (1%)
    ppermute x9, waiting for transfers between devices, block(): total = total + lax.ppermute(piece, 'x', route)  44.6 us
    ppermute x6, waiting for transfers between devices, line_gather(): lax.ppermute(near_a, axis, [(i + 1, i) for i in range(0, size - d)])  33.6 us
    all_gather x1, waiting for transfers between devices, block(): gathered = lax.all_gather(both, ('y', 'c'), axis=0, tiled=False)  21.2 us
    dot_general x15, matrix products, contribution(): jnp.einsum('chru,uk->hcrk', taken, weight, preferred_element_type=jnp.flo...  15.8 us
    ppermute x9, starting transfers between devices, block(): total = total + lax.ppermute(piece, 'x', route)  14.9 us
    ppermute x3, starting transfers between devices, line_gather(): near_b = lax.ppermute(piece, axis, [(i, i + 1) for i in range(size - 1)])  14.6 us
    ppermute x6, starting transfers between devices, line_gather(): lax.ppermute(near_a, axis, [(i + 1, i) for i in range(0, size - d)])  12.9 us
    ppermute x6, starting transfers between devices, line_gather(): lax.ppermute(near_b, axis, [(i, i + 1) for i in range(d - 1, size - 1)])  12.9 us
  transfers between devices with their start and end apart: 37, of which 21 were waited for; matrix products, arithmetic and copies ran while one was open for 8% of the time, Pallas kernels for 0%

profile of v7, /device:TPU:32, one launch (start us, length us, event | category | flops | bytes accessed | tf_op | source)
XLA Modules:
  0.0 251.5 jit_solution(18381438728377211637)
XLA Ops:
  8.3 8.8 %collective-permute-start.1 = (bf16[256,512]{1,0:T(8,128)(2,1)}, bf16[256,512]{1,0:T(8,128)(2,1)S(1)}, u32[]{:S(2)}, u32[]{:S(2)}) collective-permute-start(bf16[256,512]{1,0:T(8,128)(2,1)} %param.6), channel_id=1, source_target_pairs={{0,2},{1,18},{2,34},{3,50},{16,3},{17,19},{18,35},{19,51},{32,0},{... | collective-permute-start | bytes 786440 | tf_op jit(solution)/shard_map/ppermute | solution.py:64
  17.0 7.3 %collective-permute-done.1 = bf16[256,512]{1,0:T(8,128)(2,1)S(1)} collective-permute-done((bf16[256,512]{1,0:T(8,128)(2,1)}, bf16[256,512]{1,0:T(8,128)(2,1)S(1)}, u32[]{:S(2)}, u32[]{:S(2)}) %collective-permute-start.1) | collective-permute-done | bytes 262176 | tf_op jit(solution)/shard_map/ppermute | solution.py:64
  26.5 6.8 %collective-permute-start.2 = (bf16[512,512]{1,0:T(8,128)(2,1)}, bf16[512,512]{1,0:T(8,128)(2,1)}, u32[]{:S(2)}, u32[]{:S(2)}) collective-permute-start(bf16[512,512]{1,0:T(8,128)(2,1)} %get-tuple-element.16), channel_id=1, source_target_pairs={{0,64},{64,128},{128,192},{1,65},{65,129},{129,193},{2,66},{66,130... | collective-permute-start | bytes 1572872 | tf_op jit(solution)/shard_map/ppermute | solution.py:30
  35.3 3.9 %collective-permute-start.11 = (bf16[512,512]{1,0:T(8,128)(2,1)}, bf16[512,512]{1,0:T(8,128)(2,1)S(1)}, u32[]{:S(2)}, u32[]{:S(2)}) collective-permute-start(bf16[512,512]{1,0:T(8,128)(2,1)} %get-tuple-element.18), channel_id=1, source_target_pairs={{0,64},{64,128},{128,192},{1,65},{65,129},{129,193},{2,66},{66,130... | collective-permute-start | bytes 1572872 | tf_op jit(solution)/shard_map/ppermute | solution.py:30
  41.2 3.9 %collective-permute-start.20 = (bf16[512,512]{1,0:T(8,128)(2,1)}, bf16[512,512]{1,0:T(8,128)(2,1)S(1)}, u32[]{:S(2)}, u32[]{:S(2)}) collective-permute-start(bf16[512,512]{1,0:T(8,128)(2,1)} %get-tuple-element.17), channel_id=1, source_target_pairs={{0,64},{64,128},{128,192},{1,65},{65,129},{129,193},{2,66},{66,130... | collective-permute-start | bytes 1572872 | tf_op jit(solution)/shard_map/ppermute | solution.py:30
  45.2 21.2 %all-gather.3.cloned.1.call-done = bf16[16,256,512]{2,1,0:T(8,128)(2,1)} async-done(((bf16[2,256,512]{2,1,0:T(8,128)(2,1)}), bf16[16,256,512]{2,1,0:T(8,128)(2,1)}) %all-gather.3.cloned.1.call-update) | async-done | bytes 4194320 | tf_op jit(solution)/shard_map/all_gather | solution.py:66
  72.9 3.5 %collective-permute-start.4 = (bf16[512,512]{1,0:T(8,128)(2,1)}, bf16[512,512]{1,0:T(8,128)(2,1)S(1)}, u32[]{:S(2)}, u32[]{:S(2)}) collective-permute-start(bf16[512,512]{1,0:T(8,128)(2,1)} %collective-permute-done.2), channel_id=1, source_target_pairs={{64,128},{128,192},{65,129},{129,193},{66,130},{130,194},{67,131},... | collective-permute-start | bytes 1572872 | tf_op jit(solution)/shard_map/ppermute | solution.py:35
  78.3 4.0 %collective-permute-start.13 = (bf16[512,512]{1,0:T(8,128)(2,1)S(1)}, bf16[512,512]{1,0:T(8,128)(2,1)S(1)}, u32[]{:S(2)}, u32[]{:S(2)}) collective-permute-start(bf16[512,512]{1,0:T(8,128)(2,1)S(1)} %collective-permute-done.11), channel_id=1, source_target_pairs={{64,128},{128,192},{65,129},{129,193},{66,130},{130,194},{67,131},... | collective-permute-start | bytes 1572872 | tf_op jit(solution)/shard_map/ppermute | solution.py:35
  87.4 3.3 %collective-permute-start.22 = (bf16[512,512]{1,0:T(8,128)(2,1)S(1)}, bf16[512,512]{1,0:T(8,128)(2,1)S(1)}, u32[]{:S(2)}, u32[]{:S(2)}) collective-permute-start(bf16[512,512]{1,0:T(8,128)(2,1)S(1)} %collective-permute-done.20), channel_id=1, source_target_pairs={{64,128},{128,192},{65,129},{129,193},{66,130},{130,194},{67,131},... | collective-permute-start | bytes 1572872 | tf_op jit(solution)/shard_map/ppermute | solution.py:35
  92.7 6.0 %collective-permute-done.5 = bf16[512,512]{1,0:T(8,128)(2,1)S(1)} collective-permute-done((bf16[512,512]{1,0:T(8,128)(2,1)}, bf16[512,512]{1,0:T(8,128)(2,1)S(1)}, u32[]{:S(2)}, u32[]{:S(2)}) %collective-permute-start.5) | collective-permute-done | bytes 524320 | tf_op jit(solution)/shard_map/ppermute | solution.py:36
  104.2 5.6 %collective-permute-done.14 = bf16[512,512]{1,0:T(8,128)(2,1)S(1)} collective-permute-done((bf16[512,512]{1,0:T(8,128)(2,1)S(1)}, bf16[512,512]{1,0:T(8,128)(2,1)S(1)}, u32[]{:S(2)}, u32[]{:S(2)}) %collective-permute-start.14) | collective-permute-done | bytes 524320 | tf_op jit(solution)/shard_map/ppermute | solution.py:36
  113.0 7.4 %collective-permute-done.23 = bf16[512,512]{1,0:T(8,128)(2,1)S(1)} collective-permute-done((bf16[512,512]{1,0:T(8,128)(2,1)S(1)}, bf16[512,512]{1,0:T(8,128)(2,1)S(1)}, u32[]{:S(2)}, u32[]{:S(2)}) %collective-permute-start.23) | collective-permute-done | bytes 524320 | tf_op jit(solution)/shard_map/ppermute | solution.py:36
  121.1 3.1 %collective-permute-start.25 = (bf16[512,512]{1,0:T(8,128)(2,1)S(1)}, bf16[512,512]{1,0:T(8,128)(2,1)S(1)}, u32[]{:S(2)}, u32[]{:S(2)}) collective-permute-start(bf16[512,512]{1,0:T(8,128)(2,1)S(1)} %collective-permute-done.23), channel_id=1, source_target_pairs={{64,0},{65,1},{66,2},{67,3},{68,4},{69,5},{70,6},{71,7},{72,8},{73... | collective-permute-start | bytes 1572872 | tf_op jit(solution)/shard_map/ppermute | solution.py:36
  124.2 6.1 %collective-permute-done.7 = bf16[512,512]{1,0:T(8,128)(2,1)S(1)} collective-permute-done((bf16[512,512]{1,0:T(8,128)(2,1)S(1)}, bf16[512,512]{1,0:T(8,128)(2,1)S(1)}, u32[]{:S(2)}, u32[]{:S(2)}) %collective-permute-start.7) | collective-permute-done | bytes 524320 | tf_op jit(solution)/shard_map/ppermute | solution.py:36
  137.2 4.3 %collective-permute-done.16 = bf16[512,512]{1,0:T(8,128)(2,1)S(1)} collective-permute-done((bf16[512,512]{1,0:T(8,128)(2,1)S(1)}, bf16[512,512]{1,0:T(8,128)(2,1)S(1)}, u32[]{:S(2)}, u32[]{:S(2)}) %collective-permute-start.16) | collective-permute-done | bytes 524320 | tf_op jit(solution)/shard_map/ppermute | solution.py:36
  147.8 4.2 %collective-permute-done.25 = bf16[512,512]{1,0:T(8,128)(2,1)S(1)} collective-permute-done((bf16[512,512]{1,0:T(8,128)(2,1)S(1)}, bf16[512,512]{1,0:T(8,128)(2,1)S(1)}, u32[]{:S(2)}, u32[]{:S(2)}) %collective-permute-start.25) | collective-permute-done | bytes 524320 | tf_op jit(solution)/shard_map/ppermute | solution.py:36
  155.0 12.3 %collective-permute-done.10 = f32[256,512]{1,0:T(8,128)S(1)} collective-permute-done((f32[256,512]{1,0:T(8,128)S(1)}, f32[256,512]{1,0:T(8,128)S(1)}, u32[]{:S(2)}, u32[]{:S(2)}) %collective-permute-start.10) | collective-permute-done | bytes 524320 | tf_op jit(solution)/shard_map/ppermute | solution.py:91
  167.4 3.9 %collective-permute-start.19 = (f32[256,512]{1,0:T(8,128)S(1)}, f32[256,512]{1,0:T(8,128)S(1)}, u32[]{:S(2)}, u32[]{:S(2)}) collective-permute-start(f32[256,512]{1,0:T(8,128)S(1)} %get-tuple-element.11), channel_id=1, source_target_pairs={{0,48},{16,0},{32,16},{48,32},{1,49},{17,1},{33,17},{49,33},{2,50}... | collective-permute-start | bytes 1572872 | tf_op jit(solution)/shard_map/ppermute | solution.py:91
  174.0 12.7 %collective-permute-done.17 = f32[256,512]{1,0:T(8,128)S(1)} collective-permute-done((f32[256,512]{1,0:T(8,128)S(1)}, f32[256,512]{1,0:T(8,128)S(1)}, u32[]{:S(2)}, u32[]{:S(2)}) %collective-permute-start.17) | collective-permute-done | bytes 524320 | tf_op jit(solution)/shard_map/ppermute | solution.py:91
  187.0 7.9 %collective-permute-done.19 = f32[256,512]{1,0:T(8,128)S(1)} collective-permute-done((f32[256,512]{1,0:T(8,128)S(1)}, f32[256,512]{1,0:T(8,128)S(1)}, u32[]{:S(2)}, u32[]{:S(2)}) %collective-permute-start.19) | collective-permute-done | bytes 524320 | tf_op jit(solution)/shard_map/ppermute | solution.py:91
  195.1 11.7 %collective-permute-done.26 = f32[256,512]{1,0:T(8,128)S(1)} collective-permute-done((f32[256,512]{1,0:T(8,128)S(1)}, f32[256,512]{1,0:T(8,128)S(1)}, u32[]{:S(2)}, u32[]{:S(2)}) %collective-permute-start.26) | collective-permute-done | bytes 524320 | tf_op jit(solution)/shard_map/ppermute | solution.py:91
  209.1 5.7 %collective-permute-done.29 = bf16[2,3,512]{2,0,1:T(2,128)(2,1)S(1)} collective-permute-done((bf16[2,3,512]{2,0,1:T(2,128)(2,1)S(1)}, bf16[2,3,512]{2,0,1:T(2,128)(2,1)S(1)}, u32[]{:S(2)}, u32[]{:S(2)}) %collective-permute-start.29) | collective-permute-done | bytes 6176 | tf_op jit(solution)/shard_map/ppermute | solution.py:16
  217.3 3.1 %collective-permute-start.32 = (f32[512,16]{0,1:T(8,128)S(1)}, f32[512,16]{0,1:T(8,128)S(1)}, u32[]{:S(2)}, u32[]{:S(2)}) collective-permute-start(f32[512,16]{0,1:T(8,128)S(1)} %multiply_reduce_fusion), channel_id=1, source_target_pairs={{0,48},{16,0},{32,16},{48,32},{1,49},{17,1},{33,17},{49,33},{2,50}... | collective-permute-start | bytes 98312 | tf_op jit(solution)/shard_map/ppermute | solution.py:24
  233.8 10.1 %multiply_reduce_fusion.1 = f32[256,512]{1,0:T(8,128)S(1)} fusion(f32[512,16]{0,1:T(8,128)S(1)} %exponential_multiply_fusion, f32[512,16]{0,1:T(8,128)S(1)} %neg.8, f32[512,16]{0,1:T(8,128)S(1)} %copy-done.5, f32[512,16,256]{2,1,0:T(8,128)S(1)} %bitcast.264), kind=kOutput, calls=%fused_computation.4 | convolution fusion | flops 6452871168 | bytes 9011200 | tf_op jit(solution)/shard_map/dot_general | solution.py:126
  (112 shorter events, 70.5 us)
Async XLA Ops:
  6.5 59.9 %all-gather.3.cloned.1.call-start = ((), (), s32[]{:S(2)}) async-start(), calls=%async_computation | async-start | bytes 4718592 | tf_op jit(solution)/shard_map/all_gather | solution.py:66
  26.5 43.9 %collective-permute-start.2 = (bf16[512,512]{1,0:T(8,128)(2,1)}, bf16[512,512]{1,0:T(8,128)(2,1)}, u32[]{:S(2)}, u32[]{:S(2)}) collective-permute-start(bf16[512,512]{1,0:T(8,128)(2,1)} %get-tuple-element.16), channel_id=1, source_target_pairs={{0,64},{64,128},{128,192},{1,65},{65,129},{129,193},{2,66},{66,130... | collective-permute-start | bytes 1572872 | tf_op jit(solution)/shard_map/ppermute | solution.py:30
  33.4 39.5 %collective-permute-start.3 = (bf16[512,512]{1,0:T(8,128)(2,1)}, bf16[512,512]{1,0:T(8,128)(2,1)}, u32[]{:S(2)}, u32[]{:S(2)}) collective-permute-start(bf16[512,512]{1,0:T(8,128)(2,1)} %get-tuple-element.16), channel_id=1, source_target_pairs={{64,0},{128,64},{192,128},{65,1},{129,65},{193,129},{66,2},{130,66... | collective-permute-start | bytes 1572872 | tf_op jit(solution)/shard_map/ppermute | solution.py:31
  35.3 41.1 %collective-permute-start.11 = (bf16[512,512]{1,0:T(8,128)(2,1)}, bf16[512,512]{1,0:T(8,128)(2,1)S(1)}, u32[]{:S(2)}, u32[]{:S(2)}) collective-permute-start(bf16[512,512]{1,0:T(8,128)(2,1)} %get-tuple-element.18), channel_id=1, source_target_pairs={{0,64},{64,128},{128,192},{1,65},{65,129},{129,193},{2,66},{66,130... | collective-permute-start | bytes 1572872 | tf_op jit(solution)/shard_map/ppermute | solution.py:30
  39.2 39.1 %collective-permute-start.12 = (bf16[512,512]{1,0:T(8,128)(2,1)}, bf16[512,512]{1,0:T(8,128)(2,1)S(1)}, u32[]{:S(2)}, u32[]{:S(2)}) collective-permute-start(bf16[512,512]{1,0:T(8,128)(2,1)} %get-tuple-element.18), channel_id=1, source_target_pairs={{64,0},{128,64},{192,128},{65,1},{129,65},{193,129},{66,2},{130,66... | collective-permute-start | bytes 1572872 | tf_op jit(solution)/shard_map/ppermute | solution.py:31
  41.2 43.6 %collective-permute-start.20 = (bf16[512,512]{1,0:T(8,128)(2,1)}, bf16[512,512]{1,0:T(8,128)(2,1)S(1)}, u32[]{:S(2)}, u32[]{:S(2)}) collective-permute-start(bf16[512,512]{1,0:T(8,128)(2,1)} %get-tuple-element.17), channel_id=1, source_target_pairs={{0,64},{64,128},{128,192},{1,65},{65,129},{129,193},{2,66},{66,130... | collective-permute-start | bytes 1572872 | tf_op jit(solution)/shard_map/ppermute | solution.py:30
  76.4 22.2 %collective-permute-start.5 = (bf16[512,512]{1,0:T(8,128)(2,1)}, bf16[512,512]{1,0:T(8,128)(2,1)S(1)}, u32[]{:S(2)}, u32[]{:S(2)}) collective-permute-start(bf16[512,512]{1,0:T(8,128)(2,1)} %collective-permute-done.3), channel_id=1, source_target_pairs={{64,0},{128,64},{65,1},{129,65},{66,2},{130,66},{67,3},{131,67},{6... | collective-permute-start | bytes 1572872 | tf_op jit(solution)/shard_map/ppermute | solution.py:36
  84.8 25.1 %collective-permute-start.14 = (bf16[512,512]{1,0:T(8,128)(2,1)S(1)}, bf16[512,512]{1,0:T(8,128)(2,1)S(1)}, u32[]{:S(2)}, u32[]{:S(2)}) collective-permute-start(bf16[512,512]{1,0:T(8,128)(2,1)S(1)} %collective-permute-done.12), channel_id=1, source_target_pairs={{64,0},{128,64},{65,1},{129,65},{66,2},{130,66},{67,3},{131,67},{6... | collective-permute-start | bytes 1572872 | tf_op jit(solution)/shard_map/ppermute | solution.py:36
  87.4 23.2 %collective-permute-start.22 = (bf16[512,512]{1,0:T(8,128)(2,1)S(1)}, bf16[512,512]{1,0:T(8,128)(2,1)S(1)}, u32[]{:S(2)}, u32[]{:S(2)}) collective-permute-start(bf16[512,512]{1,0:T(8,128)(2,1)S(1)} %collective-permute-done.20), channel_id=1, source_target_pairs={{64,128},{128,192},{65,129},{129,193},{66,130},{130,194},{67,131},... | collective-permute-start | bytes 1572872 | tf_op jit(solution)/shard_map/ppermute | solution.py:35
  90.7 29.6 %collective-permute-start.23 = (bf16[512,512]{1,0:T(8,128)(2,1)S(1)}, bf16[512,512]{1,0:T(8,128)(2,1)S(1)}, u32[]{:S(2)}, u32[]{:S(2)}) collective-permute-start(bf16[512,512]{1,0:T(8,128)(2,1)S(1)} %collective-permute-done.21), channel_id=1, source_target_pairs={{64,0},{128,64},{65,1},{129,65},{66,2},{130,66},{67,3},{131,67},{6... | collective-permute-start | bytes 1572872 | tf_op jit(solution)/shard_map/ppermute | solution.py:36
  98.6 22.4 %collective-permute-start.6 = (bf16[512,512]{1,0:T(8,128)(2,1)S(1)}, bf16[512,512]{1,0:T(8,128)(2,1)S(1)}, u32[]{:S(2)}, u32[]{:S(2)}) collective-permute-start(bf16[512,512]{1,0:T(8,128)(2,1)S(1)} %collective-permute-done.4), channel_id=1, source_target_pairs={{128,192},{129,193},{130,194},{131,195},{132,196},{133,197},{134,1... | collective-permute-start | bytes 1572872 | tf_op jit(solution)/shard_map/ppermute | solution.py:35
  100.1 30.2 %collective-permute-start.7 = (bf16[512,512]{1,0:T(8,128)(2,1)S(1)}, bf16[512,512]{1,0:T(8,128)(2,1)S(1)}, u32[]{:S(2)}, u32[]{:S(2)}) collective-permute-start(bf16[512,512]{1,0:T(8,128)(2,1)S(1)} %collective-permute-done.5), channel_id=1, source_target_pairs={{64,0},{65,1},{66,2},{67,3},{68,4},{69,5},{70,6},{71,7},{72,8},{73... | collective-permute-start | bytes 1572872 | tf_op jit(solution)/shard_map/ppermute | solution.py:36
  109.8 27.3 %collective-permute-start.15 = (bf16[512,512]{1,0:T(8,128)(2,1)S(1)}, bf16[512,512]{1,0:T(8,128)(2,1)S(1)}, u32[]{:S(2)}, u32[]{:S(2)}) collective-permute-start(bf16[512,512]{1,0:T(8,128)(2,1)S(1)} %collective-permute-done.13), channel_id=1, source_target_pairs={{128,192},{129,193},{130,194},{131,195},{132,196},{133,197},{134,1... | collective-permute-start | bytes 1572872 | tf_op jit(solution)/shard_map/ppermute | solution.py:35
  110.5 31.0 %collective-permute-start.16 = (bf16[512,512]{1,0:T(8,128)(2,1)S(1)}, bf16[512,512]{1,0:T(8,128)(2,1)S(1)}, u32[]{:S(2)}, u32[]{:S(2)}) collective-permute-start(bf16[512,512]{1,0:T(8,128)(2,1)S(1)} %collective-permute-done.14), channel_id=1, source_target_pairs={{64,0},{65,1},{66,2},{67,3},{68,4},{69,5},{70,6},{71,7},{72,8},{73... | collective-permute-start | bytes 1572872 | tf_op jit(solution)/shard_map/ppermute | solution.py:36
  120.4 26.8 %collective-permute-start.24 = (bf16[512,512]{1,0:T(8,128)(2,1)S(1)}, bf16[512,512]{1,0:T(8,128)(2,1)S(1)}, u32[]{:S(2)}, u32[]{:S(2)}) collective-permute-start(bf16[512,512]{1,0:T(8,128)(2,1)S(1)} %collective-permute-done.22), channel_id=1, source_target_pairs={{128,192},{129,193},{130,194},{131,195},{132,196},{133,197},{134,1... | collective-permute-start | bytes 1572872 | tf_op jit(solution)/shard_map/ppermute | solution.py:35
  121.1 31.0 %collective-permute-start.25 = (bf16[512,512]{1,0:T(8,128)(2,1)S(1)}, bf16[512,512]{1,0:T(8,128)(2,1)S(1)}, u32[]{:S(2)}, u32[]{:S(2)}) collective-permute-start(bf16[512,512]{1,0:T(8,128)(2,1)S(1)} %collective-permute-done.23), channel_id=1, source_target_pairs={{64,0},{65,1},{66,2},{67,3},{68,4},{69,5},{70,6},{71,7},{72,8},{73... | collective-permute-start | bytes 1572872 | tf_op jit(solution)/shard_map/ppermute | solution.py:36
  131.5 35.9 %collective-permute-start.10 = (f32[256,512]{1,0:T(8,128)S(1)}, f32[256,512]{1,0:T(8,128)S(1)}, u32[]{:S(2)}, u32[]{:S(2)}) collective-permute-start(f32[256,512]{1,0:T(8,128)S(1)} %get-tuple-element.8), channel_id=1, source_target_pairs={{0,48},{16,0},{32,16},{48,32},{1,49},{17,1},{33,17},{49,33},{2,50}... | collective-permute-start | bytes 1572872 | tf_op jit(solution)/shard_map/ppermute | solution.py:91
  137.1 35.4 %collective-permute-start.8 = (f32[256,512]{1,0:T(8,128)S(1)}, f32[256,512]{1,0:T(8,128)S(1)}, u32[]{:S(2)}, u32[]{:S(2)}) collective-permute-start(f32[256,512]{1,0:T(8,128)S(1)} %get-tuple-element.7), channel_id=1, source_target_pairs={{0,16},{16,32},{32,48},{48,0},{1,17},{17,33},{33,49},{49,1},{2,18}... | collective-permute-start | bytes 1572872 | tf_op jit(solution)/shard_map/ppermute | solution.py:91
  141.5 31.1 %collective-permute-start.9 = (f32[256,512]{1,0:T(8,128)S(1)}, f32[256,512]{1,0:T(8,128)S(1)}, u32[]{:S(2)}, u32[]{:S(2)}) collective-permute-start(f32[256,512]{1,0:T(8,128)S(1)} %get-tuple-element.9), channel_id=1, source_target_pairs={{0,32},{16,48},{32,0},{48,16},{1,33},{17,49},{33,1},{49,17},{2,34}... | collective-permute-start | bytes 1572872 | tf_op jit(solution)/shard_map/ppermute | solution.py:91
  147.2 39.5 %collective-permute-start.17 = (f32[256,512]{1,0:T(8,128)S(1)}, f32[256,512]{1,0:T(8,128)S(1)}, u32[]{:S(2)}, u32[]{:S(2)}) collective-permute-start(f32[256,512]{1,0:T(8,128)S(1)} %get-tuple-element.10), channel_id=1, source_target_pairs={{0,16},{16,32},{32,48},{48,0},{1,17},{17,33},{33,49},{49,1},{2,18}... | collective-permute-start | bytes 1572872 | tf_op jit(solution)/shard_map/ppermute | solution.py:91
  152.1 34.9 %collective-permute-start.18 = (f32[256,512]{1,0:T(8,128)S(1)}, f32[256,512]{1,0:T(8,128)S(1)}, u32[]{:S(2)}, u32[]{:S(2)}) collective-permute-start(f32[256,512]{1,0:T(8,128)S(1)} %get-tuple-element.12), channel_id=1, source_target_pairs={{0,32},{16,48},{32,0},{48,16},{1,33},{17,49},{33,1},{49,17},{2,34}... | collective-permute-start | bytes 1572872 | tf_op jit(solution)/shard_map/ppermute | solution.py:91
  167.4 27.5 %collective-permute-start.19 = (f32[256,512]{1,0:T(8,128)S(1)}, f32[256,512]{1,0:T(8,128)S(1)}, u32[]{:S(2)}, u32[]{:S(2)}) collective-permute-start(f32[256,512]{1,0:T(8,128)S(1)} %get-tuple-element.11), channel_id=1, source_target_pairs={{0,48},{16,0},{32,16},{48,32},{1,49},{17,1},{33,17},{49,33},{2,50}... | collective-permute-start | bytes 1572872 | tf_op jit(solution)/shard_map/ppermute | solution.py:91
  172.5 34.3 %collective-permute-start.26 = (f32[256,512]{1,0:T(8,128)S(1)}, f32[256,512]{1,0:T(8,128)S(1)}, u32[]{:S(2)}, u32[]{:S(2)}) collective-permute-start(f32[256,512]{1,0:T(8,128)S(1)} %get-tuple-element.13), channel_id=1, source_target_pairs={{0,16},{16,32},{32,48},{48,0},{1,17},{17,33},{33,49},{49,1},{2,18}... | collective-permute-start | bytes 1572872 | tf_op jit(solution)/shard_map/ppermute | solution.py:91
  172.6 34.2 %collective-permute-start.27 = (f32[256,512]{1,0:T(8,128)S(1)}, f32[256,512]{1,0:T(8,128)S(1)}, u32[]{:S(2)}, u32[]{:S(2)}) collective-permute-start(f32[256,512]{1,0:T(8,128)S(1)} %get-tuple-element.15), channel_id=1, source_target_pairs={{0,32},{16,48},{32,0},{48,16},{1,33},{17,49},{33,1},{49,17},{2,34}... | collective-permute-start | bytes 1572872 | tf_op jit(solution)/shard_map/ppermute | solution.py:91
  (19 other events, 231.9 us)
Sparse Core Ops, SparseCore 0:
  25.5 40.9 all-gather.2

commit v8 on v7

--- a/solution.py
+++ b/solution.py
@@ -50,10 +50,11 @@
     pair = lax.axis_size("c")
     me_h = lax.axis_index("zh")
     stream_count = in_weight.shape[1]
-    order = tuple(range(1, stream_count)) + (0,)
+    order = (tuple(range(1, stream_count)), (0,))
     relays = {}
     for s in order:
-        relays[s] = line_gather(in_weight[:, s, :], "zl", down)
+        own = in_weight[:, s[0] : s[-1] + 1, :].reshape(feat_block, len(s) * width_local)
+        relays[s] = (own, line_gather(own, "zl", down))
     swap = [(a * across + b, b * across + a) for a in range(across) for b in range(across)]
     cross = [
         (a * across + b, b * across + ((a // pair + 1) % halves) * pair + a % pair)
@@ -72,8 +73,8 @@
 
     reduced = {}
     for s in order:
-        below, above = relays[s]
-        partial = contribution(me_z, in_weight[:, s, :])
+        own, (below, above) = relays[s]
+        partial = contribution(me_z, own)
         for d in range(1, down):
             low, high = jnp.maximum(me_z - d, 0), jnp.minimum(me_z + d, down - 1)
             if 2 * d <= down - 1:
@@ -83,14 +84,15 @@
                 use_low = me_z - d >= 0
                 weight = jnp.where(use_low, below[d - 1], above[d - 1])
                 partial = partial + contribution(jnp.where(use_low, low, high), weight)
-        partial = partial.reshape(across, tok_rows, width_local)
+        partial = partial.reshape(across, tok_rows, len(s) * width_local)
         total = lax.dynamic_index_in_dim(partial, me_x, axis=0, keepdims=False)
         for k in range(1, across):
             route = [(i, (i + k) % across) for i in range(across)]
             piece = lax.dynamic_index_in_dim(partial, (me_x + k) % across, axis=0, keepdims=False)
             total = total + lax.ppermute(piece, "x", route)
-        reduced[s] = total
-    projected = jnp.stack([reduced[s] for s in range(stream_count)], axis=1)
+        for n, t in enumerate(s):
+            reduced[t] = total[:, n * width_local : (n + 1) * width_local]
+    projected = jnp.stack([reduced[t] for t in range(stream_count)], axis=1)
     streams = projected.astype(jnp.bfloat16)
     tap_count = short_filter.shape[0]
     last_rows = streams[tok_rows - (tap_count - 1) :]

time: 253 us -> 278 us (1.099)
  waiting for transfers between devices: 121 us -> 133 us
  local copies, waits for them, and re-layouts: 2.63 us -> 10.6 us
  matrix products: 25.9 us -> 29.5 us
  starting transfers between devices: 80.2 us -> 77 us
  other arithmetic: 7.38 us -> 10.4 us
    ppermute x6 -> x4, waiting for transfers between devices: 33.6 us -> 7.21 us  [line_gather(): lax.ppermute(near_a, axis, [(i + 1, i) for i in range(0, size - d)])]
    ppermute x6 -> x4, waiting for transfers between devices: 0.8 us -> 23.7 us  [line_gather(): lax.ppermute(near_b, axis, [(i, i + 1) for i in range(d - 1, size - 1)])]
    all_gather x1, waiting for transfers between devices: 21.2 us -> 0.01 us  [block(): gathered = lax.all_gather(both, ('y', 'c'), axis=0, tiled=False)]
    ppermute x9 -> x6, waiting for transfers between devices: 44.6 us -> 63.5 us  [block(): total = total + lax.ppermute(piece, 'x', route)]
    ppermute x3 -> x2, waiting for transfers between devices: 0.01 us -> 17.8 us  [line_gather(): near_b = lax.ppermute(piece, axis, [(i, i + 1) for i in range(size - 1)])]
    ppermute x9 -> x6, starting transfers between devices: 14.9 us -> 20.6 us  [block(): total = total + lax.ppermute(piece, 'x', route)]
    ppermute x6 -> x4, starting transfers between devices: 12.9 us -> 8.34 us  [line_gather(): lax.ppermute(near_a, axis, [(i + 1, i) for i in range(0, size - d)])]
    ppermute x3 -> x2, starting transfers between devices: 14.6 us -> 10.7 us  [line_gather(): near_b = lax.ppermute(piece, axis, [(i, i + 1) for i in range(size - 1)])]
  transfers between devices with their start and end apart: 37 -> 28, of which waited for: 21 -> 13; matrix products, arithmetic and copies ran while one was open for 8% -> 11% of each run, Pallas kernels for 0% -> 0%
where the time goes in v8:
time: 278 us; the launch traced here: 274 us
  waiting for transfers between devices  133 us (48%)
  starting transfers between devices  77 us (28%)
  matrix products  29.5 us (11%)
  between operations  14 us (5%)
  local copies, waits for them, and re-layouts  10.6 us (4%)
  other arithmetic  10.4 us (4%)
    ppermute x6, waiting for transfers between devices, block(): total = total + lax.ppermute(piece, 'x', route)  63.5 us
    ppermute x4, waiting for transfers between devices, line_gather(): lax.ppermute(near_b, axis, [(i, i + 1) for i in range(d - 1, size - 1)])  23.7 us
    ppermute x6, starting transfers between devices, block(): total = total + lax.ppermute(piece, 'x', route)  20.6 us
    dot_general x10, matrix products, contribution(): jnp.einsum('chru,uk->hcrk', taken, weight, preferred_element_type=jnp.flo...  19.4 us
    ppermute x2, waiting for transfers between devices, line_gather(): near_b = lax.ppermute(piece, axis, [(i, i + 1) for i in range(size - 1)])  17.8 us
    ppermute x4, starting transfers between devices, line_gather(): lax.ppermute(near_b, axis, [(i, i + 1) for i in range(d - 1, size - 1)])  13.1 us
    ppermute x2, starting transfers between devices, line_gather(): near_b = lax.ppermute(piece, axis, [(i, i + 1) for i in range(size - 1)])  10.7 us
    dot_general x1, matrix products, block(): jnp.dot(lower_mask, scaled, precision=exact_mode)  10.1 us
  transfers between devices with their start and end apart: 28, of which 13 were waited for; matrix products, arithmetic and copies ran while one was open for 11% of the time, Pallas kernels for 0%

profile of v8, /device:TPU:32, one launch (start us, length us, event | category | flops | bytes accessed | tf_op | source)
XLA Modules:
  0.0 274.3 jit_solution(1252167500561312006)
XLA Ops:
  8.1 8.8 %collective-permute-start.1 = (bf16[256,512]{1,0:T(8,128)(2,1)}, bf16[256,512]{1,0:T(8,128)(2,1)S(1)}, u32[]{:S(2)}, u32[]{:S(2)}) collective-permute-start(bf16[256,512]{1,0:T(8,128)(2,1)} %param.6), channel_id=1, source_target_pairs={{0,2},{1,18},{2,34},{3,50},{16,3},{17,19},{18,35},{19,51},{32,0},{... | collective-permute-start | bytes 786440 | tf_op jit(solution)/shard_map/ppermute | solution.py:65
  16.9 7.3 %collective-permute-done.1 = bf16[256,512]{1,0:T(8,128)(2,1)S(1)} collective-permute-done((bf16[256,512]{1,0:T(8,128)(2,1)}, bf16[256,512]{1,0:T(8,128)(2,1)S(1)}, u32[]{:S(2)}, u32[]{:S(2)}) %collective-permute-start.1) | collective-permute-done | bytes 262176 | tf_op jit(solution)/shard_map/ppermute | solution.py:65
  26.6 6.8 %collective-permute-start.11 = (bf16[512,1024]{1,0:T(8,128)(2,1)S(1)}, bf16[512,1024]{1,0:T(8,128)(2,1)S(1)}, u32[]{:S(2)}, u32[]{:S(2)}) collective-permute-start(bf16[512,1024]{1,0:T(8,128)(2,1)S(1)} %bitcast.191), channel_id=1, source_target_pairs={{0,64},{64,128},{128,192},{1,65},{65,129},{129,193},{2,66},{66,130... | collective-permute-start | bytes 3145736 | tf_op jit(solution)/shard_map/ppermute | solution.py:30
  36.5 3.9 %collective-permute-start.2 = (bf16[512,512]{1,0:T(8,128)(2,1)S(1)}, bf16[512,512]{1,0:T(8,128)(2,1)}, u32[]{:S(2)}, u32[]{:S(2)}) collective-permute-start(bf16[512,512]{1,0:T(8,128)(2,1)S(1)} %slice_bitcast_fusion.1), channel_id=1, source_target_pairs={{0,64},{64,128},{128,192},{1,65},{65,129},{129,193},{2,66},{66,130... | collective-permute-start | bytes 1572872 | tf_op jit(solution)/shard_map/ppermute | solution.py:30
  40.4 2.7 collective-permute-start.3
  43.1 13.9 %collective-permute-done.11 = bf16[512,1024]{1,0:T(8,128)(2,1)S(1)} collective-permute-done((bf16[512,1024]{1,0:T(8,128)(2,1)S(1)}, bf16[512,1024]{1,0:T(8,128)(2,1)S(1)}, u32[]{:S(2)}, u32[]{:S(2)}) %collective-permute-start.11) | collective-permute-done | bytes 1048608 | tf_op jit(solution)/shard_map/ppermute | solution.py:30
  57.0 5.4 %collective-permute-start.13 = (bf16[512,1024]{1,0:T(8,128)(2,1)S(1)}, bf16[512,1024]{1,0:T(8,128)(2,1)}, u32[]{:S(2)}, u32[]{:S(2)}) collective-permute-start(bf16[512,1024]{1,0:T(8,128)(2,1)S(1)} %collective-permute-done.11), channel_id=1, source_target_pairs={{64,128},{128,192},{65,129},{129,193},{66,130},{130,194},{67,131},... | collective-permute-start | bytes 3145736 | tf_op jit(solution)/shard_map/ppermute | solution.py:35
  64.3 3.9 %collective-permute-done.2 = bf16[512,512]{1,0:T(8,128)(2,1)} collective-permute-done((bf16[512,512]{1,0:T(8,128)(2,1)S(1)}, bf16[512,512]{1,0:T(8,128)(2,1)}, u32[]{:S(2)}, u32[]{:S(2)}) %collective-permute-start.2) | collective-permute-done | bytes 524320 | tf_op jit(solution)/shard_map/ppermute | solution.py:30
  68.2 5.3 %collective-permute-start.4 = (bf16[512,512]{1,0:T(8,128)(2,1)}, bf16[512,512]{1,0:T(8,128)(2,1)}, u32[]{:S(2)}, u32[]{:S(2)}) collective-permute-start(bf16[512,512]{1,0:T(8,128)(2,1)} %collective-permute-done.2), channel_id=1, source_target_pairs={{64,128},{128,192},{65,129},{129,193},{66,130},{130,194},{67,131},... | collective-permute-start | bytes 1572872 | tf_op jit(solution)/shard_map/ppermute | solution.py:35
  77.4 23.7 %collective-permute-done.4 = bf16[512,512]{1,0:T(8,128)(2,1)} collective-permute-done((bf16[512,512]{1,0:T(8,128)(2,1)}, bf16[512,512]{1,0:T(8,128)(2,1)}, u32[]{:S(2)}, u32[]{:S(2)}) %collective-permute-start.4) | collective-permute-done | bytes 524320 | tf_op jit(solution)/shard_map/ppermute | solution.py:35
  101.8 3.4 %collective-permute-done.5 = bf16[512,512]{1,0:T(8,128)(2,1)} collective-permute-done((bf16[512,512]{1,0:T(8,128)(2,1)}, bf16[512,512]{1,0:T(8,128)(2,1)}, u32[]{:S(2)}, u32[]{:S(2)}) %collective-permute-start.5) | collective-permute-done | bytes 524320 | tf_op jit(solution)/shard_map/ppermute | solution.py:36
  109.2 2.3 collective-permute-start.16
  123.0 7.6 %collective-permute-start.10 = (f32[256,512]{1,0:T(8,128)}, f32[256,512]{1,0:T(8,128)}, u32[]{:S(2)}, u32[]{:S(2)}) collective-permute-start(f32[256,512]{1,0:T(8,128)} %get-tuple-element.11), channel_id=1, source_target_pairs={{0,48},{16,0},{32,16},{48,32},{1,49},{17,1},{33,17},{49,33},{2,50}... | collective-permute-start | bytes 1572872 | tf_op jit(solution)/shard_map/ppermute | solution.py:92
  130.6 2.5 fusion.9
  134.3 2.5 fusion.7
  136.9 3.8 %collective-permute-done.16 = bf16[512,1024]{1,0:T(8,128)(2,1)} collective-permute-done((bf16[512,1024]{1,0:T(8,128)(2,1)}, bf16[512,1024]{1,0:T(8,128)(2,1)}, u32[]{:S(2)}, u32[]{:S(2)}) %collective-permute-start.16) | collective-permute-done | bytes 1048608 | tf_op jit(solution)/shard_map/ppermute | solution.py:36
  140.7 3.2 %bitcast_add_fusion = f32[2,2,256,1024]{3,2,0,1:T(8,128)S(1)} fusion(f32[1024,2,2,256]{0,3,2,1:T(8,128)S(1)} %fusion.7, f32[2,2,256,1024]{3,2,1,0:T(8,128)S(1)} %fusion.9, f32[2,2,256,1024]{3,2,1,0:T(8,128)S(1)} %fusion.16, f32[2,2,256,1024]{3,2,1,0:T(8,128)S(1)} %fusion.11, bf16[512,1024]{1,0:T(8,128)(2,1)} %collective-permute-done.15, ...), kind=kOutput, calls=%fused_computation.5 | convolution fusion | flops 1078460416 | bytes 24117252 | tf_op jit(solution)/shard_map/chru,uk->hcrk/dot_general | solution.py:72
  148.1 7.1 %collective-permute-start.19 = (f32[256,1024]{1,0:T(8,128)}, f32[256,1024]{1,0:T(8,128)S(1)}, u32[]{:S(2)}, u32[]{:S(2)}) collective-permute-start(f32[256,1024]{1,0:T(8,128)} %get-tuple-element.8), channel_id=1, source_target_pairs={{0,48},{16,0},{32,16},{48,32},{1,49},{17,1},{33,17},{49,33},{2,50}... | collective-permute-start | bytes 3145736 | tf_op jit(solution)/shard_map/ppermute | solution.py:92
  161.1 55.7 %collective-permute-done.9 = f32[256,512]{1,0:T(8,128)} collective-permute-done((f32[256,512]{1,0:T(8,128)}, f32[256,512]{1,0:T(8,128)}, u32[]{:S(2)}, u32[]{:S(2)}) %collective-permute-start.9) | collective-permute-done | bytes 524320 | tf_op jit(solution)/shard_map/ppermute | solution.py:92
  216.9 7.7 %collective-permute-done.8 = f32[256,512]{1,0:T(8,128)} collective-permute-done((f32[256,512]{1,0:T(8,128)}, f32[256,512]{1,0:T(8,128)}, u32[]{:S(2)}, u32[]{:S(2)}) %collective-permute-start.8) | collective-permute-done | bytes 524320 | tf_op jit(solution)/shard_map/ppermute | solution.py:92
  228.4 3.1 %collective-permute-start.20 = (bf16[2,3,512]{2,0,1:T(2,128)(2,1)S(1)}, bf16[2,3,512]{2,0,1:T(2,128)(2,1)S(1)}, u32[]{:S(2)}, u32[]{:S(2)}) collective-permute-start(bf16[2,3,512]{2,0,1:T(2,128)(2,1)S(1)} %pad_maximum_fusion.2), channel_id=1, source_target_pairs={{0,16},{16,32},{32,48},{48,64},{64,80},{80,96},{96,112},{112,128},... | collective-permute-start | bytes 18440 | tf_op jit(solution)/shard_map/ppermute | solution.py:16
  231.6 4.5 %collective-permute-done.20 = bf16[2,3,512]{2,0,1:T(2,128)(2,1)S(1)} collective-permute-done((bf16[2,3,512]{2,0,1:T(2,128)(2,1)S(1)}, bf16[2,3,512]{2,0,1:T(2,128)(2,1)S(1)}, u32[]{:S(2)}, u32[]{:S(2)}) %collective-permute-start.20) | collective-permute-done | bytes 6176 | tf_op jit(solution)/shard_map/ppermute | solution.py:16
  250.7 4.5 %collective-permute-done.26 = f32[4,512,16]{1,2,0:T(8,128)S(1)} collective-permute-done((f32[4,512,16]{1,2,0:T(8,128)S(1)}, f32[4,512,16]{1,2,0:T(8,128)S(1)}, u32[]{:S(2)}, u32[]{:S(2)}) %collective-permute-start.26) | collective-permute-done | bytes 131104 | tf_op jit(solution)/shard_map/ppermute | solution.py:24
  256.5 10.1 %multiply_reduce_fusion.1 = f32[256,512]{1,0:T(8,128)S(1)} fusion(f32[512,16]{0,1:T(8,128)S(1)} %exponential_multiply_fusion, f32[512,16]{0,1:T(8,128)S(1)} %neg.8, f32[512,16]{0,1:T(8,128)S(1)} %copy-done.5, f32[512,16,256]{2,1,0:T(8,128)S(1)} %bitcast.190), kind=kOutput, calls=%fused_computation.4 | convolution fusion | flops 6452871168 | bytes 9011200 | tf_op jit(solution)/shard_map/dot_general | solution.py:128
  (91 shorter events, 60.5 us)
Async XLA Ops:
  6.5 105.0 %all-gather.3.cloned.1.call-start = ((), (), s32[]{:S(2)}) async-start(), calls=%async_computation | async-start | bytes 4718592 | tf_op jit(solution)/shard_map/all_gather | solution.py:67
  6.5 10.4 %collective-permute-start = (bf16[256,512]{1,0:T(8,128)(2,1)}, bf16[256,512]{1,0:T(8,128)(2,1)S(1)}, u32[]{:S(2)}, u32[]{:S(2)}) collective-permute-start(bf16[256,512]{1,0:T(8,128)(2,1)} %param.6), channel_id=1, source_target_pairs={{0,0},{1,16},{2,32},{3,48},{16,1},{17,17},{18,33},{19,49},{32,2},{... | collective-permute-start | bytes 786440 | tf_op jit(solution)/shard_map/ppermute | solution.py:64
  8.1 16.1 %collective-permute-start.1 = (bf16[256,512]{1,0:T(8,128)(2,1)}, bf16[256,512]{1,0:T(8,128)(2,1)S(1)}, u32[]{:S(2)}, u32[]{:S(2)}) collective-permute-start(bf16[256,512]{1,0:T(8,128)(2,1)} %param.6), channel_id=1, source_target_pairs={{0,2},{1,18},{2,34},{3,50},{16,3},{17,19},{18,35},{19,51},{32,0},{... | collective-permute-start | bytes 786440 | tf_op jit(solution)/shard_map/ppermute | solution.py:65
  26.6 30.3 %collective-permute-start.11 = (bf16[512,1024]{1,0:T(8,128)(2,1)S(1)}, bf16[512,1024]{1,0:T(8,128)(2,1)S(1)}, u32[]{:S(2)}, u32[]{:S(2)}) collective-permute-start(bf16[512,1024]{1,0:T(8,128)(2,1)S(1)} %bitcast.191), channel_id=1, source_target_pairs={{0,64},{64,128},{128,192},{1,65},{65,129},{129,193},{2,66},{66,130... | collective-permute-start | bytes 3145736 | tf_op jit(solution)/shard_map/ppermute | solution.py:30
  33.4 28.9 %collective-permute-start.12 = (bf16[512,1024]{1,0:T(8,128)(2,1)S(1)}, bf16[512,1024]{1,0:T(8,128)(2,1)}, u32[]{:S(2)}, u32[]{:S(2)}) collective-permute-start(bf16[512,1024]{1,0:T(8,128)(2,1)S(1)} %bitcast.192), channel_id=1, source_target_pairs={{64,0},{128,64},{192,128},{65,1},{129,65},{193,129},{66,2},{130,66... | collective-permute-start | bytes 3145736 | tf_op jit(solution)/shard_map/ppermute | solution.py:31
  36.5 31.8 %collective-permute-start.2 = (bf16[512,512]{1,0:T(8,128)(2,1)S(1)}, bf16[512,512]{1,0:T(8,128)(2,1)}, u32[]{:S(2)}, u32[]{:S(2)}) collective-permute-start(bf16[512,512]{1,0:T(8,128)(2,1)S(1)} %slice_bitcast_fusion.1), channel_id=1, source_target_pairs={{0,64},{64,128},{128,192},{1,65},{65,129},{129,193},{2,66},{66,130... | collective-permute-start | bytes 1572872 | tf_op jit(solution)/shard_map/ppermute | solution.py:30
  40.4 33.1 %collective-permute-start.3 = (bf16[512,512]{1,0:T(8,128)(2,1)S(1)}, bf16[512,512]{1,0:T(8,128)(2,1)}, u32[]{:S(2)}, u32[]{:S(2)}) collective-permute-start(bf16[512,512]{1,0:T(8,128)(2,1)S(1)} %slice_bitcast_fusion.1), channel_id=1, source_target_pairs={{64,0},{128,64},{192,128},{65,1},{129,65},{193,129},{66,2},{130,66... | collective-permute-start | bytes 1572872 | tf_op jit(solution)/shard_map/ppermute | solution.py:31
  57.0 50.4 %collective-permute-start.13 = (bf16[512,1024]{1,0:T(8,128)(2,1)S(1)}, bf16[512,1024]{1,0:T(8,128)(2,1)}, u32[]{:S(2)}, u32[]{:S(2)}) collective-permute-start(bf16[512,1024]{1,0:T(8,128)(2,1)S(1)} %collective-permute-done.11), channel_id=1, source_target_pairs={{64,128},{128,192},{65,129},{129,193},{66,130},{130,194},{67,131},... | collective-permute-start | bytes 3145736 | tf_op jit(solution)/shard_map/ppermute | solution.py:35
  62.4 46.8 %collective-permute-start.14 = (bf16[512,1024]{1,0:T(8,128)(2,1)}, bf16[512,1024]{1,0:T(8,128)(2,1)}, u32[]{:S(2)}, u32[]{:S(2)}) collective-permute-start(bf16[512,1024]{1,0:T(8,128)(2,1)} %collective-permute-done.12), channel_id=1, source_target_pairs={{64,0},{128,64},{65,1},{129,65},{66,2},{130,66},{67,3},{131,67},{6... | collective-permute-start | bytes 3145736 | tf_op jit(solution)/shard_map/ppermute | solution.py:36
  68.2 32.9 %collective-permute-start.4 = (bf16[512,512]{1,0:T(8,128)(2,1)}, bf16[512,512]{1,0:T(8,128)(2,1)}, u32[]{:S(2)}, u32[]{:S(2)}) collective-permute-start(bf16[512,512]{1,0:T(8,128)(2,1)} %collective-permute-done.2), channel_id=1, source_target_pairs={{64,128},{128,192},{65,129},{129,193},{66,130},{130,194},{67,131},... | collective-permute-start | bytes 1572872 | tf_op jit(solution)/shard_map/ppermute | solution.py:35
  73.5 31.7 %collective-permute-start.5 = (bf16[512,512]{1,0:T(8,128)(2,1)}, bf16[512,512]{1,0:T(8,128)(2,1)}, u32[]{:S(2)}, u32[]{:S(2)}) collective-permute-start(bf16[512,512]{1,0:T(8,128)(2,1)} %collective-permute-done.3), channel_id=1, source_target_pairs={{64,0},{128,64},{65,1},{129,65},{66,2},{130,66},{67,3},{131,67},{6... | collective-permute-start | bytes 1572872 | tf_op jit(solution)/shard_map/ppermute | solution.py:36
  101.1 19.6 %collective-permute-start.6 = (bf16[512,512]{1,0:T(8,128)(2,1)}, bf16[512,512]{1,0:T(8,128)(2,1)S(1)}, u32[]{:S(2)}, u32[]{:S(2)}) collective-permute-start(bf16[512,512]{1,0:T(8,128)(2,1)} %collective-permute-done.4), channel_id=1, source_target_pairs={{128,192},{129,193},{130,194},{131,195},{132,196},{133,197},{134,1... | collective-permute-start | bytes 1572872 | tf_op jit(solution)/shard_map/ppermute | solution.py:35
  105.2 15.5 %collective-permute-start.7 = (bf16[512,512]{1,0:T(8,128)(2,1)}, bf16[512,512]{1,0:T(8,128)(2,1)S(1)}, u32[]{:S(2)}, u32[]{:S(2)}) collective-permute-start(bf16[512,512]{1,0:T(8,128)(2,1)} %collective-permute-done.5), channel_id=1, source_target_pairs={{64,0},{65,1},{66,2},{67,3},{68,4},{69,5},{70,6},{71,7},{72,8},{73... | collective-permute-start | bytes 1572872 | tf_op jit(solution)/shard_map/ppermute | solution.py:36
  107.4 29.4 %collective-permute-start.15 = (bf16[512,1024]{1,0:T(8,128)(2,1)}, bf16[512,1024]{1,0:T(8,128)(2,1)}, u32[]{:S(2)}, u32[]{:S(2)}) collective-permute-start(bf16[512,1024]{1,0:T(8,128)(2,1)} %collective-permute-done.13), channel_id=1, source_target_pairs={{128,192},{129,193},{130,194},{131,195},{132,196},{133,197},{134,1... | collective-permute-start | bytes 3145736 | tf_op jit(solution)/shard_map/ppermute | solution.py:35
  109.2 31.5 %collective-permute-start.16 = (bf16[512,1024]{1,0:T(8,128)(2,1)}, bf16[512,1024]{1,0:T(8,128)(2,1)}, u32[]{:S(2)}, u32[]{:S(2)}) collective-permute-start(bf16[512,1024]{1,0:T(8,128)(2,1)} %collective-permute-done.14), channel_id=1, source_target_pairs={{64,0},{65,1},{66,2},{67,3},{68,4},{69,5},{70,6},{71,7},{72,8},{73... | collective-permute-start | bytes 3145736 | tf_op jit(solution)/shard_map/ppermute | solution.py:36
  123.0 36.0 %collective-permute-start.10 = (f32[256,512]{1,0:T(8,128)}, f32[256,512]{1,0:T(8,128)}, u32[]{:S(2)}, u32[]{:S(2)}) collective-permute-start(f32[256,512]{1,0:T(8,128)} %get-tuple-element.11), channel_id=1, source_target_pairs={{0,48},{16,0},{32,16},{48,32},{1,49},{17,1},{33,17},{49,33},{2,50}... | collective-permute-start | bytes 1572872 | tf_op jit(solution)/shard_map/ppermute | solution.py:92
  148.1 78.0 %collective-permute-start.19 = (f32[256,1024]{1,0:T(8,128)}, f32[256,1024]{1,0:T(8,128)S(1)}, u32[]{:S(2)}, u32[]{:S(2)}) collective-permute-start(f32[256,1024]{1,0:T(8,128)} %get-tuple-element.8), channel_id=1, source_target_pairs={{0,48},{16,0},{32,16},{48,32},{1,49},{17,1},{33,17},{49,33},{2,50}... | collective-permute-start | bytes 3145736 | tf_op jit(solution)/shard_map/ppermute | solution.py:92
  155.2 70.9 %collective-permute-start.18 = (f32[256,1024]{1,0:T(8,128)}, f32[256,1024]{1,0:T(8,128)}, u32[]{:S(2)}, u32[]{:S(2)}) collective-permute-start(f32[256,1024]{1,0:T(8,128)} %get-tuple-element.9), channel_id=1, source_target_pairs={{0,32},{16,48},{32,0},{48,16},{1,33},{17,49},{33,1},{49,17},{2,34}... | collective-permute-start | bytes 3145736 | tf_op jit(solution)/shard_map/ppermute | solution.py:92
  157.0 69.2 %collective-permute-start.17 = (f32[256,1024]{1,0:T(8,128)}, f32[256,1024]{1,0:T(8,128)}, u32[]{:S(2)}, u32[]{:S(2)}) collective-permute-start(f32[256,1024]{1,0:T(8,128)} %get-tuple-element.7), channel_id=1, source_target_pairs={{0,16},{16,32},{32,48},{48,0},{1,17},{17,33},{33,49},{49,1},{2,18}... | collective-permute-start | bytes 3145736 | tf_op jit(solution)/shard_map/ppermute | solution.py:92
  158.4 58.5 %collective-permute-start.9 = (f32[256,512]{1,0:T(8,128)}, f32[256,512]{1,0:T(8,128)}, u32[]{:S(2)}, u32[]{:S(2)}) collective-permute-start(f32[256,512]{1,0:T(8,128)} %get-tuple-element.12), channel_id=1, source_target_pairs={{0,32},{16,48},{32,0},{48,16},{1,33},{17,49},{33,1},{49,17},{2,34}... | collective-permute-start | bytes 1572872 | tf_op jit(solution)/shard_map/ppermute | solution.py:92
  159.0 65.6 %collective-permute-start.8 = (f32[256,512]{1,0:T(8,128)}, f32[256,512]{1,0:T(8,128)}, u32[]{:S(2)}, u32[]{:S(2)}) collective-permute-start(f32[256,512]{1,0:T(8,128)} %get-tuple-element.10), channel_id=1, source_target_pairs={{0,16},{16,32},{32,48},{48,0},{1,17},{17,33},{33,49},{49,1},{2,18}... | collective-permute-start | bytes 1572872 | tf_op jit(solution)/shard_map/ppermute | solution.py:92
  245.3 9.9 %collective-permute-start.26 = (f32[4,512,16]{1,2,0:T(8,128)S(1)}, f32[4,512,16]{1,2,0:T(8,128)S(1)}, u32[]{:S(2)}, u32[]{:S(2)}) collective-permute-start(f32[4,512,16]{1,2,0:T(8,128)S(1)} %get-tuple-element.20), channel_id=1, source_target_pairs={{0,192},{64,0},{128,64},{192,128},{1,193},{65,1},{129,65},{193,129... | collective-permute-start | bytes 393224 | tf_op jit(solution)/shard_map/ppermute | solution.py:24
  247.6 7.7 %collective-permute-start.25 = (f32[4,512,16]{1,2,0:T(8,128)S(1)}, f32[4,512,16]{1,2,0:T(8,128)}, u32[]{:S(2)}, u32[]{:S(2)}) collective-permute-start(f32[4,512,16]{1,2,0:T(8,128)S(1)} %get-tuple-element.20), channel_id=1, source_target_pairs={{0,128},{64,192},{128,0},{192,64},{1,129},{65,193},{129,1},{193,65... | collective-permute-start | bytes 393224 | tf_op jit(solution)/shard_map/ppermute | solution.py:24
  247.6 7.7 %collective-permute-start.24 = (f32[4,512,16]{1,2,0:T(8,128)S(1)}, f32[4,512,16]{1,2,0:T(8,128)}, u32[]{:S(2)}, u32[]{:S(2)}) collective-permute-start(f32[4,512,16]{1,2,0:T(8,128)S(1)} %get-tuple-element.20), channel_id=1, source_target_pairs={{0,64},{64,128},{128,192},{192,0},{1,65},{65,129},{129,193},{193,1... | collective-permute-start | bytes 393224 | tf_op jit(solution)/shard_map/ppermute | solution.py:24
  (10 other events, 133.6 us)
Sparse Core Ops, SparseCore 0:
  25.3 40.9 all-gather.2

commit v9 on v7

--- a/solution.py
+++ b/solution.py
@@ -123,12 +123,19 @@
     lower_mask = (jnp.arange(tok_rows)[:, None] >= jnp.arange(tok_rows)[None, :]).astype(
         jnp.float32
     )
-    running_sum = jnp.dot(lower_mask, scaled, precision=exact_mode).reshape(
-        tok_rows, width_local, mode_count
-    )
+    mask_b = lower_mask.astype(jnp.bfloat16)
+    running_sum = jnp.zeros(scaled.shape, jnp.float32)
+    rest = scaled
+    for _ in range(3):
+        part = rest.astype(jnp.bfloat16)
+        running_sum = running_sum + jnp.dot(mask_b, part, preferred_element_type=jnp.float32)
+        rest = rest - part.astype(jnp.float32)
+    running_sum = running_sum.reshape(tok_rows, width_local, mode_count)
     shrink = jnp.exp(-decay_rate[None, :, :] * position[:, None, None])
+    weighted = residue[None] * shrink
+    inside = jnp.sum(weighted * running_sum, axis=2)
     entering = (incoming * jnp.exp(-decay_rate))[None]
-    convolved = jnp.sum(residue[None] * shrink * (running_sum + entering), axis=2)
+    convolved = inside + jnp.sum(weighted * entering, axis=2)
     long_mix = convolved + skip_gain[None, :] * gated_wide
     return (query_gate * long_mix).astype(jnp.bfloat16)
 

time: 253 us -> 284 us (1.12)
  local copies, waits for them, and re-layouts: 2.63 us -> 32.4 us
  waiting for transfers between devices: 121 us -> 96.4 us
  other arithmetic: 7.38 us -> 19.4 us
  matrix products: 25.9 us -> 37 us
  starting transfers between devices: 80.2 us -> 83.3 us
    dynamic_slice x0 -> x14, local copies, waits for them, and re-layouts: none -> 16.6 us  [the longest x9 11.5 us: block(): lax.dynamic_index_in_dim(partial, (me_x + k) % across, axis=0, keepdims=F...]
    ppermute x6, waiting for transfers between devices: 33.6 us -> 17.3 us  [line_gather(): lax.ppermute(near_a, axis, [(i + 1, i) for i in range(0, size - d)])]
    add x0 -> x1, local copies, waits for them, and re-layouts: none -> 9.13 us  [block(): running_sum + jnp.dot(mask_b, part, preferred_element_type=jnp.float32)]
    dot_general x15, matrix products: 15.8 us -> 24.2 us  [contribution(): jnp.einsum('chru,uk->hcrk', taken, weight, preferred_element_type=jnp.flo...]
    reduce_sum x0 -> x1, other arithmetic: none -> 7.53 us  [block(): convolved = inside + jnp.sum(weighted * entering, axis=2)]
    ppermute x6, waiting for transfers between devices: 7.4 us -> 0.02 us  [ring_sends(): received.append(lax.ppermute(pieces(k, position), axis, route))]
    ppermute x6, starting transfers between devices: 12.9 us -> 17.4 us  [line_gather(): lax.ppermute(near_b, axis, [(i, i + 1) for i in range(d - 1, size - 1)])]
    ppermute x9, starting transfers between devices: 14.9 us -> 10.8 us  [block(): total = total + lax.ppermute(piece, 'x', route)]
  transfers between devices with their start and end apart: 37 -> 37, of which waited for: 21 -> 11; matrix products, arithmetic and copies ran while one was open for 8% -> 24% of each run, Pallas kernels for 0% -> 0%
where the time goes in v9:
time: 284 us; the launch traced here: 283 us
  waiting for transfers between devices  96.4 us (34%)
  starting transfers between devices  83.3 us (29%)
  matrix products  37 us (13%)
  local copies, waits for them, and re-layouts  32.4 us (11%)
  other arithmetic  19.4 us (7%)
  between operations  14.2 us (5%)
    ppermute x9, waiting for transfers between devices, block(): total = total + lax.ppermute(piece, 'x', route)  41.9 us
    dot_general x15, matrix products, contribution(): jnp.einsum('chru,uk->hcrk', taken, weight, preferred_element_type=jnp.flo...  24.2 us
    all_gather x1, waiting for transfers between devices, block(): gathered = lax.all_gather(both, ('y', 'c'), axis=0, tiled=False)  21.2 us
    ppermute x6, starting transfers between devices, line_gather(): lax.ppermute(near_b, axis, [(i, i + 1) for i in range(d - 1, size - 1)])  17.4 us
    ppermute x6, waiting for transfers between devices, line_gather(): lax.ppermute(near_a, axis, [(i + 1, i) for i in range(0, size - d)])  17.3 us
    ppermute x3, starting transfers between devices, line_gather(): near_b = lax.ppermute(piece, axis, [(i, i + 1) for i in range(size - 1)])  14.6 us
    ppermute x6, starting transfers between devices, line_gather(): lax.ppermute(near_a, axis, [(i + 1, i) for i in range(0, size - d)])  14.5 us
    dynamic_slice x9, local copies, waits for them, and re-layouts, block(): lax.dynamic_index_in_dim(partial, (me_x + k) % across, axis=0, keepdims=F...  11.5 us
  transfers between devices with their start and end apart: 37, of which 11 were waited for; matrix products, arithmetic and copies ran while one was open for 24% of the time, Pallas kernels for 0%

profile of v9, /device:TPU:32, one launch (start us, length us, event | category | flops | bytes accessed | tf_op | source)
XLA Modules:
  0.0 282.6 jit_solution(18350449134330226936)
XLA Ops:
  8.3 8.8 %collective-permute-start.1 = (bf16[256,512]{1,0:T(8,128)(2,1)}, bf16[256,512]{1,0:T(8,128)(2,1)S(1)}, u32[]{:S(2)}, u32[]{:S(2)}) collective-permute-start(bf16[256,512]{1,0:T(8,128)(2,1)} %param.6), channel_id=1, source_target_pairs={{0,2},{1,18},{2,34},{3,50},{16,3},{17,19},{18,35},{19,51},{32,0},{... | collective-permute-start | bytes 786440 | tf_op jit(solution)/shard_map/ppermute | solution.py:64
  17.0 7.3 %collective-permute-done.1 = bf16[256,512]{1,0:T(8,128)(2,1)S(1)} collective-permute-done((bf16[256,512]{1,0:T(8,128)(2,1)}, bf16[256,512]{1,0:T(8,128)(2,1)S(1)}, u32[]{:S(2)}, u32[]{:S(2)}) %collective-permute-start.1) | collective-permute-done | bytes 262176 | tf_op jit(solution)/shard_map/ppermute | solution.py:64
  26.6 6.8 %collective-permute-start.2 = (bf16[512,512]{1,0:T(8,128)(2,1)}, bf16[512,512]{1,0:T(8,128)(2,1)}, u32[]{:S(2)}, u32[]{:S(2)}) collective-permute-start(bf16[512,512]{1,0:T(8,128)(2,1)} %get-tuple-element.21), channel_id=1, source_target_pairs={{0,64},{64,128},{128,192},{1,65},{65,129},{129,193},{2,66},{66,130... | collective-permute-start | bytes 1572872 | tf_op jit(solution)/shard_map/ppermute | solution.py:30
  35.3 3.9 %collective-permute-start.11 = (bf16[512,512]{1,0:T(8,128)(2,1)}, bf16[512,512]{1,0:T(8,128)(2,1)S(1)}, u32[]{:S(2)}, u32[]{:S(2)}) collective-permute-start(bf16[512,512]{1,0:T(8,128)(2,1)} %get-tuple-element.23), channel_id=1, source_target_pairs={{0,64},{64,128},{128,192},{1,65},{65,129},{129,193},{2,66},{66,130... | collective-permute-start | bytes 1572872 | tf_op jit(solution)/shard_map/ppermute | solution.py:30
  41.2 3.9 %collective-permute-start.20 = (bf16[512,512]{1,0:T(8,128)(2,1)}, bf16[512,512]{1,0:T(8,128)(2,1)S(1)}, u32[]{:S(2)}, u32[]{:S(2)}) collective-permute-start(bf16[512,512]{1,0:T(8,128)(2,1)} %get-tuple-element.22), channel_id=1, source_target_pairs={{0,64},{64,128},{128,192},{1,65},{65,129},{129,193},{2,66},{66,130... | collective-permute-start | bytes 1572872 | tf_op jit(solution)/shard_map/ppermute | solution.py:30
  45.2 21.2 %all-gather.3.cloned.1.call-done = bf16[16,256,512]{2,1,0:T(8,128)(2,1)} async-done(((bf16[2,256,512]{2,1,0:T(8,128)(2,1)}), bf16[16,256,512]{2,1,0:T(8,128)(2,1)}) %all-gather.3.cloned.1.call-update) | async-done | bytes 4194320 | tf_op jit(solution)/shard_map/all_gather | solution.py:66
  73.0 3.5 %collective-permute-start.4 = (bf16[512,512]{1,0:T(8,128)(2,1)}, bf16[512,512]{1,0:T(8,128)(2,1)S(1)}, u32[]{:S(2)}, u32[]{:S(2)}) collective-permute-start(bf16[512,512]{1,0:T(8,128)(2,1)} %collective-permute-done.2), channel_id=1, source_target_pairs={{64,128},{128,192},{65,129},{129,193},{66,130},{130,194},{67,131},... | collective-permute-start | bytes 1572872 | tf_op jit(solution)/shard_map/ppermute | solution.py:35
  78.4 4.7 %collective-permute-start.13 = (bf16[512,512]{1,0:T(8,128)(2,1)S(1)}, bf16[512,512]{1,0:T(8,128)(2,1)}, u32[]{:S(2)}, u32[]{:S(2)}) collective-permute-start(bf16[512,512]{1,0:T(8,128)(2,1)S(1)} %collective-permute-done.11), channel_id=1, source_target_pairs={{64,128},{128,192},{65,129},{129,193},{66,130},{130,194},{67,131},... | collective-permute-start | bytes 1572872 | tf_op jit(solution)/shard_map/ppermute | solution.py:35
  83.2 3.1 %fusion.30 = f32[2,2,256,512]{3,2,1,0:T(8,128)} fusion(bf16[4,2,2,256,512]{4,3,2,1,0:T(8,128)(2,1)S(1)} %bitcast.247, s32[]{:T(128)S(6)} %select_n.153, bf16[512,3,512]{2,0,1:T(8,128)(2,1)} %param.7), kind=kOutput, calls=%fused_computation.48 | convolution fusion | flops 536870912 | bytes 3670020 | tf_op jit(solution)/shard_map/chru,uk->hcrk/dot_general | solution.py:71
  90.0 5.5 %collective-permute-start.22 = (bf16[512,512]{1,0:T(8,128)(2,1)S(1)}, bf16[512,512]{1,0:T(8,128)(2,1)}, u32[]{:S(2)}, u32[]{:S(2)}) collective-permute-start(bf16[512,512]{1,0:T(8,128)(2,1)S(1)} %collective-permute-done.20), channel_id=1, source_target_pairs={{64,128},{128,192},{65,129},{129,193},{66,130},{130,194},{67,131},... | collective-permute-start | bytes 1572872 | tf_op jit(solution)/shard_map/ppermute | solution.py:35
  104.3 5.7 %collective-permute-done.14 = bf16[512,512]{1,0:T(8,128)(2,1)} collective-permute-done((bf16[512,512]{1,0:T(8,128)(2,1)}, bf16[512,512]{1,0:T(8,128)(2,1)}, u32[]{:S(2)}, u32[]{:S(2)}) %collective-permute-start.14) | collective-permute-done | bytes 524320 | tf_op jit(solution)/shard_map/ppermute | solution.py:36
  111.5 3.2 %collective-permute-start.16 = (bf16[512,512]{1,0:T(8,128)(2,1)}, bf16[512,512]{1,0:T(8,128)(2,1)}, u32[]{:S(2)}, u32[]{:S(2)}) collective-permute-start(bf16[512,512]{1,0:T(8,128)(2,1)} %collective-permute-done.14), channel_id=1, source_target_pairs={{64,0},{65,1},{66,2},{67,3},{68,4},{69,5},{70,6},{71,7},{72,8},{73... | collective-permute-start | bytes 1572872 | tf_op jit(solution)/shard_map/ppermute | solution.py:36
  114.7 5.8 %collective-permute-done.23 = bf16[512,512]{1,0:T(8,128)(2,1)} collective-permute-done((bf16[512,512]{1,0:T(8,128)(2,1)S(1)}, bf16[512,512]{1,0:T(8,128)(2,1)}, u32[]{:S(2)}, u32[]{:S(2)}) %collective-permute-start.23) | collective-permute-done | bytes 524320 | tf_op jit(solution)/shard_map/ppermute | solution.py:36
  122.0 3.9 %collective-permute-start.25 = (bf16[512,512]{1,0:T(8,128)(2,1)}, bf16[512,512]{1,0:T(8,128)(2,1)}, u32[]{:S(2)}, u32[]{:S(2)}) collective-permute-start(bf16[512,512]{1,0:T(8,128)(2,1)} %collective-permute-done.23), channel_id=1, source_target_pairs={{64,0},{65,1},{66,2},{67,3},{68,4},{69,5},{70,6},{71,7},{72,8},{73... | collective-permute-start | bytes 1572872 | tf_op jit(solution)/shard_map/ppermute | solution.py:36
  125.9 4.5 %collective-permute-done.7 = bf16[512,512]{1,0:T(8,128)(2,1)S(1)} collective-permute-done((bf16[512,512]{1,0:T(8,128)(2,1)S(1)}, bf16[512,512]{1,0:T(8,128)(2,1)S(1)}, u32[]{:S(2)}, u32[]{:S(2)}) %collective-permute-start.7) | collective-permute-done | bytes 524320 | tf_op jit(solution)/shard_map/ppermute | solution.py:36
  176.8 21.6 %collective-permute-done.17 = f32[256,512]{0,1:T(8,128)} collective-permute-done((f32[256,512]{0,1:T(8,128)}, f32[256,512]{0,1:T(8,128)}, u32[]{:S(2)}, u32[]{:S(2)}) %collective-permute-start.17) | collective-permute-done | bytes 524320 | tf_op jit(solution)/shard_map/ppermute | solution.py:91
  201.4 17.2 %collective-permute-done.26 = f32[256,512]{0,1:T(8,128)S(1)} collective-permute-done((f32[256,512]{0,1:T(8,128)}, f32[256,512]{0,1:T(8,128)S(1)}, u32[]{:S(2)}, u32[]{:S(2)}) %collective-permute-start.26) | collective-permute-done | bytes 524320 | tf_op jit(solution)/shard_map/ppermute | solution.py:91
  222.9 7.8 %collective-permute-done.29 = bf16[2,3,512]{0,2,1:T(8,128)(2,1)S(1)} collective-permute-done((bf16[2,3,512]{0,2,1:T(8,128)(2,1)S(1)}, bf16[2,3,512]{0,2,1:T(8,128)(2,1)S(1)}, u32[]{:S(2)}, u32[]{:S(2)}) %collective-permute-start.29) | collective-permute-done | bytes 6176 | tf_op jit(solution)/shard_map/ppermute | solution.py:16
  233.7 5.6 %fusion = f32[512,1,16]{2,1,0:T(1,128)S(1)} fusion(f32[256]{0:T(256)S(1)} %copy-done.22, f32[512,16]{1,0:T(8,128)S(1)} %copy.37, bf16[256,512,1]{0,1,2:T(8,128)(2,1)S(1)} %bitcast.262), kind=kOutput, calls=%fused_computation.4 | convolution fusion | flops 27262976 | bytes 328704 | tf_op jit(solution)/shard_map/jc,jcr->cr/dot_general | solution.py:109
  240.0 3.2 %collective-permute-start.32 = (f32[512,16]{0,1:T(8,128)}, f32[512,16]{0,1:T(8,128)}, u32[]{:S(2)}, u32[]{:S(2)}) collective-permute-start(f32[512,16]{0,1:T(8,128)} %bitcast.76), channel_id=1, source_target_pairs={{0,48},{16,0},{32,16},{48,32},{1,49},{17,1},{33,17},{49,33},{2,50}... | collective-permute-start | bytes 98312 | tf_op jit(solution)/shard_map/ppermute | solution.py:24
  249.2 3.8 %collective-permute-start.34 = (f32[4,512,16]{1,2,0:T(8,128)S(1)}, f32[4,512,16]{1,2,0:T(8,128)S(1)}, u32[]{:S(2)}, u32[]{:S(2)}) collective-permute-start(f32[4,512,16]{1,2,0:T(8,128)S(1)} %get-tuple-element.30), channel_id=1, source_target_pairs={{0,128},{64,192},{128,0},{192,64},{1,129},{65,193},{129,1},{193,65... | collective-permute-start | bytes 393224 | tf_op jit(solution)/shard_map/ppermute | solution.py:24
  253.0 4.6 %convolution_add_fusion = f32[256,8192]{1,0:T(8,128)} fusion(f32[256,8192]{1,0:T(8,128)S(1)} %convolution_add_fusion.1, bf16[256,8192]{0,1:T(8,128)(2,1)S(1)} %get-tuple-element.24), kind=kOutput, calls=%fused_computation | convolution fusion | flops 1076035584 | bytes 20971520 | tf_op jit(solution)/shard_map/dot_general | solution.py:131
  257.6 9.1 %copy.39 = f32[256,8192]{0,1:T(8,128)} copy(f32[256,8192]{1,0:T(8,128)} %convolution_add_fusion) | data formatting | bytes 16777216 | tf_op jit(solution)/shard_map/add | solution.py:131
  267.2 7.5 %multiply_reduce_fusion = (f32[256,512]{0,1:T(8,128)S(1)}, f32[256,512]{0,1:T(8,128)S(1)}) fusion(f32[512,16]{1,0:T(8,128)S(1)} %copy.40, f32[512,16]{1,0:T(8,128)S(1)} %copy-done.8, f32[512,16]{1,0:T(8,128)S(1)} %copy-done.9, f32[256,8192]{0,1:T(8,128)} %copy.39), kind=kLoop, calls=%fused_computation.3 | loop fusion | flops 12320768 | bytes 9535488 | tf_op jit(solution)/shard_map/reduce_sum | solution.py:138
  (164 shorter events, 95.9 us)
Async XLA Ops:
  6.5 59.9 %all-gather.3.cloned.1.call-start = ((), (), s32[]{:S(2)}) async-start(), calls=%async_computation | async-start | bytes 4718592 | tf_op jit(solution)/shard_map/all_gather | solution.py:66
  26.6 44.0 %collective-permute-start.2 = (bf16[512,512]{1,0:T(8,128)(2,1)}, bf16[512,512]{1,0:T(8,128)(2,1)}, u32[]{:S(2)}, u32[]{:S(2)}) collective-permute-start(bf16[512,512]{1,0:T(8,128)(2,1)} %get-tuple-element.21), channel_id=1, source_target_pairs={{0,64},{64,128},{128,192},{1,65},{65,129},{129,193},{2,66},{66,130... | collective-permute-start | bytes 1572872 | tf_op jit(solution)/shard_map/ppermute | solution.py:30
  33.4 39.6 %collective-permute-start.3 = (bf16[512,512]{1,0:T(8,128)(2,1)}, bf16[512,512]{1,0:T(8,128)(2,1)}, u32[]{:S(2)}, u32[]{:S(2)}) collective-permute-start(bf16[512,512]{1,0:T(8,128)(2,1)} %get-tuple-element.21), channel_id=1, source_target_pairs={{64,0},{128,64},{192,128},{65,1},{129,65},{193,129},{66,2},{130,66... | collective-permute-start | bytes 1572872 | tf_op jit(solution)/shard_map/ppermute | solution.py:31
  35.3 41.2 %collective-permute-start.11 = (bf16[512,512]{1,0:T(8,128)(2,1)}, bf16[512,512]{1,0:T(8,128)(2,1)S(1)}, u32[]{:S(2)}, u32[]{:S(2)}) collective-permute-start(bf16[512,512]{1,0:T(8,128)(2,1)} %get-tuple-element.23), channel_id=1, source_target_pairs={{0,64},{64,128},{128,192},{1,65},{65,129},{129,193},{2,66},{66,130... | collective-permute-start | bytes 1572872 | tf_op jit(solution)/shard_map/ppermute | solution.py:30
  39.2 39.2 %collective-permute-start.12 = (bf16[512,512]{1,0:T(8,128)(2,1)}, bf16[512,512]{1,0:T(8,128)(2,1)}, u32[]{:S(2)}, u32[]{:S(2)}) collective-permute-start(bf16[512,512]{1,0:T(8,128)(2,1)} %get-tuple-element.23), channel_id=1, source_target_pairs={{64,0},{128,64},{192,128},{65,1},{129,65},{193,129},{66,2},{130,66... | collective-permute-start | bytes 1572872 | tf_op jit(solution)/shard_map/ppermute | solution.py:31
  41.2 46.9 %collective-permute-start.20 = (bf16[512,512]{1,0:T(8,128)(2,1)}, bf16[512,512]{1,0:T(8,128)(2,1)S(1)}, u32[]{:S(2)}, u32[]{:S(2)}) collective-permute-start(bf16[512,512]{1,0:T(8,128)(2,1)} %get-tuple-element.22), channel_id=1, source_target_pairs={{0,64},{64,128},{128,192},{1,65},{65,129},{129,193},{2,66},{66,130... | collective-permute-start | bytes 1572872 | tf_op jit(solution)/shard_map/ppermute | solution.py:30
  73.0 22.6 %collective-permute-start.4 = (bf16[512,512]{1,0:T(8,128)(2,1)}, bf16[512,512]{1,0:T(8,128)(2,1)S(1)}, u32[]{:S(2)}, u32[]{:S(2)}) collective-permute-start(bf16[512,512]{1,0:T(8,128)(2,1)} %collective-permute-done.2), channel_id=1, source_target_pairs={{64,128},{128,192},{65,129},{129,193},{66,130},{130,194},{67,131},... | collective-permute-start | bytes 1572872 | tf_op jit(solution)/shard_map/ppermute | solution.py:35
  76.5 22.2 %collective-permute-start.5 = (bf16[512,512]{1,0:T(8,128)(2,1)}, bf16[512,512]{1,0:T(8,128)(2,1)S(1)}, u32[]{:S(2)}, u32[]{:S(2)}) collective-permute-start(bf16[512,512]{1,0:T(8,128)(2,1)} %collective-permute-done.3), channel_id=1, source_target_pairs={{64,0},{128,64},{65,1},{129,65},{66,2},{130,66},{67,3},{131,67},{6... | collective-permute-start | bytes 1572872 | tf_op jit(solution)/shard_map/ppermute | solution.py:36
  88.1 22.0 %collective-permute-start.14 = (bf16[512,512]{1,0:T(8,128)(2,1)}, bf16[512,512]{1,0:T(8,128)(2,1)}, u32[]{:S(2)}, u32[]{:S(2)}) collective-permute-start(bf16[512,512]{1,0:T(8,128)(2,1)} %collective-permute-done.12), channel_id=1, source_target_pairs={{64,0},{128,64},{65,1},{129,65},{66,2},{130,66},{67,3},{131,67},{6... | collective-permute-start | bytes 1572872 | tf_op jit(solution)/shard_map/ppermute | solution.py:36
  95.6 25.0 %collective-permute-start.23 = (bf16[512,512]{1,0:T(8,128)(2,1)S(1)}, bf16[512,512]{1,0:T(8,128)(2,1)}, u32[]{:S(2)}, u32[]{:S(2)}) collective-permute-start(bf16[512,512]{1,0:T(8,128)(2,1)S(1)} %collective-permute-done.21), channel_id=1, source_target_pairs={{64,0},{128,64},{65,1},{129,65},{66,2},{130,66},{67,3},{131,67},{6... | collective-permute-start | bytes 1572872 | tf_op jit(solution)/shard_map/ppermute | solution.py:36
  98.7 23.3 %collective-permute-start.6 = (bf16[512,512]{1,0:T(8,128)(2,1)S(1)}, bf16[512,512]{1,0:T(8,128)(2,1)S(1)}, u32[]{:S(2)}, u32[]{:S(2)}) collective-permute-start(bf16[512,512]{1,0:T(8,128)(2,1)S(1)} %collective-permute-done.4), channel_id=1, source_target_pairs={{128,192},{129,193},{130,194},{131,195},{132,196},{133,197},{134,1... | collective-permute-start | bytes 1572872 | tf_op jit(solution)/shard_map/ppermute | solution.py:35
  100.2 30.2 %collective-permute-start.7 = (bf16[512,512]{1,0:T(8,128)(2,1)S(1)}, bf16[512,512]{1,0:T(8,128)(2,1)S(1)}, u32[]{:S(2)}, u32[]{:S(2)}) collective-permute-start(bf16[512,512]{1,0:T(8,128)(2,1)S(1)} %collective-permute-done.5), channel_id=1, source_target_pairs={{64,0},{65,1},{66,2},{67,3},{68,4},{69,5},{70,6},{71,7},{72,8},{73... | collective-permute-start | bytes 1572872 | tf_op jit(solution)/shard_map/ppermute | solution.py:36
  110.1 38.5 %collective-permute-start.15 = (bf16[512,512]{1,0:T(8,128)(2,1)}, bf16[512,512]{1,0:T(8,128)(2,1)}, u32[]{:S(2)}, u32[]{:S(2)}) collective-permute-start(bf16[512,512]{1,0:T(8,128)(2,1)} %collective-permute-done.13), channel_id=1, source_target_pairs={{128,192},{129,193},{130,194},{131,195},{132,196},{133,197},{134,1... | collective-permute-start | bytes 1572872 | tf_op jit(solution)/shard_map/ppermute | solution.py:35
  111.5 37.3 %collective-permute-start.16 = (bf16[512,512]{1,0:T(8,128)(2,1)}, bf16[512,512]{1,0:T(8,128)(2,1)}, u32[]{:S(2)}, u32[]{:S(2)}) collective-permute-start(bf16[512,512]{1,0:T(8,128)(2,1)} %collective-permute-done.14), channel_id=1, source_target_pairs={{64,0},{65,1},{66,2},{67,3},{68,4},{69,5},{70,6},{71,7},{72,8},{73... | collective-permute-start | bytes 1572872 | tf_op jit(solution)/shard_map/ppermute | solution.py:36
  120.6 32.6 %collective-permute-start.24 = (bf16[512,512]{1,0:T(8,128)(2,1)}, bf16[512,512]{1,0:T(8,128)(2,1)}, u32[]{:S(2)}, u32[]{:S(2)}) collective-permute-start(bf16[512,512]{1,0:T(8,128)(2,1)} %collective-permute-done.22), channel_id=1, source_target_pairs={{128,192},{129,193},{130,194},{131,195},{132,196},{133,197},{134,1... | collective-permute-start | bytes 1572872 | tf_op jit(solution)/shard_map/ppermute | solution.py:35
  122.0 31.2 %collective-permute-start.25 = (bf16[512,512]{1,0:T(8,128)(2,1)}, bf16[512,512]{1,0:T(8,128)(2,1)}, u32[]{:S(2)}, u32[]{:S(2)}) collective-permute-start(bf16[512,512]{1,0:T(8,128)(2,1)} %collective-permute-done.23), channel_id=1, source_target_pairs={{64,0},{65,1},{66,2},{67,3},{68,4},{69,5},{70,6},{71,7},{72,8},{73... | collective-permute-start | bytes 1572872 | tf_op jit(solution)/shard_map/ppermute | solution.py:36
  134.6 31.4 %collective-permute-start.10 = (f32[256,512]{0,1:T(8,128)}, f32[256,512]{0,1:T(8,128)}, u32[]{:S(2)}, u32[]{:S(2)}) collective-permute-start(f32[256,512]{0,1:T(8,128)} %bitcast.263), channel_id=1, source_target_pairs={{0,48},{16,0},{32,16},{48,32},{1,49},{17,1},{33,17},{49,33},{2,50}... | collective-permute-start | bytes 1572872 | tf_op jit(solution)/shard_map/ppermute | solution.py:91
  148.5 27.4 %collective-permute-start.8 = (f32[256,512]{0,1:T(8,128)}, f32[256,512]{0,1:T(8,128)}, u32[]{:S(2)}, u32[]{:S(2)}) collective-permute-start(f32[256,512]{0,1:T(8,128)} %bitcast.25), channel_id=1, source_target_pairs={{0,16},{16,32},{32,48},{48,0},{1,17},{17,33},{33,49},{49,1},{2,18}... | collective-permute-start | bytes 1572872 | tf_op jit(solution)/shard_map/ppermute | solution.py:91
  148.8 27.1 %collective-permute-start.9 = (f32[256,512]{0,1:T(8,128)}, f32[256,512]{0,1:T(8,128)}, u32[]{:S(2)}, u32[]{:S(2)}) collective-permute-start(f32[256,512]{0,1:T(8,128)} %bitcast.26), channel_id=1, source_target_pairs={{0,32},{16,48},{32,0},{48,16},{1,33},{17,49},{33,1},{49,17},{2,34}... | collective-permute-start | bytes 1572872 | tf_op jit(solution)/shard_map/ppermute | solution.py:91
  159.1 39.3 %collective-permute-start.17 = (f32[256,512]{0,1:T(8,128)}, f32[256,512]{0,1:T(8,128)}, u32[]{:S(2)}, u32[]{:S(2)}) collective-permute-start(f32[256,512]{0,1:T(8,128)} %bitcast.266), channel_id=1, source_target_pairs={{0,16},{16,32},{32,48},{48,0},{1,17},{17,33},{33,49},{49,1},{2,18}... | collective-permute-start | bytes 1572872 | tf_op jit(solution)/shard_map/ppermute | solution.py:91
  163.6 36.3 %collective-permute-start.18 = (f32[256,512]{0,1:T(8,128)}, f32[256,512]{0,1:T(8,128)}, u32[]{:S(2)}, u32[]{:S(2)}) collective-permute-start(f32[256,512]{0,1:T(8,128)} %bitcast.264), channel_id=1, source_target_pairs={{0,32},{16,48},{32,0},{48,16},{1,33},{17,49},{33,1},{49,17},{2,34}... | collective-permute-start | bytes 1572872 | tf_op jit(solution)/shard_map/ppermute | solution.py:91
  166.1 33.8 %collective-permute-start.19 = (f32[256,512]{0,1:T(8,128)}, f32[256,512]{0,1:T(8,128)}, u32[]{:S(2)}, u32[]{:S(2)}) collective-permute-start(f32[256,512]{0,1:T(8,128)} %bitcast.265), channel_id=1, source_target_pairs={{0,48},{16,0},{32,16},{48,32},{1,49},{17,1},{33,17},{49,33},{2,50}... | collective-permute-start | bytes 1572872 | tf_op jit(solution)/shard_map/ppermute | solution.py:91
  175.9 42.7 %collective-permute-start.26 = (f32[256,512]{0,1:T(8,128)}, f32[256,512]{0,1:T(8,128)S(1)}, u32[]{:S(2)}, u32[]{:S(2)}) collective-permute-start(f32[256,512]{0,1:T(8,128)} %bitcast.269), channel_id=1, source_target_pairs={{0,16},{16,32},{32,48},{48,0},{1,17},{17,33},{33,49},{49,1},{2,18}... | collective-permute-start | bytes 1572872 | tf_op jit(solution)/shard_map/ppermute | solution.py:91
  175.9 42.7 %collective-permute-start.27 = (f32[256,512]{0,1:T(8,128)}, f32[256,512]{0,1:T(8,128)S(1)}, u32[]{:S(2)}, u32[]{:S(2)}) collective-permute-start(f32[256,512]{0,1:T(8,128)} %bitcast.268), channel_id=1, source_target_pairs={{0,32},{16,48},{32,0},{48,16},{1,33},{17,49},{33,1},{49,17},{2,34}... | collective-permute-start | bytes 1572872 | tf_op jit(solution)/shard_map/ppermute | solution.py:91
  (36 other events, 430.1 us)
Sparse Core Ops, SparseCore 0:
  25.4 40.9 all-gather.2
